TPU v7x, 768 devices: a whole 4x8x12 slice. The times are simulated.
768 devices in a mesh: seq: 16 (over x, y_lo), grp: 48 (over z, y_hi, core).
Axes of the slice: x: 4, y: 8 (y_hi: 2, y_lo: 4; y = y_hi * 4 + y_lo), z: 12, core: 2. Of those that a mesh axis runs over, the one named last changes fastest.
Arguments:
- embeddings: bfloat16 [16, 48, 512, 1024], P('seq', 'grp'), may hold values from -8 to 8
- seed_labels: float32 [16, 48, 512, 128], P('seq', 'grp'), may hold values from -8 to 8
- sources: int32 [16, 48, 3, 4], P('seq', 'grp'), may hold values from -1 to 47, as said below
- counts: int32 [16, 48], P('seq', 'grp'), may hold values from 4 to 8
Outputs:
- diffused: float32 [16, 48, 512, 128], P('seq', 'grp')
Inputs may be any that keep to these rules, and one draw needn't show every extreme that they name: `sources`: an entry at [q,g,s,j] is -1 or the group of a source block at the same seq index q in another group than g; the entries other than -1 in one list are distinct, come before the -1 entries, and some list is full in every draw.
All inputs are finite; a program needn't handle non-finite values.
Results may differ from a plain program's by a relative error of at most 0.0006.
Values may be sent and summed in bfloat16 or wider, within the bound.
No kernel may reach another device: no remote copies, remote signals or barrier semaphores. Data moves between devices by JAX's collectives and lax.ppermute only.
A program may use at most 32 MiB of HBM per device.

v0:
```python
import jax
import jax.numpy as jnp
from jax import lax
from jax.sharding import PartitionSpec as P

CLUS = 32
STEPS = 3


tile_scale = 8.0
pair_scale = 2.0
keep_share = 0.2
eps = 1e-06
highest = lax.Precision.HIGHEST


def padded(block, sides, width):
    for axis, dim in sides:
        count = lax.axis_size(axis)
        forward = [(i, i + 1) for i in range(count - 1)]
        forward.append((count - 1, 0))
        backward = [(target, source) for source, target in forward]
        low = lax.ppermute(
            lax.slice_in_dim(block, block.shape[dim] - width, None, axis=dim), axis, forward
        )
        high = lax.ppermute(lax.slice_in_dim(block, 0, width, axis=dim), axis, backward)
        block = jnp.concatenate([low, block, high], axis=dim)
    return block


def normalized(values):
    floats = values.astype(jnp.float32)
    return (floats * lax.rsqrt(jnp.sum(floats * floats, axis=-1, keepdims=True) + eps)).astype(
        jnp.bfloat16
    )


def kernel_tile(left, right, blank):
    score = jnp.dot(left, right.T, preferred_element_type=jnp.float32)
    weights = jnp.exp(tile_scale * (score - 1.0))
    if blank:
        weights = weights * (1.0 - jnp.eye(left.shape[0], dtype=jnp.float32))
    return weights.astype(jnp.bfloat16)


def body(embeddings, seed_labels, sources, counts):
    row_count = embeddings.shape[2]
    classes = seed_labels.shape[3]
    groups = lax.axis_size("grp")
    unit_emb = normalized(embeddings[0, 0])
    self_tile = kernel_tile(unit_emb, unit_emb, True)
    self_rows = jnp.sum(self_tile, axis=1, dtype=jnp.float32)
    centre = jnp.mean(unit_emb, axis=0, dtype=jnp.float32)
    centre_unit = centre * lax.rsqrt(jnp.sum(centre * centre) + eps)
    table = lax.all_gather(centre_unit[None], "grp", axis=0, tiled=True)
    pair_weight = jnp.exp(pair_scale * jnp.dot(table, centre_unit, precision=highest))
    extended = padded(unit_emb, (("seq", 0),), row_count)
    before_unit = extended[:row_count]
    after_unit = extended[2 * row_count :]
    next_tile = kernel_tile(unit_emb, after_unit, False)
    prior_tile = kernel_tile(unit_emb, before_unit, False)
    degree = (
        self_rows
        + jnp.sum(next_tile, axis=1, dtype=jnp.float32)
        + jnp.sum(prior_tile, axis=1, dtype=jnp.float32)
    )
    seed = seed_labels[0, 0]
    labels = seed
    count_value = counts[0, 0].astype(jnp.float32)
    member = jnp.arange(groups, dtype=jnp.int32)
    coarse_count = row_count // CLUS
    for iteration in range(STEPS):
        label_bf = labels.astype(jnp.bfloat16)
        widened = padded(label_bf, (("seq", 0),), row_count)
        local = jnp.dot(self_tile, label_bf, preferred_element_type=jnp.float32) + jnp.dot(
            next_tile, widened[2 * row_count :], preferred_element_type=jnp.float32
        )
        local = local + jnp.dot(prior_tile, widened[:row_count], preferred_element_type=jnp.float32)
        spread = local / degree[:, None]
        summary = jnp.sum(labels.reshape(coarse_count, CLUS, classes), axis=1) / CLUS
        chosen = jnp.sum(
            (sources[0, 0, iteration][:, None] == member[None, :]).astype(jnp.float32), axis=0
        )
        coefficient = chosen * pair_weight / count_value

        def fold_far(running, piece, start, coefficient=coefficient):
            return jnp.einsum("h,hkc->kc", coefficient, piece, precision=highest)

        far = fold_far(
            jnp.zeros_like(summary),
            lax.all_gather(summary[None], "grp", axis=0, tiled=True),
            jnp.int32(0),
        )
        far_rows = jnp.broadcast_to(far[:, None, :], (coarse_count, CLUS, classes)).reshape(
            row_count, classes
        )
        labels = keep_share * seed + (1.0 - keep_share) * (spread + far_rows)
    return labels[None, None]


def solution(mesh):
    return jax.shard_map(
        body,
        mesh=mesh,
        in_specs=(
            P("seq", "grp", None, None),
            P("seq", "grp", None, None),
            P("seq", "grp", None, None),
            P("seq", "grp"),
        ),
        out_specs=P("seq", "grp", None, None),
        check_vma=False,
    )
```

profile of v0, /device:TPU:1, one launch (start us, length us, event | category | flops | bytes accessed | tf_op | source)
XLA Modules:
  0.0 382.3 jit_solution(13725702487248082103)
XLA Ops:
  0.0 0.0 copy-start
  0.0 1.6 fusion.2
  1.6 0.0 copy-done
  1.6 0.0 copy-start.1
  1.6 0.0 copy-start.2
  1.6 0.3 convert_reduce_fusion
  2.0 4.0 %collective-permute-start.2 = (bf16[512,1024]{1,0:T(8,128)(2,1)S(1)}, bf16[512,1024]{1,0:T(8,128)(2,1)}, u32[]{:S(2)}, u32[]{:S(2)}) collective-permute-start(bf16[512,1024]{1,0:T(8,128)(2,1)S(1)} %get-tuple-element.6), channel_id=1, source_target_pairs={{0,48},{48,96},{96,144},{144,192},{192,240},{240,288},{288,336},{3... | collective-permute-start | bytes 3145736 | tf_op jit(solution)/shard_map/ppermute | solution.py:23
  6.0 6.1 %collective-permute-start = (bf16[512,1024]{1,0:T(8,128)(2,1)S(1)}, bf16[512,1024]{1,0:T(8,128)(2,1)}, u32[]{:S(2)}, u32[]{:S(2)}) collective-permute-start(bf16[512,1024]{1,0:T(8,128)(2,1)S(1)} %get-tuple-element.6), channel_id=1, source_target_pairs={{48,0},{96,48},{144,96},{192,144},{240,192},{288,240},{336,288},{3... | collective-permute-start | bytes 3145736 | tf_op jit(solution)/shard_map/ppermute | solution.py:26
  12.1 0.0 copy-done.1
  12.2 3.4 collective-permute-start.1
  15.6 1.9 collective-permute-start.3
  17.5 0.6 multiply_reduce_fusion
  18.8 116.0 %all-gather = f32[49152]{0:T(1024)S(1)} all-gather(f32[1024]{0:T(1024)S(1)} %broadcast_multiply_fusion.3), channel_id=2, replica_groups=mesh['seq'=16,'grp'=48] {'grp'}, dimensions={0}, use_global_device_ids=true | all-gather | bytes 200704 | tf_op jit(solution)/shard_map/all_gather | solution.py:55
  134.8 0.0 copy-done.2
  134.8 0.1 convert_reduce_fusion.6
  135.0 0.1 convert_reduce_fusion.5
  135.1 0.2 fusion.29
  135.3 72.1 %all-gather.1 = f32[768,128]{1,0:T(8,128)S(1)} all-gather(f32[16,128]{1,0:T(8,128)S(1)} %broadcast_multiply_fusion.2), channel_id=3, replica_groups=mesh['seq'=16,'grp'=48] {'grp'}, dimensions={0}, use_global_device_ids=true | all-gather | bytes 401408 | tf_op jit(solution)/shard_map/all_gather | solution.py:91
  207.4 0.1 convert_reduce_fusion.4
  208.1 0.4 fusion.37
  208.5 0.9 convert_reduce_fusion.3
  209.5 0.3 fusion.52
  209.8 0.0 collective-permute-done.2
  209.8 2.0 convert_reduce_fusion.1
  211.9 0.0 collective-permute-done
  211.9 2.0 convert_reduce_fusion.2
  213.9 0.0 collective-permute-done.1
  214.0 0.3 convolution_add_fusion.8
  214.3 0.0 collective-permute-done.3
  214.3 0.4 bitcast_reduce_fusion.1
  214.7 0.3 fusion.53
  215.1 7.1 %collective-permute-start.4 = (bf16[512,128]{1,0:T(8,128)(2,1)S(1)}, bf16[512,128]{1,0:T(8,128)(2,1)S(1)}, u32[]{:S(2)}, u32[]{:S(2)}) collective-permute-start(bf16[512,128]{1,0:T(8,128)(2,1)S(1)} %get-tuple-element.17), channel_id=1, source_target_pairs={{48,0},{96,48},{144,96},{192,144},{240,192},{288,240},{336,288},{3... | collective-permute-start | bytes 393224 | tf_op jit(solution)/shard_map/ppermute | solution.py:26
  222.1 1.9 collective-permute-start.5
  224.1 71.7 %all-gather.2 = f32[768,128]{1,0:T(8,128)S(1)} all-gather(f32[16,128]{1,0:T(8,128)S(1)} %broadcast_multiply_fusion.1), channel_id=4, replica_groups=mesh['seq'=16,'grp'=48] {'grp'}, dimensions={0}, use_global_device_ids=true | all-gather | bytes 401408 | tf_op jit(solution)/shard_map/all_gather | solution.py:91
  295.8 0.4 fusion.35
  296.2 0.0 collective-permute-done.4
  296.2 0.3 convolution_add_fusion.6
  296.6 0.0 collective-permute-done.5
  296.6 0.4 bitcast_reduce_fusion
  297.0 0.3 fusion.54
  297.3 7.7 %collective-permute-start.6 = (bf16[512,128]{1,0:T(8,128)(2,1)S(1)}, bf16[512,128]{1,0:T(8,128)(2,1)S(1)}, u32[]{:S(2)}, u32[]{:S(2)}) collective-permute-start(bf16[512,128]{1,0:T(8,128)(2,1)S(1)} %get-tuple-element.19), channel_id=1, source_target_pairs={{48,0},{96,48},{144,96},{192,144},{240,192},{288,240},{336,288},{3... | collective-permute-start | bytes 393224 | tf_op jit(solution)/shard_map/ppermute | solution.py:26
  305.0 1.9 collective-permute-start.7
  307.0 73.5 %all-gather.3 = f32[768,128]{1,0:T(8,128)S(1)} all-gather(f32[16,128]{1,0:T(8,128)S(1)} %broadcast_multiply_fusion), channel_id=5, replica_groups=mesh['seq'=16,'grp'=48] {'grp'}, dimensions={0}, use_global_device_ids=true | all-gather | bytes 401408 | tf_op jit(solution)/shard_map/all_gather | solution.py:91
  380.5 0.4 fusion.33
  380.9 0.0 collective-permute-done.6
  380.9 0.3 convolution_add_fusion.4
  381.2 0.0 collective-permute-done.7
  381.3 1.1 fusion.21
  (13 shorter events, 0.2 us)
Async XLA Ops:
  0.0 1.6 copy-start
  1.6 10.5 %copy-start.1 = (f32[1,1,512,128]{3,2,1,0:T(8,128)S(1)}, f32[1,1,512,128]{3,2,1,0:T(8,128)}, u32[]{:S(2)}) copy-start(f32[1,1,512,128]{3,2,1,0:T(8,128)} %param.5) | copy-start | bytes 786436
  1.6 133.2 %copy-start.2 = (s32[1,1,3,4]{3,1,2,0:T(1,128)S(1)}, s32[1,1,3,4]{3,1,2,0:T(1,128)}, u32[]{:S(2)}) copy-start(s32[1,1,3,4]{3,1,2,0:T(1,128)} %param.6) | copy-start | bytes 148
  2.0 207.9 %collective-permute-start.2 = (bf16[512,1024]{1,0:T(8,128)(2,1)S(1)}, bf16[512,1024]{1,0:T(8,128)(2,1)}, u32[]{:S(2)}, u32[]{:S(2)}) collective-permute-start(bf16[512,1024]{1,0:T(8,128)(2,1)S(1)} %get-tuple-element.6), channel_id=1, source_target_pairs={{0,48},{48,96},{96,144},{144,192},{192,240},{240,288},{288,336},{3... | collective-permute-start | bytes 3145736 | tf_op jit(solution)/shard_map/ppermute | solution.py:23
  6.0 205.9 %collective-permute-start = (bf16[512,1024]{1,0:T(8,128)(2,1)S(1)}, bf16[512,1024]{1,0:T(8,128)(2,1)}, u32[]{:S(2)}, u32[]{:S(2)}) collective-permute-start(bf16[512,1024]{1,0:T(8,128)(2,1)S(1)} %get-tuple-element.6), channel_id=1, source_target_pairs={{48,0},{96,48},{144,96},{192,144},{240,192},{288,240},{336,288},{3... | collective-permute-start | bytes 3145736 | tf_op jit(solution)/shard_map/ppermute | solution.py:26
  12.2 201.8 %collective-permute-start.1 = (bf16[512,128]{1,0:T(8,128)(2,1)S(1)}, bf16[512,128]{1,0:T(8,128)(2,1)S(1)}, u32[]{:S(2)}, u32[]{:S(2)}) collective-permute-start(bf16[512,128]{1,0:T(8,128)(2,1)S(1)} %convert_bitcast_fusion.1), channel_id=1, source_target_pairs={{48,0},{96,48},{144,96},{192,144},{240,192},{288,240},{336,288},{3... | collective-permute-start | bytes 393224 | tf_op jit(solution)/shard_map/ppermute | solution.py:26
  15.6 198.8 %collective-permute-start.3 = (bf16[512,128]{1,0:T(8,128)(2,1)S(1)}, bf16[512,128]{1,0:T(8,128)(2,1)S(1)}, u32[]{:S(2)}, u32[]{:S(2)}) collective-permute-start(bf16[512,128]{1,0:T(8,128)(2,1)S(1)} %convert_bitcast_fusion.1), channel_id=1, source_target_pairs={{0,48},{48,96},{96,144},{144,192},{192,240},{240,288},{288,336},{3... | collective-permute-start | bytes 393224 | tf_op jit(solution)/shard_map/ppermute | solution.py:23
  215.1 81.2 %collective-permute-start.4 = (bf16[512,128]{1,0:T(8,128)(2,1)S(1)}, bf16[512,128]{1,0:T(8,128)(2,1)S(1)}, u32[]{:S(2)}, u32[]{:S(2)}) collective-permute-start(bf16[512,128]{1,0:T(8,128)(2,1)S(1)} %get-tuple-element.17), channel_id=1, source_target_pairs={{48,0},{96,48},{144,96},{192,144},{240,192},{288,240},{336,288},{3... | collective-permute-start | bytes 393224 | tf_op jit(solution)/shard_map/ppermute | solution.py:26
  222.1 74.5 %collective-permute-start.5 = (bf16[512,128]{1,0:T(8,128)(2,1)S(1)}, bf16[512,128]{1,0:T(8,128)(2,1)S(1)}, u32[]{:S(2)}, u32[]{:S(2)}) collective-permute-start(bf16[512,128]{1,0:T(8,128)(2,1)S(1)} %get-tuple-element.17), channel_id=1, source_target_pairs={{0,48},{48,96},{96,144},{144,192},{192,240},{240,288},{288,336},{3... | collective-permute-start | bytes 393224 | tf_op jit(solution)/shard_map/ppermute | solution.py:23
  297.3 83.5 %collective-permute-start.6 = (bf16[512,128]{1,0:T(8,128)(2,1)S(1)}, bf16[512,128]{1,0:T(8,128)(2,1)S(1)}, u32[]{:S(2)}, u32[]{:S(2)}) collective-permute-start(bf16[512,128]{1,0:T(8,128)(2,1)S(1)} %get-tuple-element.19), channel_id=1, source_target_pairs={{48,0},{96,48},{144,96},{192,144},{240,192},{288,240},{336,288},{3... | collective-permute-start | bytes 393224 | tf_op jit(solution)/shard_map/ppermute | solution.py:26
  305.0 76.2 %collective-permute-start.7 = (bf16[512,128]{1,0:T(8,128)(2,1)S(1)}, bf16[512,128]{1,0:T(8,128)(2,1)S(1)}, u32[]{:S(2)}, u32[]{:S(2)}) collective-permute-start(bf16[512,128]{1,0:T(8,128)(2,1)S(1)} %get-tuple-element.19), channel_id=1, source_target_pairs={{0,48},{48,96},{96,144},{144,192},{192,240},{240,288},{288,336},{3... | collective-permute-start | bytes 393224 | tf_op jit(solution)/shard_map/ppermute | solution.py:23
where the time goes:
time: 383 us; the launch traced here: 382 us
  blocking collectives  333 us (87%)
  starting transfers between devices  34.1 us (9%)
  matrix products  10.3 us (3%)
    all_gather x3, blocking collectives, body(): lax.all_gather(summary[None], 'grp', axis=0, tiled=True)  217 us
    all_gather x1, blocking collectives, body(): table = lax.all_gather(centre_unit[None], 'grp', axis=0, tiled=True)  116 us
    ppermute x4, starting transfers between devices, padded(): lax.ppermute(lax.slice_in_dim(block, 0, width, axis=dim), axis, backward)  24.3 us
    ppermute x4, starting transfers between devices, padded(): lax.ppermute(lax.slice_in_dim(block, block.shape[dim] - width, None, axis...  9.8 us
  transfers between devices with their start and end apart: 8, of which 0 were waited for; matrix products, arithmetic and copies ran while one was open for 2% of the time, Pallas kernels for 0%

commit v1 on v0

--- a/solution.py
+++ b/solution.py
@@ -1,7 +1,8 @@
+import numpy as np
 import jax
 import jax.numpy as jnp
 from jax import lax
-from jax.sharding import PartitionSpec as P
+from jax.sharding import Mesh, PartitionSpec as P
 
 CLUS = 32
 STEPS = 3
@@ -12,6 +13,8 @@
 keep_share = 0.2
 eps = 1e-06
 highest = lax.Precision.HIGHEST
+
+GRP_PARTS = ("grp_z", "grp_y", "grp_c")
 
 
 def padded(block, sides, width):
@@ -26,6 +29,12 @@
         high = lax.ppermute(lax.slice_in_dim(block, 0, width, axis=dim), axis, backward)
         block = jnp.concatenate([low, block, high], axis=dim)
     return block
+
+
+def gather_groups(value):
+    for axis in reversed(GRP_PARTS):
+        value = lax.all_gather(value, axis, axis=0, tiled=True)
+    return value
 
 
 def normalized(values):
@@ -43,16 +52,26 @@
     return weights.astype(jnp.bfloat16)
 
 
-def body(embeddings, seed_labels, sources, counts):
+def body(groups, embeddings, seed_labels, sources, counts):
     row_count = embeddings.shape[2]
     classes = seed_labels.shape[3]
-    groups = lax.axis_size("grp")
+    width = embeddings.shape[3]
     unit_emb = normalized(embeddings[0, 0])
     self_tile = kernel_tile(unit_emb, unit_emb, True)
     self_rows = jnp.sum(self_tile, axis=1, dtype=jnp.float32)
     centre = jnp.mean(unit_emb, axis=0, dtype=jnp.float32)
     centre_unit = centre * lax.rsqrt(jnp.sum(centre * centre) + eps)
-    table = lax.all_gather(centre_unit[None], "grp", axis=0, tiled=True)
+    seed = seed_labels[0, 0]
+    coarse_count = row_count // CLUS
+    centre_rows = width // classes
+
+    def summarize(labels):
+        return jnp.sum(labels.reshape(coarse_count, CLUS, classes), axis=1) / CLUS
+
+    first = gather_groups(
+        jnp.concatenate([centre_unit.reshape(centre_rows, classes), summarize(seed)])[None]
+    )
+    table = first[:, :centre_rows].reshape(groups, width)
     pair_weight = jnp.exp(pair_scale * jnp.dot(table, centre_unit, precision=highest))
     extended = padded(unit_emb, (("seq", 0),), row_count)
     before_unit = extended[:row_count]
@@ -64,11 +83,9 @@
         + jnp.sum(next_tile, axis=1, dtype=jnp.float32)
         + jnp.sum(prior_tile, axis=1, dtype=jnp.float32)
     )
-    seed = seed_labels[0, 0]
     labels = seed
     count_value = counts[0, 0].astype(jnp.float32)
     member = jnp.arange(groups, dtype=jnp.int32)
-    coarse_count = row_count // CLUS
     for iteration in range(STEPS):
         label_bf = labels.astype(jnp.bfloat16)
         widened = padded(label_bf, (("seq", 0),), row_count)
@@ -77,20 +94,15 @@
         )
         local = local + jnp.dot(prior_tile, widened[:row_count], preferred_element_type=jnp.float32)
         spread = local / degree[:, None]
-        summary = jnp.sum(labels.reshape(coarse_count, CLUS, classes), axis=1) / CLUS
+        if iteration == 0:
+            gathered = first[:, centre_rows:]
+        else:
+            gathered = gather_groups(summarize(labels)[None])
         chosen = jnp.sum(
             (sources[0, 0, iteration][:, None] == member[None, :]).astype(jnp.float32), axis=0
         )
         coefficient = chosen * pair_weight / count_value
-
-        def fold_far(running, piece, start, coefficient=coefficient):
-            return jnp.einsum("h,hkc->kc", coefficient, piece, precision=highest)
-
-        far = fold_far(
-            jnp.zeros_like(summary),
-            lax.all_gather(summary[None], "grp", axis=0, tiled=True),
-            jnp.int32(0),
-        )
+        far = jnp.einsum("h,hkc->kc", coefficient, gathered, precision=highest)
         far_rows = jnp.broadcast_to(far[:, None, :], (coarse_count, CLUS, classes)).reshape(
             row_count, classes
         )
@@ -99,15 +111,18 @@
 
 
 def solution(mesh):
+    groups = mesh.shape["grp"]
+    devices = np.asarray(mesh.devices)
+    if groups % 4 == 0:
+        parts = (groups // 4, 2, 2)
+    else:
+        parts = (groups, 1, 1)
+    split = Mesh(devices.reshape((mesh.shape["seq"],) + parts), ("seq",) + GRP_PARTS)
+    block = P("seq", GRP_PARTS, None, None)
     return jax.shard_map(
-        body,
-        mesh=mesh,
-        in_specs=(
-            P("seq", "grp", None, None),
-            P("seq", "grp", None, None),
-            P("seq", "grp", None, None),
-            P("seq", "grp"),
-        ),
-        out_specs=P("seq", "grp", None, None),
+        lambda *args: body(groups, *args),
+        mesh=split,
+        in_specs=(block, block, block, P("seq", GRP_PARTS)),
+        out_specs=block,
         check_vma=False,
     )

time: 383 us -> 195 us (0.51)
  the two profiles are of different devices: /device:TPU:1 before, /device:TPU:30 now
where the time goes in v1:
time: 195 us; the launch traced here: 194 us
  blocking collectives  137 us (70%)
  starting transfers between devices  42.2 us (22%)
  matrix products  10.3 us (5%)
  other arithmetic  2.85 us (1%)
    all_gather x9, blocking collectives, gather_groups(): value = lax.all_gather(value, axis, axis=0, tiled=True)  137 us
    ppermute x4, starting transfers between devices, padded(): lax.ppermute(lax.slice_in_dim(block, block.shape[dim] - width, None, axis...  34.5 us
    ppermute x4, starting transfers between devices, padded(): lax.ppermute(lax.slice_in_dim(block, 0, width, axis=dim), axis, backward)  7.68 us
    dot_general x3, matrix products, kernel_tile(): score = jnp.dot(left, right.T, preferred_element_type=jnp.float32)  5.02 us
  transfers between devices with their start and end apart: 8, of which 0 were waited for; matrix products, arithmetic and copies ran while one was open for 5% of the time, Pallas kernels for 0%

profile of v1, /device:TPU:30, one launch (start us, length us, event | category | flops | bytes accessed | tf_op | source)
XLA Modules:
  0.0 194.0 jit_solution(14786911302347529088)
XLA Ops:
  0.0 1.6 fusion.2
  1.6 0.0 copy-start.1
  1.6 0.3 convert_reduce_fusion
  1.9 0.0 copy-start.2
  2.0 11.1 %collective-permute-start.2 = (bf16[512,1024]{1,0:T(8,128)(2,1)S(1)}, bf16[512,1024]{1,0:T(8,128)(2,1)}, u32[]{:S(2)}, u32[]{:S(2)}) collective-permute-start(bf16[512,1024]{1,0:T(8,128)(2,1)S(1)} %get-tuple-element.6), channel_id=1, source_target_pairs={{0,48},{48,96},{96,144},{144,192},{192,240},{240,288},{288,336},{3... | collective-permute-start | bytes 3145736 | tf_op jit(solution)/shard_map/ppermute | solution.py:26
  13.0 1.9 collective-permute-start
  15.0 1.9 collective-permute-start.1
  16.9 7.8 %collective-permute-start.3 = (bf16[512,128]{1,0:T(8,128)(2,1)S(1)}, bf16[512,128]{1,0:T(8,128)(2,1)S(1)}, u32[]{:S(2)}, u32[]{:S(2)}) collective-permute-start(bf16[512,128]{1,0:T(8,128)(2,1)S(1)} %convert_bitcast_fusion.1), channel_id=1, source_target_pairs={{0,48},{48,96},{96,144},{144,192},{192,240},{240,288},{288,336},{3... | collective-permute-start | bytes 393224 | tf_op jit(solution)/shard_map/ppermute | solution.py:26
  24.7 0.6 multiply_reduce_fusion
  26.1 1.8 all-gather
  28.0 33.9 %all_gather.28 = f32[4,24,128]{2,1,0:T(8,128)S(1)} all-gather(f32[2,24,128]{2,1,0:T(8,128)S(1)} %bitcast.98), channel_id=1, replica_groups=mesh['seq'=16,'grp_z'=12,'grp_y'=2,'grp_c'=2] {'grp_y'}, dimensions={0}, use_global_device_ids=true | all-gather | bytes 73728 | tf_op jit(solution)/shard_map/all_gather | solution.py:36
  61.9 35.4 %all_gather.29 = f32[48,24,128]{2,1,0:T(8,128)S(1)} all-gather(f32[4,24,128]{2,1,0:T(8,128)S(1)} %all_gather.28), channel_id=1, replica_groups=mesh['seq'=16,'grp_z'=12,'grp_y'=2,'grp_c'=2] {'grp_z'}, dimensions={0}, use_global_device_ids=true | all-gather | bytes 638976 | tf_op jit(solution)/shard_map/all_gather | solution.py:36
  97.3 0.1 convert_reduce_fusion.6
  97.4 0.1 convert_reduce_fusion.5
  97.5 0.2 fusion.29
  97.7 0.1 convert_reduce_fusion.4
  97.8 0.1 slice.21
  98.5 0.4 fusion.37
  99.0 0.9 convert_reduce_fusion.3
  99.9 0.3 fusion.54
  100.2 0.0 collective-permute-done.2
  100.2 2.0 %convert_reduce_fusion.1 = (f32[512]{0:T(512)S(1)}, bf16[512,512]{0,1:T(8,128)(2,1)S(1)}) fusion(bf16[512,1024]{1,0:T(8,128)(2,1)S(1)} %get-tuple-element.6, bf16[512,1024]{1,0:T(8,128)(2,1)} %collective-permute-done.2), kind=kOutput, calls=%fused_computation.44 | convolution fusion | flops 538181120 | bytes 2623488 | tf_op jit(solution)/shard_map/dot_general | solution.py:48
  102.3 2.0 %convert_reduce_fusion.2 = (f32[512]{0:T(512)S(1)}, bf16[512,512]{0,1:T(8,128)(2,1)S(1)}) fusion(bf16[512,1024]{1,0:T(8,128)(2,1)S(1)} %get-tuple-element.6, bf16[512,1024]{1,0:T(8,128)(2,1)} %collective-permute-done), kind=kOutput, calls=%fused_computation.45 | convolution fusion | flops 538181120 | bytes 2623488 | tf_op jit(solution)/shard_map/dot_general | solution.py:48
  104.3 0.0 collective-permute-done.1
  104.4 0.3 convolution_add_fusion.8
  104.7 0.0 collective-permute-done.3
  104.7 0.4 bitcast_reduce_fusion.1
  105.1 0.3 fusion.55
  105.5 1.9 collective-permute-start.4
  107.4 7.8 %collective-permute-start.5 = (bf16[512,128]{1,0:T(8,128)(2,1)S(1)}, bf16[512,128]{1,0:T(8,128)(2,1)S(1)}, u32[]{:S(2)}, u32[]{:S(2)}) collective-permute-start(bf16[512,128]{1,0:T(8,128)(2,1)S(1)} %get-tuple-element.17), channel_id=1, source_target_pairs={{0,48},{48,96},{96,144},{144,192},{192,240},{240,288},{288,336},{3... | collective-permute-start | bytes 393224 | tf_op jit(solution)/shard_map/ppermute | solution.py:26
  115.2 1.8 all-gather.1
  117.0 8.3 %all_gather.31 = f32[4,16,128]{2,1,0:T(8,128)S(1)} all-gather(f32[2,16,128]{2,1,0:T(8,128)S(1)} %bitcast.99), channel_id=1, replica_groups=mesh['seq'=16,'grp_z'=12,'grp_y'=2,'grp_c'=2] {'grp_y'}, dimensions={0}, use_global_device_ids=true | all-gather | bytes 49152 | tf_op jit(solution)/shard_map/all_gather | solution.py:36
  125.4 21.7 %all_gather.32 = f32[48,16,128]{2,1,0:T(8,128)S(1)} all-gather(f32[4,16,128]{2,1,0:T(8,128)S(1)} %all_gather.31), channel_id=1, replica_groups=mesh['seq'=16,'grp_z'=12,'grp_y'=2,'grp_c'=2] {'grp_z'}, dimensions={0}, use_global_device_ids=true | all-gather | bytes 425984 | tf_op jit(solution)/shard_map/all_gather | solution.py:36
  147.1 0.4 fusion.35
  147.5 0.3 convolution_add_fusion.6
  147.9 0.0 collective-permute-done.5
  147.9 0.4 bitcast_reduce_fusion
  148.3 0.3 fusion.56
  148.6 1.9 collective-permute-start.6
  150.5 7.8 %collective-permute-start.7 = (bf16[512,128]{1,0:T(8,128)(2,1)S(1)}, bf16[512,128]{1,0:T(8,128)(2,1)S(1)}, u32[]{:S(2)}, u32[]{:S(2)}) collective-permute-start(bf16[512,128]{1,0:T(8,128)(2,1)S(1)} %get-tuple-element.19), channel_id=1, source_target_pairs={{0,48},{48,96},{96,144},{144,192},{192,240},{240,288},{288,336},{3... | collective-permute-start | bytes 393224 | tf_op jit(solution)/shard_map/ppermute | solution.py:26
  158.4 1.8 all-gather.2
  160.2 8.3 %all_gather.34 = f32[4,16,128]{2,1,0:T(8,128)S(1)} all-gather(f32[2,16,128]{2,1,0:T(8,128)S(1)} %bitcast.100), channel_id=1, replica_groups=mesh['seq'=16,'grp_z'=12,'grp_y'=2,'grp_c'=2] {'grp_y'}, dimensions={0}, use_global_device_ids=true | all-gather | bytes 49152 | tf_op jit(solution)/shard_map/all_gather | solution.py:36
  168.5 23.6 %all_gather.35 = f32[48,16,128]{2,1,0:T(8,128)S(1)} all-gather(f32[4,16,128]{2,1,0:T(8,128)S(1)} %all_gather.34), channel_id=1, replica_groups=mesh['seq'=16,'grp_z'=12,'grp_y'=2,'grp_c'=2] {'grp_z'}, dimensions={0}, use_global_device_ids=true | all-gather | bytes 425984 | tf_op jit(solution)/shard_map/all_gather | solution.py:36
  192.2 0.4 fusion.33
  192.6 0.0 collective-permute-done.6
  192.6 0.3 convolution_add_fusion.4
  192.9 0.0 collective-permute-done.7
  193.0 1.1 fusion.21
  (21 shorter events, 0.2 us)
Async XLA Ops:
  0.0 1.6 copy-start
  1.6 13.3 %copy-start.1 = (f32[1,1,512,128]{3,2,1,0:T(8,128)S(1)}, f32[1,1,512,128]{3,2,1,0:T(8,128)}, u32[]{:S(2)}) copy-start(f32[1,1,512,128]{3,2,1,0:T(8,128)} %param.5) | copy-start | bytes 786436
  1.9 95.3 %copy-start.2 = (s32[1,1,3,4]{3,1,2,0:T(1,128)S(1)}, s32[1,1,3,4]{3,1,2,0:T(1,128)}, u32[]{:S(2)}) copy-start(s32[1,1,3,4]{3,1,2,0:T(1,128)} %param.6) | copy-start | bytes 148
  2.0 98.3 %collective-permute-start.2 = (bf16[512,1024]{1,0:T(8,128)(2,1)S(1)}, bf16[512,1024]{1,0:T(8,128)(2,1)}, u32[]{:S(2)}, u32[]{:S(2)}) collective-permute-start(bf16[512,1024]{1,0:T(8,128)(2,1)S(1)} %get-tuple-element.6), channel_id=1, source_target_pairs={{0,48},{48,96},{96,144},{144,192},{192,240},{240,288},{288,336},{3... | collective-permute-start | bytes 3145736 | tf_op jit(solution)/shard_map/ppermute | solution.py:26
  13.0 89.3 %collective-permute-start = (bf16[512,1024]{1,0:T(8,128)(2,1)S(1)}, bf16[512,1024]{1,0:T(8,128)(2,1)}, u32[]{:S(2)}, u32[]{:S(2)}) collective-permute-start(bf16[512,1024]{1,0:T(8,128)(2,1)S(1)} %get-tuple-element.6), channel_id=1, source_target_pairs={{48,0},{96,48},{144,96},{192,144},{240,192},{288,240},{336,288},{3... | collective-permute-start | bytes 3145736 | tf_op jit(solution)/shard_map/ppermute | solution.py:29
  15.0 89.4 %collective-permute-start.1 = (bf16[512,128]{1,0:T(8,128)(2,1)S(1)}, bf16[512,128]{1,0:T(8,128)(2,1)S(1)}, u32[]{:S(2)}, u32[]{:S(2)}) collective-permute-start(bf16[512,128]{1,0:T(8,128)(2,1)S(1)} %convert_bitcast_fusion.1), channel_id=1, source_target_pairs={{48,0},{96,48},{144,96},{192,144},{240,192},{288,240},{336,288},{3... | collective-permute-start | bytes 393224 | tf_op jit(solution)/shard_map/ppermute | solution.py:29
  16.9 87.8 %collective-permute-start.3 = (bf16[512,128]{1,0:T(8,128)(2,1)S(1)}, bf16[512,128]{1,0:T(8,128)(2,1)S(1)}, u32[]{:S(2)}, u32[]{:S(2)}) collective-permute-start(bf16[512,128]{1,0:T(8,128)(2,1)S(1)} %convert_bitcast_fusion.1), channel_id=1, source_target_pairs={{0,48},{48,96},{96,144},{144,192},{192,240},{240,288},{288,336},{3... | collective-permute-start | bytes 393224 | tf_op jit(solution)/shard_map/ppermute | solution.py:26
  105.5 42.1 %collective-permute-start.4 = (bf16[512,128]{1,0:T(8,128)(2,1)S(1)}, bf16[512,128]{1,0:T(8,128)(2,1)S(1)}, u32[]{:S(2)}, u32[]{:S(2)}) collective-permute-start(bf16[512,128]{1,0:T(8,128)(2,1)S(1)} %get-tuple-element.17), channel_id=1, source_target_pairs={{48,0},{96,48},{144,96},{192,144},{240,192},{288,240},{336,288},{3... | collective-permute-start | bytes 393224 | tf_op jit(solution)/shard_map/ppermute | solution.py:29
  107.4 40.5 %collective-permute-start.5 = (bf16[512,128]{1,0:T(8,128)(2,1)S(1)}, bf16[512,128]{1,0:T(8,128)(2,1)S(1)}, u32[]{:S(2)}, u32[]{:S(2)}) collective-permute-start(bf16[512,128]{1,0:T(8,128)(2,1)S(1)} %get-tuple-element.17), channel_id=1, source_target_pairs={{0,48},{48,96},{96,144},{144,192},{192,240},{240,288},{288,336},{3... | collective-permute-start | bytes 393224 | tf_op jit(solution)/shard_map/ppermute | solution.py:26
  148.6 43.9 %collective-permute-start.6 = (bf16[512,128]{1,0:T(8,128)(2,1)S(1)}, bf16[512,128]{1,0:T(8,128)(2,1)S(1)}, u32[]{:S(2)}, u32[]{:S(2)}) collective-permute-start(bf16[512,128]{1,0:T(8,128)(2,1)S(1)} %get-tuple-element.19), channel_id=1, source_target_pairs={{48,0},{96,48},{144,96},{192,144},{240,192},{288,240},{336,288},{3... | collective-permute-start | bytes 393224 | tf_op jit(solution)/shard_map/ppermute | solution.py:29
  150.5 42.4 %collective-permute-start.7 = (bf16[512,128]{1,0:T(8,128)(2,1)S(1)}, bf16[512,128]{1,0:T(8,128)(2,1)S(1)}, u32[]{:S(2)}, u32[]{:S(2)}) collective-permute-start(bf16[512,128]{1,0:T(8,128)(2,1)S(1)} %get-tuple-element.19), channel_id=1, source_target_pairs={{0,48},{48,96},{96,144},{144,192},{192,240},{240,288},{288,336},{3... | collective-permute-start | bytes 393224 | tf_op jit(solution)/shard_map/ppermute | solution.py:26

commit v2 on v1

--- a/solution.py
+++ b/solution.py
@@ -73,7 +73,8 @@
     )
     table = first[:, :centre_rows].reshape(groups, width)
     pair_weight = jnp.exp(pair_scale * jnp.dot(table, centre_unit, precision=highest))
-    extended = padded(unit_emb, (("seq", 0),), row_count)
+    unit_send, first = lax.optimization_barrier((unit_emb, first))
+    extended = padded(unit_send, (("seq", 0),), row_count)
     before_unit = extended[:row_count]
     after_unit = extended[2 * row_count :]
     next_tile = kernel_tile(unit_emb, after_unit, False)

time: 195 us -> 191 us (0.979)
  the two profiles are of different devices: /device:TPU:30 before, /device:TPU:62 now
where the time goes in v2:
time: 191 us; the launch traced here: 190 us
  blocking collectives  112 us (59%)
  starting transfers between devices  39 us (20%)
  waiting for transfers between devices  27.2 us (14%)
  matrix products  7.84 us (4%)
  other arithmetic  2.85 us (1%)
    all_gather x9, blocking collectives, gather_groups(): value = lax.all_gather(value, axis, axis=0, tiled=True)  112 us
    ppermute x4, starting transfers between devices, padded(): lax.ppermute(lax.slice_in_dim(block, block.shape[dim] - width, None, axis...  30 us
    ppermute x4, waiting for transfers between devices, padded(): lax.ppermute(lax.slice_in_dim(block, block.shape[dim] - width, None, axis...  14 us
    ppermute x4, waiting for transfers between devices, padded(): lax.ppermute(lax.slice_in_dim(block, 0, width, axis=dim), axis, backward)  13.3 us
    ppermute x4, starting transfers between devices, padded(): lax.ppermute(lax.slice_in_dim(block, 0, width, axis=dim), axis, backward)  8.97 us
  transfers between devices with their start and end apart: 8, of which 3 were waited for; matrix products, arithmetic and copies ran while one was open for 3% of the time, Pallas kernels for 0%

profile of v2, /device:TPU:62, one launch (start us, length us, event | category | flops | bytes accessed | tf_op | source)
XLA Modules:
  0.0 190.4 jit_solution(13301340089113636414)
XLA Ops:
  0.0 1.6 fusion.2
  1.6 0.0 copy-start.1
  1.6 0.3 convert_reduce_fusion
  1.9 0.0 copy-start.2
  2.0 0.6 multiply_reduce_fusion
  3.3 1.8 all-gather
  5.2 8.4 %all_gather.28 = f32[4,24,128]{2,1,0:T(8,128)S(1)} all-gather(f32[2,24,128]{2,1,0:T(8,128)S(1)} %bitcast.98), channel_id=1, replica_groups=mesh['seq'=16,'grp_z'=12,'grp_y'=2,'grp_c'=2] {'grp_y'}, dimensions={0}, use_global_device_ids=true | all-gather | bytes 73728 | tf_op jit(solution)/shard_map/all_gather | solution.py:36
  13.6 35.7 %all_gather.29 = f32[48,24,128]{2,1,0:T(8,128)S(1)} all-gather(f32[4,24,128]{2,1,0:T(8,128)S(1)} %all_gather.28), channel_id=1, replica_groups=mesh['seq'=16,'grp_z'=12,'grp_y'=2,'grp_c'=2] {'grp_z'}, dimensions={0}, use_global_device_ids=true | all-gather | bytes 638976 | tf_op jit(solution)/shard_map/all_gather | solution.py:36
  49.3 3.2 %collective-permute-start = (bf16[512,1024]{1,0:T(8,128)(2,1)S(1)}, bf16[512,1024]{1,0:T(8,128)(2,1)S(1)}, u32[]{:S(2)}, u32[]{:S(2)}) collective-permute-start(bf16[512,1024]{1,0:T(8,128)(2,1)S(1)} %get-tuple-element.7), channel_id=1, source_target_pairs={{48,0},{96,48},{144,96},{192,144},{240,192},{288,240},{336,288},{3... | collective-permute-start | bytes 3145736 | tf_op jit(solution)/shard_map/ppermute | solution.py:29
  52.5 6.5 %collective-permute-start.2 = (bf16[512,1024]{1,0:T(8,128)(2,1)S(1)}, bf16[512,1024]{1,0:T(8,128)(2,1)S(1)}, u32[]{:S(2)}, u32[]{:S(2)}) collective-permute-start(bf16[512,1024]{1,0:T(8,128)(2,1)S(1)} %get-tuple-element.7), channel_id=1, source_target_pairs={{0,48},{48,96},{96,144},{144,192},{192,240},{240,288},{288,336},{3... | collective-permute-start | bytes 3145736 | tf_op jit(solution)/shard_map/ppermute | solution.py:26
  59.1 1.9 %collective-permute-start.1 = (bf16[512,128]{1,0:T(8,128)(2,1)S(1)}, bf16[512,128]{1,0:T(8,128)(2,1)S(1)}, u32[]{:S(2)}, u32[]{:S(2)}) collective-permute-start(bf16[512,128]{1,0:T(8,128)(2,1)S(1)} %convert_bitcast_fusion.1), channel_id=1, source_target_pairs={{48,0},{96,48},{144,96},{192,144},{240,192},{288,240},{336,288},{3... | collective-permute-start | bytes 393224 | tf_op jit(solution)/shard_map/ppermute | solution.py:29
  61.0 7.8 %collective-permute-start.3 = (bf16[512,128]{1,0:T(8,128)(2,1)S(1)}, bf16[512,128]{1,0:T(8,128)(2,1)S(1)}, u32[]{:S(2)}, u32[]{:S(2)}) collective-permute-start(bf16[512,128]{1,0:T(8,128)(2,1)S(1)} %convert_bitcast_fusion.1), channel_id=1, source_target_pairs={{0,48},{48,96},{96,144},{144,192},{192,240},{240,288},{288,336},{3... | collective-permute-start | bytes 393224 | tf_op jit(solution)/shard_map/ppermute | solution.py:26
  68.9 0.1 convert_reduce_fusion.6
  69.0 0.1 convert_reduce_fusion.5
  69.1 0.2 fusion.29
  69.3 0.1 convert_reduce_fusion.4
  69.4 0.1 slice.17
  70.2 0.4 fusion.37
  70.6 0.9 convert_reduce_fusion.3
  71.5 0.3 fusion.54
  71.8 9.4 %collective-permute-done = bf16[512,1024]{1,0:T(8,128)(2,1)S(1)} collective-permute-done((bf16[512,1024]{1,0:T(8,128)(2,1)S(1)}, bf16[512,1024]{1,0:T(8,128)(2,1)S(1)}, u32[]{:S(2)}, u32[]{:S(2)}) %collective-permute-start) | collective-permute-done | bytes 1048608 | tf_op jit(solution)/shard_map/ppermute | solution.py:29
  81.2 0.8 convert_reduce_fusion.2
  82.0 13.9 %collective-permute-done.2 = bf16[512,1024]{1,0:T(8,128)(2,1)S(1)} collective-permute-done((bf16[512,1024]{1,0:T(8,128)(2,1)S(1)}, bf16[512,1024]{1,0:T(8,128)(2,1)S(1)}, u32[]{:S(2)}, u32[]{:S(2)}) %collective-permute-start.2) | collective-permute-done | bytes 1048608 | tf_op jit(solution)/shard_map/ppermute | solution.py:26
  96.0 0.8 convert_reduce_fusion.1
  96.8 3.9 %collective-permute-done.1 = bf16[512,128]{1,0:T(8,128)(2,1)S(1)} collective-permute-done((bf16[512,128]{1,0:T(8,128)(2,1)S(1)}, bf16[512,128]{1,0:T(8,128)(2,1)S(1)}, u32[]{:S(2)}, u32[]{:S(2)}) %collective-permute-start.1) | collective-permute-done | bytes 131104 | tf_op jit(solution)/shard_map/ppermute | solution.py:29
  100.7 0.3 convolution_add_fusion.8
  101.1 0.0 collective-permute-done.3
  101.1 0.4 bitcast_reduce_fusion.1
  101.5 0.3 fusion.55
  101.8 1.9 %collective-permute-start.4 = (bf16[512,128]{1,0:T(8,128)(2,1)S(1)}, bf16[512,128]{1,0:T(8,128)(2,1)S(1)}, u32[]{:S(2)}, u32[]{:S(2)}) collective-permute-start(bf16[512,128]{1,0:T(8,128)(2,1)S(1)} %get-tuple-element.21), channel_id=1, source_target_pairs={{48,0},{96,48},{144,96},{192,144},{240,192},{288,240},{336,288},{3... | collective-permute-start | bytes 393224 | tf_op jit(solution)/shard_map/ppermute | solution.py:29
  103.7 7.8 %collective-permute-start.5 = (bf16[512,128]{1,0:T(8,128)(2,1)S(1)}, bf16[512,128]{1,0:T(8,128)(2,1)S(1)}, u32[]{:S(2)}, u32[]{:S(2)}) collective-permute-start(bf16[512,128]{1,0:T(8,128)(2,1)S(1)} %get-tuple-element.21), channel_id=1, source_target_pairs={{0,48},{48,96},{96,144},{144,192},{192,240},{240,288},{288,336},{3... | collective-permute-start | bytes 393224 | tf_op jit(solution)/shard_map/ppermute | solution.py:26
  111.6 1.8 all-gather.1
  113.4 8.3 %all_gather.31 = f32[4,16,128]{2,1,0:T(8,128)S(1)} all-gather(f32[2,16,128]{2,1,0:T(8,128)S(1)} %bitcast.99), channel_id=1, replica_groups=mesh['seq'=16,'grp_z'=12,'grp_y'=2,'grp_c'=2] {'grp_y'}, dimensions={0}, use_global_device_ids=true | all-gather | bytes 49152 | tf_op jit(solution)/shard_map/all_gather | solution.py:36
  121.7 21.7 %all_gather.32 = f32[48,16,128]{2,1,0:T(8,128)S(1)} all-gather(f32[4,16,128]{2,1,0:T(8,128)S(1)} %all_gather.31), channel_id=1, replica_groups=mesh['seq'=16,'grp_z'=12,'grp_y'=2,'grp_c'=2] {'grp_z'}, dimensions={0}, use_global_device_ids=true | all-gather | bytes 425984 | tf_op jit(solution)/shard_map/all_gather | solution.py:36
  143.4 0.4 fusion.35
  143.9 0.0 collective-permute-done.4
  143.9 0.3 convolution_add_fusion.6
  144.3 0.4 bitcast_reduce_fusion
  144.6 0.3 fusion.56
  145.0 1.9 %collective-permute-start.6 = (bf16[512,128]{1,0:T(8,128)(2,1)S(1)}, bf16[512,128]{1,0:T(8,128)(2,1)S(1)}, u32[]{:S(2)}, u32[]{:S(2)}) collective-permute-start(bf16[512,128]{1,0:T(8,128)(2,1)S(1)} %get-tuple-element.23), channel_id=1, source_target_pairs={{48,0},{96,48},{144,96},{192,144},{240,192},{288,240},{336,288},{3... | collective-permute-start | bytes 393224 | tf_op jit(solution)/shard_map/ppermute | solution.py:29
  146.9 7.8 %collective-permute-start.7 = (bf16[512,128]{1,0:T(8,128)(2,1)S(1)}, bf16[512,128]{1,0:T(8,128)(2,1)S(1)}, u32[]{:S(2)}, u32[]{:S(2)}) collective-permute-start(bf16[512,128]{1,0:T(8,128)(2,1)S(1)} %get-tuple-element.23), channel_id=1, source_target_pairs={{0,48},{48,96},{96,144},{144,192},{192,240},{240,288},{288,336},{3... | collective-permute-start | bytes 393224 | tf_op jit(solution)/shard_map/ppermute | solution.py:26
  154.7 1.8 all-gather.2
  156.6 8.3 %all_gather.34 = f32[4,16,128]{2,1,0:T(8,128)S(1)} all-gather(f32[2,16,128]{2,1,0:T(8,128)S(1)} %bitcast.100), channel_id=1, replica_groups=mesh['seq'=16,'grp_z'=12,'grp_y'=2,'grp_c'=2] {'grp_y'}, dimensions={0}, use_global_device_ids=true | all-gather | bytes 49152 | tf_op jit(solution)/shard_map/all_gather | solution.py:36
  164.9 23.6 %all_gather.35 = f32[48,16,128]{2,1,0:T(8,128)S(1)} all-gather(f32[4,16,128]{2,1,0:T(8,128)S(1)} %all_gather.34), channel_id=1, replica_groups=mesh['seq'=16,'grp_z'=12,'grp_y'=2,'grp_c'=2] {'grp_z'}, dimensions={0}, use_global_device_ids=true | all-gather | bytes 425984 | tf_op jit(solution)/shard_map/all_gather | solution.py:36
  188.5 0.4 fusion.33
  188.9 0.0 collective-permute-done.6
  188.9 0.3 convolution_add_fusion.4
  189.3 1.1 fusion.21
  (21 shorter events, 0.2 us)
Async XLA Ops:
  0.0 1.6 copy-start
  1.6 1.6 copy-start.1
  1.9 67.0 %copy-start.2 = (s32[1,1,3,4]{3,1,2,0:T(1,128)S(1)}, s32[1,1,3,4]{3,1,2,0:T(1,128)}, u32[]{:S(2)}) copy-start(s32[1,1,3,4]{3,1,2,0:T(1,128)} %param.6) | copy-start | bytes 148
  49.3 31.9 %collective-permute-start = (bf16[512,1024]{1,0:T(8,128)(2,1)S(1)}, bf16[512,1024]{1,0:T(8,128)(2,1)S(1)}, u32[]{:S(2)}, u32[]{:S(2)}) collective-permute-start(bf16[512,1024]{1,0:T(8,128)(2,1)S(1)} %get-tuple-element.7), channel_id=1, source_target_pairs={{48,0},{96,48},{144,96},{192,144},{240,192},{288,240},{336,288},{3... | collective-permute-start | bytes 3145736 | tf_op jit(solution)/shard_map/ppermute | solution.py:29
  52.5 43.4 %collective-permute-start.2 = (bf16[512,1024]{1,0:T(8,128)(2,1)S(1)}, bf16[512,1024]{1,0:T(8,128)(2,1)S(1)}, u32[]{:S(2)}, u32[]{:S(2)}) collective-permute-start(bf16[512,1024]{1,0:T(8,128)(2,1)S(1)} %get-tuple-element.7), channel_id=1, source_target_pairs={{0,48},{48,96},{96,144},{144,192},{192,240},{240,288},{288,336},{3... | collective-permute-start | bytes 3145736 | tf_op jit(solution)/shard_map/ppermute | solution.py:26
  59.1 41.6 %collective-permute-start.1 = (bf16[512,128]{1,0:T(8,128)(2,1)S(1)}, bf16[512,128]{1,0:T(8,128)(2,1)S(1)}, u32[]{:S(2)}, u32[]{:S(2)}) collective-permute-start(bf16[512,128]{1,0:T(8,128)(2,1)S(1)} %convert_bitcast_fusion.1), channel_id=1, source_target_pairs={{48,0},{96,48},{144,96},{192,144},{240,192},{288,240},{336,288},{3... | collective-permute-start | bytes 393224 | tf_op jit(solution)/shard_map/ppermute | solution.py:29
  61.0 40.0 %collective-permute-start.3 = (bf16[512,128]{1,0:T(8,128)(2,1)S(1)}, bf16[512,128]{1,0:T(8,128)(2,1)S(1)}, u32[]{:S(2)}, u32[]{:S(2)}) collective-permute-start(bf16[512,128]{1,0:T(8,128)(2,1)S(1)} %convert_bitcast_fusion.1), channel_id=1, source_target_pairs={{0,48},{48,96},{96,144},{144,192},{192,240},{240,288},{288,336},{3... | collective-permute-start | bytes 393224 | tf_op jit(solution)/shard_map/ppermute | solution.py:26
  101.8 42.1 %collective-permute-start.4 = (bf16[512,128]{1,0:T(8,128)(2,1)S(1)}, bf16[512,128]{1,0:T(8,128)(2,1)S(1)}, u32[]{:S(2)}, u32[]{:S(2)}) collective-permute-start(bf16[512,128]{1,0:T(8,128)(2,1)S(1)} %get-tuple-element.21), channel_id=1, source_target_pairs={{48,0},{96,48},{144,96},{192,144},{240,192},{288,240},{336,288},{3... | collective-permute-start | bytes 393224 | tf_op jit(solution)/shard_map/ppermute | solution.py:29
  103.7 40.5 %collective-permute-start.5 = (bf16[512,128]{1,0:T(8,128)(2,1)S(1)}, bf16[512,128]{1,0:T(8,128)(2,1)S(1)}, u32[]{:S(2)}, u32[]{:S(2)}) collective-permute-start(bf16[512,128]{1,0:T(8,128)(2,1)S(1)} %get-tuple-element.21), channel_id=1, source_target_pairs={{0,48},{48,96},{96,144},{144,192},{192,240},{240,288},{288,336},{3... | collective-permute-start | bytes 393224 | tf_op jit(solution)/shard_map/ppermute | solution.py:26
  145.0 44.0 %collective-permute-start.6 = (bf16[512,128]{1,0:T(8,128)(2,1)S(1)}, bf16[512,128]{1,0:T(8,128)(2,1)S(1)}, u32[]{:S(2)}, u32[]{:S(2)}) collective-permute-start(bf16[512,128]{1,0:T(8,128)(2,1)S(1)} %get-tuple-element.23), channel_id=1, source_target_pairs={{48,0},{96,48},{144,96},{192,144},{240,192},{288,240},{336,288},{3... | collective-permute-start | bytes 393224 | tf_op jit(solution)/shard_map/ppermute | solution.py:29
  146.9 42.4 %collective-permute-start.7 = (bf16[512,128]{1,0:T(8,128)(2,1)S(1)}, bf16[512,128]{1,0:T(8,128)(2,1)S(1)}, u32[]{:S(2)}, u32[]{:S(2)}) collective-permute-start(bf16[512,128]{1,0:T(8,128)(2,1)S(1)} %get-tuple-element.23), channel_id=1, source_target_pairs={{0,48},{48,96},{96,144},{144,192},{192,240},{240,288},{288,336},{3... | collective-permute-start | bytes 393224 | tf_op jit(solution)/shard_map/ppermute | solution.py:26

commit v3 on v2

--- a/solution.py
+++ b/solution.py
@@ -17,18 +17,14 @@
 GRP_PARTS = ("grp_z", "grp_y", "grp_c")
 
 
-def padded(block, sides, width):
-    for axis, dim in sides:
-        count = lax.axis_size(axis)
-        forward = [(i, i + 1) for i in range(count - 1)]
-        forward.append((count - 1, 0))
-        backward = [(target, source) for source, target in forward]
-        low = lax.ppermute(
-            lax.slice_in_dim(block, block.shape[dim] - width, None, axis=dim), axis, forward
-        )
-        high = lax.ppermute(lax.slice_in_dim(block, 0, width, axis=dim), axis, backward)
-        block = jnp.concatenate([low, block, high], axis=dim)
-    return block
+def from_next(block):
+    count = lax.axis_size("seq")
+    return lax.ppermute(block, "seq", [((i + 1) % count, i) for i in range(count)])
+
+
+def from_prev(block):
+    count = lax.axis_size("seq")
+    return lax.ppermute(block, "seq", [(i, (i + 1) % count) for i in range(count)])
 
 
 def gather_groups(value):
@@ -74,26 +70,30 @@
     table = first[:, :centre_rows].reshape(groups, width)
     pair_weight = jnp.exp(pair_scale * jnp.dot(table, centre_unit, precision=highest))
     unit_send, first = lax.optimization_barrier((unit_emb, first))
-    extended = padded(unit_send, (("seq", 0),), row_count)
-    before_unit = extended[:row_count]
-    after_unit = extended[2 * row_count :]
+    after_unit = from_next(unit_send)
     next_tile = kernel_tile(unit_emb, after_unit, False)
-    prior_tile = kernel_tile(unit_emb, before_unit, False)
-    degree = (
-        self_rows
-        + jnp.sum(next_tile, axis=1, dtype=jnp.float32)
-        + jnp.sum(prior_tile, axis=1, dtype=jnp.float32)
-    )
+    next_rows = jnp.sum(next_tile, axis=1, dtype=jnp.float32)
+    next_cols = jnp.sum(next_tile, axis=0, dtype=jnp.float32)
     labels = seed
     count_value = counts[0, 0].astype(jnp.float32)
     member = jnp.arange(groups, dtype=jnp.int32)
+    col_rows = row_count // classes
     for iteration in range(STEPS):
         label_bf = labels.astype(jnp.bfloat16)
-        widened = padded(label_bf, (("seq", 0),), row_count)
+        ahead = from_next(label_bf)
+        back = lax.dot_general(
+            next_tile, label_bf, (((0,), (0,)), ((), ())), preferred_element_type=jnp.float32
+        )
+        if iteration == 0:
+            packet = from_prev(jnp.concatenate([back, next_cols.reshape(col_rows, classes)]))
+            back_in = packet[:row_count]
+            degree = self_rows + next_rows + packet[row_count:].reshape(row_count)
+        else:
+            back_in = from_prev(back)
         local = jnp.dot(self_tile, label_bf, preferred_element_type=jnp.float32) + jnp.dot(
-            next_tile, widened[2 * row_count :], preferred_element_type=jnp.float32
+            next_tile, ahead, preferred_element_type=jnp.float32
         )
-        local = local + jnp.dot(prior_tile, widened[:row_count], preferred_element_type=jnp.float32)
+        local = local + back_in
         spread = local / degree[:, None]
         if iteration == 0:
             gathered = first[:, centre_rows:]

time: 191 us -> 180 us (0.942)
  the two profiles are of different devices: /device:TPU:62 before, /device:TPU:30 now
where the time goes in v3:
time: 180 us
  blocking collectives  112 us (62%)
  waiting for transfers between devices  28.9 us (16%)
  starting transfers between devices  26.4 us (15%)
  matrix products  7.06 us (4%)
  other arithmetic  2.86 us (2%)
    all_gather x9, blocking collectives, gather_groups(): value = lax.all_gather(value, axis, axis=0, tiled=True)  112 us
    ppermute x4, waiting for transfers between devices, from_next(): lax.ppermute(block, 'seq', [((i + 1) % count, i) for i in range(count)])  21.6 us
    ppermute x3, starting transfers between devices, from_prev(): lax.ppermute(block, 'seq', [(i, (i + 1) % count) for i in range(count)])  17.8 us
    ppermute x4, starting transfers between devices, from_next(): lax.ppermute(block, 'seq', [((i + 1) % count, i) for i in range(count)])  8.59 us
    ppermute x3, waiting for transfers between devices, from_prev(): lax.ppermute(block, 'seq', [(i, (i + 1) % count) for i in range(count)])  7.37 us
  transfers between devices with their start and end apart: 7, of which 2 were waited for; matrix products, arithmetic and copies ran while one was open for 2% of the time, Pallas kernels for 0%

profile of v3, /device:TPU:30, one launch (start us, length us, event | category | flops | bytes accessed | tf_op | source)
XLA Modules:
  0.0 179.6 jit_solution(12873401297169062973)
XLA Ops:
  0.0 1.6 fusion.2
  1.6 0.0 copy-done
  1.6 0.0 copy-start.1
  1.6 0.3 convert_reduce_fusion
  1.9 0.6 copy-done.1
  2.6 0.6 multiply_reduce_fusion
  3.9 1.8 %all-gather = f32[48,128]{1,0:T(8,128)S(1)} all-gather(f32[24,128]{1,0:T(8,128)S(1)} %pad_maximum_fusion.1), channel_id=2, replica_groups=mesh['seq'=16,'grp_z'=12,'grp_y'=2,'grp_c'=2] {'grp_c'}, dimensions={0}, use_global_device_ids=true | all-gather | bytes 36864 | tf_op jit(solution)/shard_map/all_gather | solution.py:32
  5.8 8.4 %all_gather.28 = f32[4,24,128]{2,1,0:T(8,128)S(1)} all-gather(f32[2,24,128]{2,1,0:T(8,128)S(1)} %bitcast.101), channel_id=1, replica_groups=mesh['seq'=16,'grp_z'=12,'grp_y'=2,'grp_c'=2] {'grp_y'}, dimensions={0}, use_global_device_ids=true | all-gather | bytes 73728 | tf_op jit(solution)/shard_map/all_gather | solution.py:32
  14.2 35.9 %all_gather.29 = f32[48,24,128]{2,1,0:T(8,128)S(1)} all-gather(f32[4,24,128]{2,1,0:T(8,128)S(1)} %all_gather.28), channel_id=1, replica_groups=mesh['seq'=16,'grp_z'=12,'grp_y'=2,'grp_c'=2] {'grp_z'}, dimensions={0}, use_global_device_ids=true | all-gather | bytes 638976 | tf_op jit(solution)/shard_map/all_gather | solution.py:32
  50.0 2.6 %collective-permute-start = (bf16[512,1024]{1,0:T(8,128)(2,1)S(1)}, bf16[512,1024]{1,0:T(8,128)(2,1)S(1)}, u32[]{:S(2)}, u32[]{:S(2)}) collective-permute-start(bf16[512,1024]{1,0:T(8,128)(2,1)S(1)} %get-tuple-element.7), channel_id=1, source_target_pairs={{48,0},{96,48},{144,96},{192,144},{240,192},{288,240},{336,288},{3... | collective-permute-start | bytes 3145736 | tf_op jit(solution)/shard_map/ppermute | solution.py:22
  52.6 2.2 %collective-permute-start.1 = (bf16[512,128]{1,0:T(8,128)(2,1)S(1)}, bf16[512,128]{1,0:T(8,128)(2,1)S(1)}, u32[]{:S(2)}, u32[]{:S(2)}) collective-permute-start(bf16[512,128]{1,0:T(8,128)(2,1)S(1)} %convert_bitcast_fusion.1), channel_id=1, source_target_pairs={{48,0},{96,48},{144,96},{192,144},{240,192},{288,240},{336,288},{3... | collective-permute-start | bytes 393224 | tf_op jit(solution)/shard_map/ppermute | solution.py:22
  54.9 0.0 copy-done.2
  54.9 0.1 convert_reduce_fusion.6
  55.6 0.1 convert_reduce_fusion.5
  55.7 0.2 fusion.29
  55.9 0.5 fusion.37
  56.4 0.9 convert_reduce_fusion.3
  57.4 21.5 %collective-permute-done = bf16[512,1024]{1,0:T(8,128)(2,1)S(1)} collective-permute-done((bf16[512,1024]{1,0:T(8,128)(2,1)S(1)}, bf16[512,1024]{1,0:T(8,128)(2,1)S(1)}, u32[]{:S(2)}, u32[]{:S(2)}) %collective-permute-start) | collective-permute-done | bytes 1048608 | tf_op jit(solution)/shard_map/ppermute | solution.py:22
  78.9 0.9 convert_reduce_fusion.1
  79.8 0.3 fusion.56
  80.2 1.9 %collective-permute-start.2 = (f32[516,128]{1,0:T(8,128)S(1)}, f32[516,128]{1,0:T(8,128)S(1)}, u32[]{:S(2)}, u32[]{:S(2)}) collective-permute-start(f32[516,128]{1,0:T(8,128)S(1)} %pad_maximum_fusion), channel_id=1, source_target_pairs={{0,48},{48,96},{96,144},{144,192},{192,240},{240,288},{288,336},{3... | collective-permute-start | bytes 792584 | tf_op jit(solution)/shard_map/ppermute | solution.py:27
  82.1 0.1 convert_reduce_fusion.4
  82.2 0.3 fusion.55
  82.5 7.4 %collective-permute-done.2 = f32[516,128]{1,0:T(8,128)S(1)} collective-permute-done((f32[516,128]{1,0:T(8,128)S(1)}, f32[516,128]{1,0:T(8,128)S(1)}, u32[]{:S(2)}, u32[]{:S(2)}) %collective-permute-start.2) | collective-permute-done | bytes 264224 | tf_op jit(solution)/shard_map/ppermute | solution.py:27
  89.9 0.0 collective-permute-done.1
  89.9 0.4 bitcast_reduce_fusion.1
  90.3 0.3 fusion.58
  90.6 0.3 fusion.57
  90.9 1.9 %collective-permute-start.3 = (bf16[512,128]{1,0:T(8,128)(2,1)S(1)}, bf16[512,128]{1,0:T(8,128)(2,1)S(1)}, u32[]{:S(2)}, u32[]{:S(2)}) collective-permute-start(bf16[512,128]{1,0:T(8,128)(2,1)S(1)} %get-tuple-element.20), channel_id=1, source_target_pairs={{48,0},{96,48},{144,96},{192,144},{240,192},{288,240},{336,288},{3... | collective-permute-start | bytes 393224 | tf_op jit(solution)/shard_map/ppermute | solution.py:22
  92.9 1.8 %all-gather.1 = f32[32,128]{1,0:T(8,128)S(1)} all-gather(f32[16,128]{1,0:T(8,128)S(1)} %broadcast_multiply_fusion.1), channel_id=3, replica_groups=mesh['seq'=16,'grp_z'=12,'grp_y'=2,'grp_c'=2] {'grp_c'}, dimensions={0}, use_global_device_ids=true | all-gather | bytes 24576 | tf_op jit(solution)/shard_map/all_gather | solution.py:32
  94.7 8.3 %all_gather.31 = f32[4,16,128]{2,1,0:T(8,128)S(1)} all-gather(f32[2,16,128]{2,1,0:T(8,128)S(1)} %bitcast.102), channel_id=1, replica_groups=mesh['seq'=16,'grp_z'=12,'grp_y'=2,'grp_c'=2] {'grp_y'}, dimensions={0}, use_global_device_ids=true | all-gather | bytes 49152 | tf_op jit(solution)/shard_map/all_gather | solution.py:32
  103.0 7.9 %collective-permute-start.4 = (f32[512,128]{1,0:T(8,128)S(1)}, f32[512,128]{1,0:T(8,128)S(1)}, u32[]{:S(2)}, u32[]{:S(2)}) collective-permute-start(f32[512,128]{1,0:T(8,128)S(1)} %fusion.58), channel_id=1, source_target_pairs={{0,48},{48,96},{96,144},{144,192},{192,240},{240,288},{288,336},{3... | collective-permute-start | bytes 786440 | tf_op jit(solution)/shard_map/ppermute | solution.py:27
  110.9 21.8 %all_gather.32 = f32[48,16,128]{2,1,0:T(8,128)S(1)} all-gather(f32[4,16,128]{2,1,0:T(8,128)S(1)} %all_gather.31), channel_id=1, replica_groups=mesh['seq'=16,'grp_z'=12,'grp_y'=2,'grp_c'=2] {'grp_z'}, dimensions={0}, use_global_device_ids=true | all-gather | bytes 425984 | tf_op jit(solution)/shard_map/all_gather | solution.py:32
  132.7 0.4 fusion.35
  133.1 0.0 collective-permute-done.3
  133.1 0.0 collective-permute-done.4
  133.1 0.4 bitcast_reduce_fusion
  133.5 0.3 fusion.60
  133.8 0.3 fusion.59
  134.1 1.9 %collective-permute-start.5 = (bf16[512,128]{1,0:T(8,128)(2,1)S(1)}, bf16[512,128]{1,0:T(8,128)(2,1)S(1)}, u32[]{:S(2)}, u32[]{:S(2)}) collective-permute-start(bf16[512,128]{1,0:T(8,128)(2,1)S(1)} %get-tuple-element.22), channel_id=1, source_target_pairs={{48,0},{96,48},{144,96},{192,144},{240,192},{288,240},{336,288},{3... | collective-permute-start | bytes 393224 | tf_op jit(solution)/shard_map/ppermute | solution.py:22
  136.1 1.8 %all-gather.2 = f32[32,128]{1,0:T(8,128)S(1)} all-gather(f32[16,128]{1,0:T(8,128)S(1)} %broadcast_multiply_fusion), channel_id=4, replica_groups=mesh['seq'=16,'grp_z'=12,'grp_y'=2,'grp_c'=2] {'grp_c'}, dimensions={0}, use_global_device_ids=true | all-gather | bytes 24576 | tf_op jit(solution)/shard_map/all_gather | solution.py:32
  137.9 8.3 %all_gather.34 = f32[4,16,128]{2,1,0:T(8,128)S(1)} all-gather(f32[2,16,128]{2,1,0:T(8,128)S(1)} %bitcast.103), channel_id=1, replica_groups=mesh['seq'=16,'grp_z'=12,'grp_y'=2,'grp_c'=2] {'grp_y'}, dimensions={0}, use_global_device_ids=true | all-gather | bytes 49152 | tf_op jit(solution)/shard_map/all_gather | solution.py:32
  146.2 7.9 %collective-permute-start.6 = (f32[512,128]{1,0:T(8,128)S(1)}, f32[512,128]{1,0:T(8,128)S(1)}, u32[]{:S(2)}, u32[]{:S(2)}) collective-permute-start(f32[512,128]{1,0:T(8,128)S(1)} %fusion.60), channel_id=1, source_target_pairs={{0,48},{48,96},{96,144},{144,192},{192,240},{240,288},{288,336},{3... | collective-permute-start | bytes 786440 | tf_op jit(solution)/shard_map/ppermute | solution.py:27
  154.1 23.9 %all_gather.35 = f32[48,16,128]{2,1,0:T(8,128)S(1)} all-gather(f32[4,16,128]{2,1,0:T(8,128)S(1)} %all_gather.34), channel_id=1, replica_groups=mesh['seq'=16,'grp_z'=12,'grp_y'=2,'grp_c'=2] {'grp_z'}, dimensions={0}, use_global_device_ids=true | all-gather | bytes 425984 | tf_op jit(solution)/shard_map/all_gather | solution.py:32
  178.1 0.4 fusion.33
  178.5 0.0 collective-permute-done.5
  178.5 0.0 collective-permute-done.6
  178.5 1.1 fusion.19
  (19 shorter events, 0.2 us)
Async XLA Ops:
  0.0 1.6 copy-start
  1.6 1.0 copy-start.1
  14.2 40.7 %copy-start.2 = (s32[1,1,3,4]{3,1,2,0:T(1,128)S(1)}, s32[1,1,3,4]{3,1,2,0:T(1,128)}, u32[]{:S(2)}) copy-start(s32[1,1,3,4]{3,1,2,0:T(1,128)} %param.6) | copy-start | bytes 148
  50.0 28.9 %collective-permute-start = (bf16[512,1024]{1,0:T(8,128)(2,1)S(1)}, bf16[512,1024]{1,0:T(8,128)(2,1)S(1)}, u32[]{:S(2)}, u32[]{:S(2)}) collective-permute-start(bf16[512,1024]{1,0:T(8,128)(2,1)S(1)} %get-tuple-element.7), channel_id=1, source_target_pairs={{48,0},{96,48},{144,96},{192,144},{240,192},{288,240},{336,288},{3... | collective-permute-start | bytes 3145736 | tf_op jit(solution)/shard_map/ppermute | solution.py:22
  52.6 37.3 %collective-permute-start.1 = (bf16[512,128]{1,0:T(8,128)(2,1)S(1)}, bf16[512,128]{1,0:T(8,128)(2,1)S(1)}, u32[]{:S(2)}, u32[]{:S(2)}) collective-permute-start(bf16[512,128]{1,0:T(8,128)(2,1)S(1)} %convert_bitcast_fusion.1), channel_id=1, source_target_pairs={{48,0},{96,48},{144,96},{192,144},{240,192},{288,240},{336,288},{3... | collective-permute-start | bytes 393224 | tf_op jit(solution)/shard_map/ppermute | solution.py:22
  80.2 9.7 %collective-permute-start.2 = (f32[516,128]{1,0:T(8,128)S(1)}, f32[516,128]{1,0:T(8,128)S(1)}, u32[]{:S(2)}, u32[]{:S(2)}) collective-permute-start(f32[516,128]{1,0:T(8,128)S(1)} %pad_maximum_fusion), channel_id=1, source_target_pairs={{0,48},{48,96},{96,144},{144,192},{192,240},{240,288},{288,336},{3... | collective-permute-start | bytes 792584 | tf_op jit(solution)/shard_map/ppermute | solution.py:27
  90.9 42.2 %collective-permute-start.3 = (bf16[512,128]{1,0:T(8,128)(2,1)S(1)}, bf16[512,128]{1,0:T(8,128)(2,1)S(1)}, u32[]{:S(2)}, u32[]{:S(2)}) collective-permute-start(bf16[512,128]{1,0:T(8,128)(2,1)S(1)} %get-tuple-element.20), channel_id=1, source_target_pairs={{48,0},{96,48},{144,96},{192,144},{240,192},{288,240},{336,288},{3... | collective-permute-start | bytes 393224 | tf_op jit(solution)/shard_map/ppermute | solution.py:22
  103.0 30.1 %collective-permute-start.4 = (f32[512,128]{1,0:T(8,128)S(1)}, f32[512,128]{1,0:T(8,128)S(1)}, u32[]{:S(2)}, u32[]{:S(2)}) collective-permute-start(f32[512,128]{1,0:T(8,128)S(1)} %fusion.58), channel_id=1, source_target_pairs={{0,48},{48,96},{96,144},{144,192},{192,240},{240,288},{288,336},{3... | collective-permute-start | bytes 786440 | tf_op jit(solution)/shard_map/ppermute | solution.py:27
  134.1 44.4 %collective-permute-start.5 = (bf16[512,128]{1,0:T(8,128)(2,1)S(1)}, bf16[512,128]{1,0:T(8,128)(2,1)S(1)}, u32[]{:S(2)}, u32[]{:S(2)}) collective-permute-start(bf16[512,128]{1,0:T(8,128)(2,1)S(1)} %get-tuple-element.22), channel_id=1, source_target_pairs={{48,0},{96,48},{144,96},{192,144},{240,192},{288,240},{336,288},{3... | collective-permute-start | bytes 393224 | tf_op jit(solution)/shard_map/ppermute | solution.py:22
  146.2 32.3 %collective-permute-start.6 = (f32[512,128]{1,0:T(8,128)S(1)}, f32[512,128]{1,0:T(8,128)S(1)}, u32[]{:S(2)}, u32[]{:S(2)}) collective-permute-start(f32[512,128]{1,0:T(8,128)S(1)} %fusion.60), channel_id=1, source_target_pairs={{0,48},{48,96},{96,144},{144,192},{192,240},{240,288},{288,336},{3... | collective-permute-start | bytes 786440 | tf_op jit(solution)/shard_map/ppermute | solution.py:27

commit v4 on v3

v4 whole, which is shorter than its diff:
```python
import numpy as np
import jax
import jax.numpy as jnp
from jax import lax
from jax.sharding import Mesh, PartitionSpec as P

CLUS = 32
STEPS = 3


tile_scale = 8.0
pair_scale = 2.0
keep_share = 0.2
eps = 1e-06
highest = lax.Precision.HIGHEST

GRP_PARTS = ("grp_z", "grp_y", "grp_c")


def from_next(block):
    count = lax.axis_size("seq")
    return lax.ppermute(block, "seq", [((i + 1) % count, i) for i in range(count)])


def from_prev(block):
    count = lax.axis_size("seq")
    return lax.ppermute(block, "seq", [(i, (i + 1) % count) for i in range(count)])


def gather_groups(value):
    for axis in reversed(GRP_PARTS):
        value = lax.all_gather(value, axis, axis=0, tiled=True)
    return value


def normalized(values):
    floats = values.astype(jnp.float32)
    return (floats * lax.rsqrt(jnp.sum(floats * floats, axis=-1, keepdims=True) + eps)).astype(
        jnp.bfloat16
    )


def kernel_tile(left, right, blank):
    score = jnp.dot(left, right.T, preferred_element_type=jnp.float32)
    weights = jnp.exp(tile_scale * (score - 1.0))
    if blank:
        weights = weights * (1.0 - jnp.eye(left.shape[0], dtype=jnp.float32))
    return weights.astype(jnp.bfloat16)


def body(groups, parts, embeddings, seed_labels, sources, counts):
    row_count = embeddings.shape[2]
    classes = seed_labels.shape[3]
    width = embeddings.shape[3]
    unit_emb = normalized(embeddings[0, 0])
    self_tile = kernel_tile(unit_emb, unit_emb, True)
    self_rows = jnp.sum(self_tile, axis=1, dtype=jnp.float32)
    centre = jnp.mean(unit_emb, axis=0, dtype=jnp.float32)
    centre_unit = centre * lax.rsqrt(jnp.sum(centre * centre) + eps)
    seed = seed_labels[0, 0]
    coarse_count = row_count // CLUS
    centre_rows = width // classes
    col_rows = row_count // classes
    steps, slots = sources.shape[2], sources.shape[3]
    me = lax.axis_index(GRP_PARTS[0])
    for axis, size in zip(GRP_PARTS[1:], parts[1:]):
        me = me * size + lax.axis_index(axis)

    def summarize(values):
        return jnp.sum(values.reshape(coarse_count, CLUS, classes), axis=1) / CLUS

    def rows_of(far):
        return jnp.broadcast_to(far[:, None, :], (coarse_count, CLUS, classes)).reshape(
            row_count, classes
        )

    after_unit = from_next(unit_emb)
    next_tile = kernel_tile(unit_emb, after_unit, False)
    next_rows = jnp.sum(next_tile, axis=1, dtype=jnp.float32)
    next_cols = jnp.sum(next_tile, axis=0, dtype=jnp.float32)

    def spread_of(labels, first):
        label_bf = labels.astype(jnp.bfloat16)
        ahead = from_next(label_bf)
        back = lax.dot_general(
            next_tile, label_bf, (((0,), (0,)), ((), ())), preferred_element_type=jnp.float32
        )
        if first:
            packet = from_prev(jnp.concatenate([back, next_cols.reshape(col_rows, classes)]))
            back_in = packet[:row_count]
            degree = self_rows + next_rows + packet[row_count:].reshape(row_count)
        else:
            back_in, degree = from_prev(back), None
        local = jnp.dot(self_tile, label_bf, preferred_element_type=jnp.float32) + jnp.dot(
            next_tile, ahead, preferred_element_type=jnp.float32
        )
        return local + back_in, degree

    local, degree = spread_of(seed, True)
    spread = local / degree[:, None]

    info = jnp.zeros((1, classes), jnp.float32)
    info = info.at[0, : steps * slots].set(sources[0, 0].reshape(-1).astype(jnp.float32))
    info = info.at[0, steps * slots].set(counts[0, 0].astype(jnp.float32))
    seed_mean = summarize(seed)
    table_a = gather_groups(
        jnp.concatenate(
            [centre_unit.reshape(centre_rows, classes), seed_mean, summarize(spread), info]
        )[None]
    )
    table = table_a[:, :centre_rows].reshape(groups, width)
    seed_means = table_a[:, centre_rows : centre_rows + coarse_count]
    spread_means = table_a[:, centre_rows + coarse_count : centre_rows + 2 * coarse_count]
    info_all = table_a[:, centre_rows + 2 * coarse_count]
    source_all = jnp.round(info_all[:, : steps * slots]).astype(jnp.int32).reshape(groups, steps, slots)
    count_all = info_all[:, steps * slots]
    pair_weight = jnp.exp(pair_scale * jnp.dot(table, table.T, precision=highest))
    member = jnp.arange(groups, dtype=jnp.int32)

    def far_all(iteration, summary):
        chosen = jnp.sum(
            (source_all[:, iteration, :, None] == member[None, None, :]).astype(jnp.float32), axis=1
        )
        coefficient = chosen * pair_weight / count_all[:, None]
        return jnp.einsum("gh,hkc->gkc", coefficient, summary, precision=highest)

    def own(values):
        return lax.dynamic_index_in_dim(values, me, axis=0, keepdims=False)

    def next_summary(spread_mean, far):
        return keep_share * seed_means + (1.0 - keep_share) * (spread_mean + far)

    far_0 = far_all(0, seed_means)
    far_1 = far_all(1, next_summary(spread_means, far_0))
    labels = keep_share * seed + (1.0 - keep_share) * (spread + rows_of(own(far_0)))

    local, _ = spread_of(labels, False)
    spread = local / degree[:, None]
    labels = keep_share * seed + (1.0 - keep_share) * (spread + rows_of(own(far_1)))
    spread_means = gather_groups(summarize(spread)[None])
    far_2 = far_all(2, next_summary(spread_means, far_1))

    local, _ = spread_of(labels, False)
    spread = local / degree[:, None]
    labels = keep_share * seed + (1.0 - keep_share) * (spread + rows_of(own(far_2)))
    return labels[None, None]


def solution(mesh):
    groups = mesh.shape["grp"]
    devices = np.asarray(mesh.devices)
    if groups % 4 == 0:
        parts = (groups // 4, 2, 2)
    else:
        parts = (groups, 1, 1)
    split = Mesh(devices.reshape((mesh.shape["seq"],) + parts), ("seq",) + GRP_PARTS)
    block = P("seq", GRP_PARTS, None, None)
    return jax.shard_map(
        lambda *args: body(groups, parts, *args),
        mesh=split,
        in_specs=(block, block, block, P("seq", GRP_PARTS)),
        out_specs=block,
        check_vma=False,
    )
```

time: 180 us -> 161 us (0.89)
  the two profiles are of different devices: /device:TPU:30 before, /device:TPU:64 now
where the time goes in v4:
time: 161 us
  blocking collectives  82 us (51%)
  waiting for transfers between devices  34.1 us (21%)
  starting transfers between devices  23.7 us (15%)
  matrix products  9.52 us (6%)
  other arithmetic  7.2 us (4%)
  local copies, waits for them, and re-layouts  2.38 us (1%)
  between operations  1.73 us (1%)
    all_gather x6, blocking collectives, gather_groups(): value = lax.all_gather(value, axis, axis=0, tiled=True)  82 us
    ppermute x4, waiting for transfers between devices, from_next(): lax.ppermute(block, 'seq', [((i + 1) % count, i) for i in range(count)])  19.2 us
    ppermute x4, starting transfers between devices, from_next(): lax.ppermute(block, 'seq', [((i + 1) % count, i) for i in range(count)])  15.9 us
    ppermute x3, waiting for transfers between devices, from_prev(): lax.ppermute(block, 'seq', [(i, (i + 1) % count) for i in range(count)])  14.9 us
    ppermute x3, starting transfers between devices, from_prev(): lax.ppermute(block, 'seq', [(i, (i + 1) % count) for i in range(count)])  7.76 us
    dot_general x2, matrix products, kernel_tile(): score = jnp.dot(left, right.T, preferred_element_type=jnp.float32)  3.38 us
  transfers between devices with their start and end apart: 7, of which 4 were waited for; matrix products, arithmetic and copies ran while one was open for 8% of the time, Pallas kernels for 0%

profile of v4, /device:TPU:64, one launch (start us, length us, event | category | flops | bytes accessed | tf_op | source)
XLA Modules:
  0.0 160.6 jit_solution(15895855726830947813)
XLA Ops:
  0.0 1.6 fusion.2
  1.6 1.3 convert_reduce_fusion
  2.9 7.7 %collective-permute-start = (bf16[512,1024]{1,0:T(8,128)(2,1)}, bf16[512,1024]{1,0:T(8,128)(2,1)}, u32[]{:S(2)}, u32[]{:S(2)}) collective-permute-start(bf16[512,1024]{1,0:T(8,128)(2,1)} %get-tuple-element.32), channel_id=1, source_target_pairs={{48,0},{96,48},{144,96},{192,144},{240,192},{288,240},{336,288},{3... | collective-permute-start | bytes 3145736 | tf_op jit(solution)/shard_map/ppermute | solution.py:22
  10.7 2.4 %collective-permute-start.1 = (bf16[512,128]{1,0:T(8,128)(2,1)S(1)}, bf16[512,128]{1,0:T(8,128)(2,1)S(1)}, u32[]{:S(2)}, u32[]{:S(2)}) collective-permute-start(bf16[512,128]{1,0:T(8,128)(2,1)S(1)} %convert_bitcast_fusion.1), channel_id=1, source_target_pairs={{48,0},{96,48},{144,96},{192,144},{240,192},{288,240},{336,288},{3... | collective-permute-start | bytes 393224 | tf_op jit(solution)/shard_map/ppermute | solution.py:22
  13.0 0.6 multiply_reduce_fusion
  14.3 0.6 and_reduce_fusion
  15.0 0.6 fusion.62
  15.6 0.9 convert_reduce_fusion.3
  16.6 17.9 %collective-permute-done = bf16[512,1024]{1,0:T(8,128)(2,1)} collective-permute-done((bf16[512,1024]{1,0:T(8,128)(2,1)}, bf16[512,1024]{1,0:T(8,128)(2,1)}, u32[]{:S(2)}, u32[]{:S(2)}) %collective-permute-start) | collective-permute-done | bytes 1048608 | tf_op jit(solution)/shard_map/ppermute | solution.py:22
  34.5 2.4 %convert_reduce_fusion.1 = (f32[512]{0:T(512)S(1)}, f32[512]{0:T(512)S(1)}, bf16[512,512]{0,1:T(8,128)(2,1)S(1)}) fusion(bf16[512,1024]{1,0:T(8,128)(2,1)} %get-tuple-element.32, bf16[512,1024]{1,0:T(8,128)(2,1)} %collective-permute-done), kind=kOutput, calls=%fused_computation.15 | convolution fusion | flops 538442752 | bytes 2625536 | tf_op jit(solution)/shard_map/dot_general | solution.py:44
  36.9 0.3 fusion.71
  37.3 1.9 %collective-permute-start.2 = (f32[516,128]{1,0:T(8,128)S(1)}, f32[516,128]{1,0:T(8,128)S(1)}, u32[]{:S(2)}, u32[]{:S(2)}) collective-permute-start(f32[516,128]{1,0:T(8,128)S(1)} %pad_maximum_fusion), channel_id=1, source_target_pairs={{0,48},{48,96},{96,144},{144,192},{192,240},{240,288},{288,336},{3... | collective-permute-start | bytes 792584 | tf_op jit(solution)/shard_map/ppermute | solution.py:27
  39.2 0.1 reshape.165
  39.3 0.7 slice.71
  40.7 1.9 %fusion.69 = f32[1,1]{1,0:T(1,128)} fusion(pred[1,1]{1,0:T(4,128)(4,1)} %bitcast.9, f32[1,1]{1,0:T(1,128)S(6)} %convert_element_type.90, s32[]{:T(128)} %bitcast.10, f32[1,12]{1,0:T(1,128)S(1)} %reshape.165), kind=kLoop, calls=%fused_computation.114 | loop fusion | flops 1 | bytes 61 | tf_op jit(solution)/shard_map/select.3
  42.6 1.4 scatter.9
  44.0 0.3 fusion.70
  44.3 5.7 %collective-permute-done.2 = f32[516,128]{1,0:T(8,128)S(1)} collective-permute-done((f32[516,128]{1,0:T(8,128)S(1)}, f32[516,128]{1,0:T(8,128)S(1)}, u32[]{:S(2)}, u32[]{:S(2)}) %collective-permute-start.2) | collective-permute-done | bytes 264224 | tf_op jit(solution)/shard_map/ppermute | solution.py:27
  50.0 0.4 bitcast_reduce_fusion.1
  50.3 1.8 %all-gather.2 = f32[2,41,128]{2,1,0:T(8,128)S(1)} all-gather(f32[1,41,128]{2,1,0:T(8,128)S(1)} %maximum_bitcast_fusion), channel_id=2, replica_groups=mesh['seq'=16,'grp_z'=12,'grp_y'=2,'grp_c'=2] {'grp_c'}, dimensions={0}, use_global_device_ids=true | all-gather | bytes 62976 | tf_op jit(solution)/shard_map/all_gather | solution.py:32
  52.2 8.7 %all_gather.19 = f32[4,41,128]{2,1,0:T(8,128)S(1)} all-gather(f32[2,41,128]{2,1,0:T(8,128)S(1)} %all-gather.2), channel_id=1, replica_groups=mesh['seq'=16,'grp_z'=12,'grp_y'=2,'grp_c'=2] {'grp_y'}, dimensions={0}, use_global_device_ids=true | all-gather | bytes 125952 | tf_op jit(solution)/shard_map/all_gather | solution.py:32
  60.8 37.1 %all_gather.20 = f32[48,41,128]{2,1,0:T(8,128)S(1)} all-gather(f32[4,41,128]{2,1,0:T(8,128)S(1)} %all_gather.19), channel_id=1, replica_groups=mesh['seq'=16,'grp_z'=12,'grp_y'=2,'grp_c'=2] {'grp_z'}, dimensions={0}, use_global_device_ids=true | all-gather | bytes 1091584 | tf_op jit(solution)/shard_map/all_gather | solution.py:32
  97.9 0.1 fusion.68
  98.0 0.1 copy.34
  98.1 0.3 fusion.23
  98.5 0.1 convert_reduce_fusion.6
  98.6 0.6 fusion.35
  99.2 0.1 fusion.42
  99.2 0.3 fusion.72
  99.6 0.3 fusion.73
  99.9 3.9 %collective-permute-start.3 = (bf16[512,128]{1,0:T(8,128)(2,1)S(1)}, bf16[512,128]{1,0:T(8,128)(2,1)S(1)}, u32[]{:S(2)}, u32[]{:S(2)}) collective-permute-start(bf16[512,128]{1,0:T(8,128)(2,1)S(1)} %fusion.42), channel_id=1, source_target_pairs={{48,0},{96,48},{144,96},{192,144},{240,192},{288,240},{336,288},{3... | collective-permute-start | bytes 393224 | tf_op jit(solution)/shard_map/ppermute | solution.py:22
  103.8 1.9 %collective-permute-start.4 = (f32[512,128]{1,0:T(8,128)S(1)}, f32[512,128]{1,0:T(8,128)S(1)}, u32[]{:S(2)}, u32[]{:S(2)}) collective-permute-start(f32[512,128]{1,0:T(8,128)S(1)} %fusion.73), channel_id=1, source_target_pairs={{0,48},{48,96},{96,144},{144,192},{192,240},{240,288},{288,336},{3... | collective-permute-start | bytes 786440 | tf_op jit(solution)/shard_map/ppermute | solution.py:27
  105.7 0.1 convert_reduce_fusion.5
  105.8 0.8 fusion.29
  106.7 0.1 convert_reduce_fusion.4
  106.8 1.3 collective-permute-done.3
  108.0 9.3 %collective-permute-done.4 = f32[512,128]{1,0:T(8,128)S(1)} collective-permute-done((f32[512,128]{1,0:T(8,128)S(1)}, f32[512,128]{1,0:T(8,128)S(1)}, u32[]{:S(2)}, u32[]{:S(2)}) %collective-permute-start.4) | collective-permute-done | bytes 262176 | tf_op jit(solution)/shard_map/ppermute | solution.py:27
  117.3 0.4 bitcast_reduce_fusion
  117.6 0.1 fusion.39
  117.7 0.3 fusion.75
  118.0 1.9 %collective-permute-start.5 = (bf16[512,128]{1,0:T(8,128)(2,1)S(1)}, bf16[512,128]{1,0:T(8,128)(2,1)S(1)}, u32[]{:S(2)}, u32[]{:S(2)}) collective-permute-start(bf16[512,128]{1,0:T(8,128)(2,1)S(1)} %fusion.39), channel_id=1, source_target_pairs={{48,0},{96,48},{144,96},{192,144},{240,192},{288,240},{336,288},{3... | collective-permute-start | bytes 393224 | tf_op jit(solution)/shard_map/ppermute | solution.py:22
  119.9 3.9 %collective-permute-start.6 = (f32[512,128]{1,0:T(8,128)S(1)}, f32[512,128]{1,0:T(8,128)S(1)}, u32[]{:S(2)}, u32[]{:S(2)}) collective-permute-start(f32[512,128]{1,0:T(8,128)S(1)} %fusion.75), channel_id=1, source_target_pairs={{0,48},{48,96},{96,144},{144,192},{192,240},{240,288},{288,336},{3... | collective-permute-start | bytes 786440 | tf_op jit(solution)/shard_map/ppermute | solution.py:27
  123.9 1.8 %all-gather.1 = f32[32,128]{1,0:T(8,128)S(1)} all-gather(f32[16,128]{1,0:T(8,128)S(1)} %broadcast_multiply_fusion), channel_id=3, replica_groups=mesh['seq'=16,'grp_z'=12,'grp_y'=2,'grp_c'=2] {'grp_c'}, dimensions={0}, use_global_device_ids=true | all-gather | bytes 24576 | tf_op jit(solution)/shard_map/all_gather | solution.py:32
  125.7 8.3 %all_gather.22 = f32[4,16,128]{2,1,0:T(8,128)S(1)} all-gather(f32[2,16,128]{2,1,0:T(8,128)S(1)} %bitcast.111), channel_id=1, replica_groups=mesh['seq'=16,'grp_z'=12,'grp_y'=2,'grp_c'=2] {'grp_y'}, dimensions={0}, use_global_device_ids=true | all-gather | bytes 49152 | tf_op jit(solution)/shard_map/all_gather | solution.py:32
  134.0 24.3 %all_gather.23 = f32[48,16,128]{2,1,0:T(8,128)S(1)} all-gather(f32[4,16,128]{2,1,0:T(8,128)S(1)} %all_gather.22), channel_id=1, replica_groups=mesh['seq'=16,'grp_z'=12,'grp_y'=2,'grp_c'=2] {'grp_z'}, dimensions={0}, use_global_device_ids=true | all-gather | bytes 425984 | tf_op jit(solution)/shard_map/all_gather | solution.py:32
  158.3 0.8 fusion.33
  159.1 0.3 fusion.74
  159.5 1.1 fusion.19
  (30 shorter events, 0.2 us)
Async XLA Ops:
  0.0 1.6 %copy-start.1 = (bf16[1,1,512,1024]{3,2,1,0:T(8,128)(2,1)S(1)}, bf16[1,1,512,1024]{3,2,1,0:T(8,128)(2,1)}, u32[]{:S(2)}) copy-start(bf16[1,1,512,1024]{3,2,1,0:T(8,128)(2,1)} %param.8) | copy-start | bytes 3145732
  1.6 9.0 %copy-start = (f32[1,1,512,128]{3,2,1,0:T(8,128)S(1)}, f32[1,1,512,128]{3,2,1,0:T(8,128)}, u32[]{:S(2)}) copy-start(f32[1,1,512,128]{3,2,1,0:T(8,128)} %param.9) | copy-start | bytes 786436
  1.6 13.4 %copy-start.2 = (s32[1,1,3,4]{3,1,2,0:T(1,128)S(1)}, s32[1,1,3,4]{3,1,2,0:T(1,128)}, u32[]{:S(2)}) copy-start(s32[1,1,3,4]{3,1,2,0:T(1,128)} %param.10) | copy-start | bytes 148
  2.9 31.6 %collective-permute-start = (bf16[512,1024]{1,0:T(8,128)(2,1)}, bf16[512,1024]{1,0:T(8,128)(2,1)}, u32[]{:S(2)}, u32[]{:S(2)}) collective-permute-start(bf16[512,1024]{1,0:T(8,128)(2,1)} %get-tuple-element.32), channel_id=1, source_target_pairs={{48,0},{96,48},{144,96},{192,144},{240,192},{288,240},{336,288},{3... | collective-permute-start | bytes 3145736 | tf_op jit(solution)/shard_map/ppermute | solution.py:22
  10.7 39.3 %collective-permute-start.1 = (bf16[512,128]{1,0:T(8,128)(2,1)S(1)}, bf16[512,128]{1,0:T(8,128)(2,1)S(1)}, u32[]{:S(2)}, u32[]{:S(2)}) collective-permute-start(bf16[512,128]{1,0:T(8,128)(2,1)S(1)} %convert_bitcast_fusion.1), channel_id=1, source_target_pairs={{48,0},{96,48},{144,96},{192,144},{240,192},{288,240},{336,288},{3... | collective-permute-start | bytes 393224 | tf_op jit(solution)/shard_map/ppermute | solution.py:22
  37.3 12.7 %collective-permute-start.2 = (f32[516,128]{1,0:T(8,128)S(1)}, f32[516,128]{1,0:T(8,128)S(1)}, u32[]{:S(2)}, u32[]{:S(2)}) collective-permute-start(f32[516,128]{1,0:T(8,128)S(1)} %pad_maximum_fusion), channel_id=1, source_target_pairs={{0,48},{48,96},{96,144},{144,192},{192,240},{240,288},{288,336},{3... | collective-permute-start | bytes 792584 | tf_op jit(solution)/shard_map/ppermute | solution.py:27
  99.9 8.1 %collective-permute-start.3 = (bf16[512,128]{1,0:T(8,128)(2,1)S(1)}, bf16[512,128]{1,0:T(8,128)(2,1)S(1)}, u32[]{:S(2)}, u32[]{:S(2)}) collective-permute-start(bf16[512,128]{1,0:T(8,128)(2,1)S(1)} %fusion.42), channel_id=1, source_target_pairs={{48,0},{96,48},{144,96},{192,144},{240,192},{288,240},{336,288},{3... | collective-permute-start | bytes 393224 | tf_op jit(solution)/shard_map/ppermute | solution.py:22
  103.8 13.5 %collective-permute-start.4 = (f32[512,128]{1,0:T(8,128)S(1)}, f32[512,128]{1,0:T(8,128)S(1)}, u32[]{:S(2)}, u32[]{:S(2)}) collective-permute-start(f32[512,128]{1,0:T(8,128)S(1)} %fusion.73), channel_id=1, source_target_pairs={{0,48},{48,96},{96,144},{144,192},{192,240},{240,288},{288,336},{3... | collective-permute-start | bytes 786440 | tf_op jit(solution)/shard_map/ppermute | solution.py:27
  118.0 41.4 %collective-permute-start.5 = (bf16[512,128]{1,0:T(8,128)(2,1)S(1)}, bf16[512,128]{1,0:T(8,128)(2,1)S(1)}, u32[]{:S(2)}, u32[]{:S(2)}) collective-permute-start(bf16[512,128]{1,0:T(8,128)(2,1)S(1)} %fusion.39), channel_id=1, source_target_pairs={{48,0},{96,48},{144,96},{192,144},{240,192},{288,240},{336,288},{3... | collective-permute-start | bytes 393224 | tf_op jit(solution)/shard_map/ppermute | solution.py:22
  119.9 39.5 %collective-permute-start.6 = (f32[512,128]{1,0:T(8,128)S(1)}, f32[512,128]{1,0:T(8,128)S(1)}, u32[]{:S(2)}, u32[]{:S(2)}) collective-permute-start(f32[512,128]{1,0:T(8,128)S(1)} %fusion.75), channel_id=1, source_target_pairs={{0,48},{48,96},{96,144},{144,192},{192,240},{240,288},{288,336},{3... | collective-permute-start | bytes 786440 | tf_op jit(solution)/shard_map/ppermute | solution.py:27

commit v5 on v4

--- a/solution.py
+++ b/solution.py
@@ -102,16 +102,14 @@
     info = jnp.zeros((1, classes), jnp.float32)
     info = info.at[0, : steps * slots].set(sources[0, 0].reshape(-1).astype(jnp.float32))
     info = info.at[0, steps * slots].set(counts[0, 0].astype(jnp.float32))
-    seed_mean = summarize(seed)
-    table_a = gather_groups(
-        jnp.concatenate(
-            [centre_unit.reshape(centre_rows, classes), seed_mean, summarize(spread), info]
-        )[None]
-    )
-    table = table_a[:, :centre_rows].reshape(groups, width)
-    seed_means = table_a[:, centre_rows : centre_rows + coarse_count]
-    spread_means = table_a[:, centre_rows + coarse_count : centre_rows + 2 * coarse_count]
-    info_all = table_a[:, centre_rows + 2 * coarse_count]
+    static = jnp.concatenate([centre_unit.reshape(centre_rows, classes), summarize(seed), info])
+    table_0 = static[None]
+    for axis in (GRP_PARTS[2], GRP_PARTS[0], GRP_PARTS[1]):
+        table_0 = lax.all_gather(table_0, axis, axis=0, tiled=False)
+    table_0 = jnp.swapaxes(table_0, 0, 1).reshape((groups,) + static.shape)
+    table = table_0[:, :centre_rows].reshape(groups, width)
+    seed_means = table_0[:, centre_rows : centre_rows + coarse_count]
+    info_all = table_0[:, centre_rows + coarse_count]
     source_all = jnp.round(info_all[:, : steps * slots]).astype(jnp.int32).reshape(groups, steps, slots)
     count_all = info_all[:, steps * slots]
     pair_weight = jnp.exp(pair_scale * jnp.dot(table, table.T, precision=highest))
@@ -131,8 +129,9 @@
         return keep_share * seed_means + (1.0 - keep_share) * (spread_mean + far)
 
     far_0 = far_all(0, seed_means)
+    labels = keep_share * seed + (1.0 - keep_share) * (spread + rows_of(own(far_0)))
+    spread_means = gather_groups(summarize(spread)[None])
     far_1 = far_all(1, next_summary(spread_means, far_0))
-    labels = keep_share * seed + (1.0 - keep_share) * (spread + rows_of(own(far_0)))
 
     local, _ = spread_of(labels, False)
     spread = local / degree[:, None]

time: 161 us -> 183 us (1.14)
  blocking collectives: 82 us -> 114 us
  waiting for transfers between devices: 34.1 us -> 24.9 us
    all_gather x0 -> x3, blocking collectives: none -> 47.9 us  [body(): table_0 = lax.all_gather(table_0, axis, axis=0, tiled=False)]
    ppermute x4, waiting for transfers between devices: 19.2 us -> 0.01 us  [from_next(): lax.ppermute(block, 'seq', [((i + 1) % count, i) for i in range(count)])]
    all_gather x6, blocking collectives: 82 us -> 66.1 us  [gather_groups(): value = lax.all_gather(value, axis, axis=0, tiled=True)]
    ppermute x3, waiting for transfers between devices: 14.9 us -> 24.9 us  [from_prev(): lax.ppermute(block, 'seq', [(i, (i + 1) % count) for i in range(count)])]
    ppermute x4, starting transfers between devices: 15.9 us -> 13.9 us  [from_next(): lax.ppermute(block, 'seq', [((i + 1) % count, i) for i in range(count)])]
    ppermute x3, starting transfers between devices: 7.76 us -> 9.74 us  [from_prev(): lax.ppermute(block, 'seq', [(i, (i + 1) % count) for i in range(count)])]
  transfers between devices with their start and end apart: 7 -> 7, of which waited for: 4 -> 3; matrix products, arithmetic and copies ran while one was open for 8% -> 7% of each run, Pallas kernels for 0% -> 0%
where the time goes in v5:
time: 183 us; the launch traced here: 182 us
  blocking collectives  114 us (62%)
  waiting for transfers between devices  24.9 us (14%)
  starting transfers between devices  23.6 us (13%)
  matrix products  8.92 us (5%)
  other arithmetic  6.36 us (3%)
  local copies, waits for them, and re-layouts  2.7 us (1%)
    all_gather x6, blocking collectives, gather_groups(): value = lax.all_gather(value, axis, axis=0, tiled=True)  66.1 us
    all_gather x3, blocking collectives, body(): table_0 = lax.all_gather(table_0, axis, axis=0, tiled=False)  47.9 us
    ppermute x3, waiting for transfers between devices, from_prev(): lax.ppermute(block, 'seq', [(i, (i + 1) % count) for i in range(count)])  24.9 us
    ppermute x4, starting transfers between devices, from_next(): lax.ppermute(block, 'seq', [((i + 1) % count, i) for i in range(count)])  13.9 us
    ppermute x3, starting transfers between devices, from_prev(): lax.ppermute(block, 'seq', [(i, (i + 1) % count) for i in range(count)])  9.74 us
  transfers between devices with their start and end apart: 7, of which 3 were waited for; matrix products, arithmetic and copies ran while one was open for 7% of the time, Pallas kernels for 0%

profile of v5, /device:TPU:64, one launch (start us, length us, event | category | flops | bytes accessed | tf_op | source)
XLA Modules:
  0.0 182.2 jit_solution(6371679872030359372)
XLA Ops:
  0.0 1.6 fusion.2
  1.6 0.3 convert_reduce_fusion
  2.0 7.7 %collective-permute-start = (bf16[512,1024]{1,0:T(8,128)(2,1)S(1)}, bf16[512,1024]{1,0:T(8,128)(2,1)}, u32[]{:S(2)}, u32[]{:S(2)}) collective-permute-start(bf16[512,1024]{1,0:T(8,128)(2,1)S(1)} %get-tuple-element.32), channel_id=1, source_target_pairs={{48,0},{96,48},{144,96},{192,144},{240,192},{288,240},{336,288},{3... | collective-permute-start | bytes 3145736 | tf_op jit(solution)/shard_map/ppermute | solution.py:22
  9.7 2.4 %collective-permute-start.1 = (bf16[512,128]{1,0:T(8,128)(2,1)S(1)}, bf16[512,128]{1,0:T(8,128)(2,1)S(1)}, u32[]{:S(2)}, u32[]{:S(2)}) collective-permute-start(bf16[512,128]{1,0:T(8,128)(2,1)S(1)} %convert_bitcast_fusion.1), channel_id=1, source_target_pairs={{48,0},{96,48},{144,96},{192,144},{240,192},{288,240},{336,288},{3... | collective-permute-start | bytes 393224 | tf_op jit(solution)/shard_map/ppermute | solution.py:22
  12.1 0.7 and_reduce_fusion
  12.8 0.7 fusion.62
  14.2 0.7 slice.68
  15.0 0.6 multiply_reduce_fusion
  16.2 1.9 %fusion.68 = f32[1,1]{1,0:T(1,128)} fusion(pred[1,1]{1,0:T(4,128)(4,1)} %bitcast.8, f32[1,1]{1,0:T(1,128)S(6)} %convert_element_type.90, s32[]{:T(128)} %bitcast.9, f32[1,12]{1,0:T(1,128)S(1)} %reshape.176), kind=kLoop, calls=%fused_computation.113 | loop fusion | flops 1 | bytes 61 | tf_op jit(solution)/shard_map/select.3
  18.1 1.4 scatter.9
  19.5 1.8 %all-gather.5 = f32[2,25,128]{2,1,0:T(8,128)S(1)} all-gather(f32[1,25,128]{2,1,0:T(8,128)S(1)} %maximum_bitcast_fusion), channel_id=2, replica_groups=mesh['seq'=16,'grp_z'=12,'grp_y'=2,'grp_c'=2] {'grp_c'}, dimensions={0}, use_global_device_ids=true | all-gather | bytes 38400 | tf_op jit(solution)/shard_map/all_gather | solution.py:108
  21.3 30.9 %all-gather.1 = f32[24,1,25,128]{3,1,2,0:T(1,128)S(1)} all-gather(f32[2,1,25,128]{3,1,2,0:T(1,128)S(1)} %copy.46), channel_id=3, replica_groups=mesh['seq'=16,'grp_z'=12,'grp_y'=2,'grp_c'=2] {'grp_z'}, dimensions={0}, use_global_device_ids=true | all-gather | bytes 332800 | tf_op jit(solution)/shard_map/all_gather | solution.py:108
  52.2 0.2 copy.47
  52.4 15.1 %all-gather.2 = f32[24,2,1,25,128]{4,1,3,2,0:T(2,128)S(1)} all-gather(f32[12,2,1,25,128]{4,1,3,2,0:T(2,128)S(1)} %copy.47), channel_id=4, replica_groups=mesh['seq'=16,'grp_z'=12,'grp_y'=2,'grp_c'=2] {'grp_y'}, dimensions={0}, use_global_device_ids=true | all-gather | bytes 921600 | tf_op jit(solution)/shard_map/all_gather | solution.py:108
  67.5 0.2 copy.48
  67.7 0.1 copy.53
  67.9 0.1 convert_reduce_fusion.6
  68.0 0.1 convert_reduce_fusion.5
  68.1 0.1 convert_reduce_fusion.4
  68.2 0.3 fusion.23
  68.5 0.5 fusion.35
  69.1 0.9 convert_reduce_fusion.3
  70.0 2.1 %convert_reduce_fusion.1 = (f32[512]{0:T(512)S(1)}, f32[512]{0:T(512)S(1)}, bf16[512,512]{0,1:T(8,128)(2,1)S(1)}) fusion(bf16[512,1024]{1,0:T(8,128)(2,1)S(1)} %get-tuple-element.32, bf16[512,1024]{1,0:T(8,128)(2,1)} %collective-permute-done), kind=kOutput, calls=%fused_computation.15 | convolution fusion | flops 538442752 | bytes 2625536 | tf_op jit(solution)/shard_map/dot_general | solution.py:44
  72.2 0.3 fusion.70
  72.5 1.9 %collective-permute-start.2 = (f32[516,128]{1,0:T(8,128)S(1)}, f32[516,128]{1,0:T(8,128)S(1)}, u32[]{:S(2)}, u32[]{:S(2)}) collective-permute-start(f32[516,128]{1,0:T(8,128)S(1)} %pad_maximum_fusion), channel_id=1, source_target_pairs={{0,48},{48,96},{96,144},{144,192},{192,240},{240,288},{288,336},{3... | collective-permute-start | bytes 792584 | tf_op jit(solution)/shard_map/ppermute | solution.py:27
  74.4 0.3 fusion.69
  74.8 10.2 %collective-permute-done.2 = f32[516,128]{1,0:T(8,128)S(1)} collective-permute-done((f32[516,128]{1,0:T(8,128)S(1)}, f32[516,128]{1,0:T(8,128)S(1)}, u32[]{:S(2)}, u32[]{:S(2)}) %collective-permute-start.2) | collective-permute-done | bytes 264224 | tf_op jit(solution)/shard_map/ppermute | solution.py:27
  84.9 0.4 bitcast_reduce_fusion.1
  85.4 0.3 fusion.72
  85.6 1.9 %collective-permute-start.3 = (bf16[512,128]{1,0:T(8,128)(2,1)S(1)}, bf16[512,128]{1,0:T(8,128)(2,1)S(1)}, u32[]{:S(2)}, u32[]{:S(2)}) collective-permute-start(bf16[512,128]{1,0:T(8,128)(2,1)S(1)} %fusion.42), channel_id=1, source_target_pairs={{48,0},{96,48},{144,96},{192,144},{240,192},{288,240},{336,288},{3... | collective-permute-start | bytes 393224 | tf_op jit(solution)/shard_map/ppermute | solution.py:22
  87.6 1.8 all-gather.3
  89.4 8.3 %all_gather.39 = f32[4,16,128]{2,1,0:T(8,128)S(1)} all-gather(f32[2,16,128]{2,1,0:T(8,128)S(1)} %bitcast.127), channel_id=1, replica_groups=mesh['seq'=16,'grp_z'=12,'grp_y'=2,'grp_c'=2] {'grp_y'}, dimensions={0}, use_global_device_ids=true | all-gather | bytes 49152 | tf_op jit(solution)/shard_map/all_gather | solution.py:32
  97.7 24.3 %all_gather.40 = f32[48,16,128]{2,1,0:T(8,128)S(1)} all-gather(f32[4,16,128]{2,1,0:T(8,128)S(1)} %all_gather.39), channel_id=1, replica_groups=mesh['seq'=16,'grp_z'=12,'grp_y'=2,'grp_c'=2] {'grp_z'}, dimensions={0}, use_global_device_ids=true | all-gather | bytes 425984 | tf_op jit(solution)/shard_map/all_gather | solution.py:32
  122.0 3.9 %collective-permute-start.4 = (f32[512,128]{1,0:T(8,128)S(1)}, f32[512,128]{1,0:T(8,128)S(1)}, u32[]{:S(2)}, u32[]{:S(2)}) collective-permute-start(f32[512,128]{1,0:T(8,128)S(1)} %fusion.72), channel_id=1, source_target_pairs={{0,48},{48,96},{96,144},{144,192},{192,240},{240,288},{288,336},{3... | collective-permute-start | bytes 786440 | tf_op jit(solution)/shard_map/ppermute | solution.py:27
  125.9 0.7 fusion.33
  126.6 0.3 fusion.71
  127.0 7.6 %collective-permute-done.4 = f32[512,128]{1,0:T(8,128)S(1)} collective-permute-done((f32[512,128]{1,0:T(8,128)S(1)}, f32[512,128]{1,0:T(8,128)S(1)}, u32[]{:S(2)}, u32[]{:S(2)}) %collective-permute-start.4) | collective-permute-done | bytes 262176 | tf_op jit(solution)/shard_map/ppermute | solution.py:27
  134.5 0.4 bitcast_reduce_fusion
  134.9 0.3 fusion.74
  135.2 1.9 %collective-permute-start.5 = (bf16[512,128]{1,0:T(8,128)(2,1)S(1)}, bf16[512,128]{1,0:T(8,128)(2,1)S(1)}, u32[]{:S(2)}, u32[]{:S(2)}) collective-permute-start(bf16[512,128]{1,0:T(8,128)(2,1)S(1)} %fusion.39), channel_id=1, source_target_pairs={{48,0},{96,48},{144,96},{192,144},{240,192},{288,240},{336,288},{3... | collective-permute-start | bytes 393224 | tf_op jit(solution)/shard_map/ppermute | solution.py:22
  137.2 1.8 all-gather.4
  139.0 8.3 %all_gather.42 = f32[4,16,128]{2,1,0:T(8,128)S(1)} all-gather(f32[2,16,128]{2,1,0:T(8,128)S(1)} %bitcast.128), channel_id=1, replica_groups=mesh['seq'=16,'grp_z'=12,'grp_y'=2,'grp_c'=2] {'grp_y'}, dimensions={0}, use_global_device_ids=true | all-gather | bytes 49152 | tf_op jit(solution)/shard_map/all_gather | solution.py:32
  147.3 21.6 %all_gather.43 = f32[48,16,128]{2,1,0:T(8,128)S(1)} all-gather(f32[4,16,128]{2,1,0:T(8,128)S(1)} %all_gather.42), channel_id=1, replica_groups=mesh['seq'=16,'grp_z'=12,'grp_y'=2,'grp_c'=2] {'grp_z'}, dimensions={0}, use_global_device_ids=true | all-gather | bytes 425984 | tf_op jit(solution)/shard_map/all_gather | solution.py:32
  168.9 3.9 %collective-permute-start.6 = (f32[512,128]{1,0:T(8,128)S(1)}, f32[512,128]{1,0:T(8,128)S(1)}, u32[]{:S(2)}, u32[]{:S(2)}) collective-permute-start(f32[512,128]{1,0:T(8,128)S(1)} %fusion.74), channel_id=1, source_target_pairs={{0,48},{48,96},{96,144},{144,192},{192,240},{240,288},{288,336},{3... | collective-permute-start | bytes 786440 | tf_op jit(solution)/shard_map/ppermute | solution.py:27
  172.8 0.7 fusion.29
  173.5 0.3 fusion.73
  173.9 7.2 %collective-permute-done.6 = f32[512,128]{1,0:T(8,128)S(1)} collective-permute-done((f32[512,128]{1,0:T(8,128)S(1)}, f32[512,128]{1,0:T(8,128)S(1)}, u32[]{:S(2)}, u32[]{:S(2)}) %collective-permute-start.6) | collective-permute-done | bytes 262176 | tf_op jit(solution)/shard_map/ppermute | solution.py:27
  181.1 1.1 fusion.19
  (35 shorter events, 0.5 us)
Async XLA Ops:
  0.0 1.6 copy-start.1
  1.6 8.1 %copy-start = (f32[1,1,512,128]{3,2,1,0:T(8,128)S(1)}, f32[1,1,512,128]{3,2,1,0:T(8,128)}, u32[]{:S(2)}) copy-start(f32[1,1,512,128]{3,2,1,0:T(8,128)} %param.9) | copy-start | bytes 786436
  1.6 11.2 %copy-start.2 = (s32[1,1,3,4]{3,1,2,0:T(1,128)S(1)}, s32[1,1,3,4]{3,1,2,0:T(1,128)}, u32[]{:S(2)}) copy-start(s32[1,1,3,4]{3,1,2,0:T(1,128)} %param.10) | copy-start | bytes 148
  2.0 68.1 %collective-permute-start = (bf16[512,1024]{1,0:T(8,128)(2,1)S(1)}, bf16[512,1024]{1,0:T(8,128)(2,1)}, u32[]{:S(2)}, u32[]{:S(2)}) collective-permute-start(bf16[512,1024]{1,0:T(8,128)(2,1)S(1)} %get-tuple-element.32), channel_id=1, source_target_pairs={{48,0},{96,48},{144,96},{192,144},{240,192},{288,240},{336,288},{3... | collective-permute-start | bytes 3145736 | tf_op jit(solution)/shard_map/ppermute | solution.py:22
  9.7 75.2 %collective-permute-start.1 = (bf16[512,128]{1,0:T(8,128)(2,1)S(1)}, bf16[512,128]{1,0:T(8,128)(2,1)S(1)}, u32[]{:S(2)}, u32[]{:S(2)}) collective-permute-start(bf16[512,128]{1,0:T(8,128)(2,1)S(1)} %convert_bitcast_fusion.1), channel_id=1, source_target_pairs={{48,0},{96,48},{144,96},{192,144},{240,192},{288,240},{336,288},{3... | collective-permute-start | bytes 393224 | tf_op jit(solution)/shard_map/ppermute | solution.py:22
  72.5 12.5 %collective-permute-start.2 = (f32[516,128]{1,0:T(8,128)S(1)}, f32[516,128]{1,0:T(8,128)S(1)}, u32[]{:S(2)}, u32[]{:S(2)}) collective-permute-start(f32[516,128]{1,0:T(8,128)S(1)} %pad_maximum_fusion), channel_id=1, source_target_pairs={{0,48},{48,96},{96,144},{144,192},{192,240},{240,288},{288,336},{3... | collective-permute-start | bytes 792584 | tf_op jit(solution)/shard_map/ppermute | solution.py:27
  85.6 41.3 %collective-permute-start.3 = (bf16[512,128]{1,0:T(8,128)(2,1)S(1)}, bf16[512,128]{1,0:T(8,128)(2,1)S(1)}, u32[]{:S(2)}, u32[]{:S(2)}) collective-permute-start(bf16[512,128]{1,0:T(8,128)(2,1)S(1)} %fusion.42), channel_id=1, source_target_pairs={{48,0},{96,48},{144,96},{192,144},{240,192},{288,240},{336,288},{3... | collective-permute-start | bytes 393224 | tf_op jit(solution)/shard_map/ppermute | solution.py:22
  122.0 12.5 %collective-permute-start.4 = (f32[512,128]{1,0:T(8,128)S(1)}, f32[512,128]{1,0:T(8,128)S(1)}, u32[]{:S(2)}, u32[]{:S(2)}) collective-permute-start(f32[512,128]{1,0:T(8,128)S(1)} %fusion.72), channel_id=1, source_target_pairs={{0,48},{48,96},{96,144},{144,192},{192,240},{240,288},{288,336},{3... | collective-permute-start | bytes 786440 | tf_op jit(solution)/shard_map/ppermute | solution.py:27
  135.2 38.6 %collective-permute-start.5 = (bf16[512,128]{1,0:T(8,128)(2,1)S(1)}, bf16[512,128]{1,0:T(8,128)(2,1)S(1)}, u32[]{:S(2)}, u32[]{:S(2)}) collective-permute-start(bf16[512,128]{1,0:T(8,128)(2,1)S(1)} %fusion.39), channel_id=1, source_target_pairs={{48,0},{96,48},{144,96},{192,144},{240,192},{288,240},{336,288},{3... | collective-permute-start | bytes 393224 | tf_op jit(solution)/shard_map/ppermute | solution.py:22
  168.9 12.2 %collective-permute-start.6 = (f32[512,128]{1,0:T(8,128)S(1)}, f32[512,128]{1,0:T(8,128)S(1)}, u32[]{:S(2)}, u32[]{:S(2)}) collective-permute-start(f32[512,128]{1,0:T(8,128)S(1)} %fusion.74), channel_id=1, source_target_pairs={{0,48},{48,96},{96,144},{144,192},{192,240},{240,288},{288,336},{3... | collective-permute-start | bytes 786440 | tf_op jit(solution)/shard_map/ppermute | solution.py:27

commit v6 on v4

--- a/solution.py
+++ b/solution.py
@@ -103,11 +103,13 @@
     info = info.at[0, : steps * slots].set(sources[0, 0].reshape(-1).astype(jnp.float32))
     info = info.at[0, steps * slots].set(counts[0, 0].astype(jnp.float32))
     seed_mean = summarize(seed)
-    table_a = gather_groups(
-        jnp.concatenate(
-            [centre_unit.reshape(centre_rows, classes), seed_mean, summarize(spread), info]
-        )[None]
+    payload = jnp.concatenate(
+        [centre_unit.reshape(centre_rows, classes), seed_mean, summarize(spread), info]
     )
+    table_a = payload
+    for axis in GRP_PARTS:
+        table_a = lax.all_gather(table_a, axis, axis=0, tiled=False)
+    table_a = jnp.transpose(table_a, (2, 1, 0, 3, 4)).reshape((groups,) + payload.shape)
     table = table_a[:, :centre_rows].reshape(groups, width)
     seed_means = table_a[:, centre_rows : centre_rows + coarse_count]
     spread_means = table_a[:, centre_rows + coarse_count : centre_rows + 2 * coarse_count]

time: 161 us -> 160 us (level)
    all_gather x6 -> x3, blocking collectives: 82 us -> 34.6 us  [gather_groups(): value = lax.all_gather(value, axis, axis=0, tiled=True)]
    all_gather x0 -> x3, blocking collectives: none -> 46.2 us  [body(): table_a = lax.all_gather(table_a, axis, axis=0, tiled=False)]
  transfers between devices with their start and end apart: 7 -> 7, of which waited for: 4 -> 4; matrix products, arithmetic and copies ran while one was open for 8% -> 7% of each run, Pallas kernels for 0% -> 0%
where the time goes in v6:
time: 160 us; the launch traced here: 159 us
  blocking collectives  80.8 us (50%)
  waiting for transfers between devices  34.4 us (22%)
  starting transfers between devices  23.9 us (15%)
  matrix products  8.81 us (6%)
  other arithmetic  6.34 us (4%)
  local copies, waits for them, and re-layouts  3.47 us (2%)
  between operations  1.73 us (1%)
    all_gather x3, blocking collectives, body(): table_a = lax.all_gather(table_a, axis, axis=0, tiled=False)  46.2 us
    all_gather x3, blocking collectives, gather_groups(): value = lax.all_gather(value, axis, axis=0, tiled=True)  34.6 us
    ppermute x4, waiting for transfers between devices, from_next(): lax.ppermute(block, 'seq', [((i + 1) % count, i) for i in range(count)])  18.6 us
    ppermute x4, starting transfers between devices, from_next(): lax.ppermute(block, 'seq', [((i + 1) % count, i) for i in range(count)])  16.1 us
    ppermute x3, waiting for transfers between devices, from_prev(): lax.ppermute(block, 'seq', [(i, (i + 1) % count) for i in range(count)])  15.8 us
    ppermute x3, starting transfers between devices, from_prev(): lax.ppermute(block, 'seq', [(i, (i + 1) % count) for i in range(count)])  7.76 us
    another operation x4, other arithmetic  3.35 us
  transfers between devices with their start and end apart: 7, of which 4 were waited for; matrix products, arithmetic and copies ran while one was open for 7% of the time, Pallas kernels for 0%

profile of v6, /device:TPU:64, one launch (start us, length us, event | category | flops | bytes accessed | tf_op | source)
XLA Modules:
  0.0 159.4 jit_solution(10550141454687881844)
XLA Ops:
  0.0 1.6 fusion.2
  1.6 0.3 convert_reduce_fusion
  2.0 7.7 %collective-permute-start = (bf16[512,1024]{1,0:T(8,128)(2,1)S(1)}, bf16[512,1024]{1,0:T(8,128)(2,1)}, u32[]{:S(2)}, u32[]{:S(2)}) collective-permute-start(bf16[512,1024]{1,0:T(8,128)(2,1)S(1)} %get-tuple-element.32), channel_id=1, source_target_pairs={{48,0},{96,48},{144,96},{192,144},{240,192},{288,240},{336,288},{3... | collective-permute-start | bytes 3145736 | tf_op jit(solution)/shard_map/ppermute | solution.py:22
  9.7 2.4 %collective-permute-start.1 = (bf16[512,128]{1,0:T(8,128)(2,1)S(1)}, bf16[512,128]{1,0:T(8,128)(2,1)S(1)}, u32[]{:S(2)}, u32[]{:S(2)}) collective-permute-start(bf16[512,128]{1,0:T(8,128)(2,1)S(1)} %convert_bitcast_fusion.1), channel_id=1, source_target_pairs={{48,0},{96,48},{144,96},{192,144},{240,192},{288,240},{336,288},{3... | collective-permute-start | bytes 393224 | tf_op jit(solution)/shard_map/ppermute | solution.py:22
  12.1 0.6 multiply_reduce_fusion
  13.4 0.7 and_reduce_fusion
  14.1 0.7 fusion.62
  14.8 0.9 convert_reduce_fusion.3
  15.7 17.5 %collective-permute-done = bf16[512,1024]{1,0:T(8,128)(2,1)} collective-permute-done((bf16[512,1024]{1,0:T(8,128)(2,1)S(1)}, bf16[512,1024]{1,0:T(8,128)(2,1)}, u32[]{:S(2)}, u32[]{:S(2)}) %collective-permute-start) | collective-permute-done | bytes 1048608 | tf_op jit(solution)/shard_map/ppermute | solution.py:22
  33.2 2.1 %convert_reduce_fusion.1 = (f32[512]{0:T(512)S(1)}, f32[512]{0:T(512)S(1)}, bf16[512,512]{0,1:T(8,128)(2,1)S(1)}) fusion(bf16[512,1024]{1,0:T(8,128)(2,1)S(1)} %get-tuple-element.32, bf16[512,1024]{1,0:T(8,128)(2,1)} %collective-permute-done), kind=kOutput, calls=%fused_computation.15 | convolution fusion | flops 538442752 | bytes 2625536 | tf_op jit(solution)/shard_map/dot_general | solution.py:44
  35.3 0.3 fusion.70
  35.7 1.9 %collective-permute-start.2 = (f32[516,128]{1,0:T(8,128)S(1)}, f32[516,128]{1,0:T(8,128)S(1)}, u32[]{:S(2)}, u32[]{:S(2)}) collective-permute-start(f32[516,128]{1,0:T(8,128)S(1)} %pad_maximum_fusion), channel_id=1, source_target_pairs={{0,48},{48,96},{96,144},{144,192},{192,240},{240,288},{288,336},{3... | collective-permute-start | bytes 792584 | tf_op jit(solution)/shard_map/ppermute | solution.py:27
  37.6 0.1 reshape.168
  37.7 0.7 slice.71
  39.1 1.9 %fusion.68 = f32[1,1]{1,0:T(1,128)} fusion(pred[1,1]{1,0:T(4,128)(4,1)} %bitcast.9, f32[1,1]{1,0:T(1,128)S(6)} %convert_element_type.90, s32[]{:T(128)} %bitcast.10, f32[1,12]{1,0:T(1,128)S(1)} %reshape.168), kind=kLoop, calls=%fused_computation.113 | loop fusion | flops 1 | bytes 61 | tf_op jit(solution)/shard_map/select.3
  41.0 1.4 scatter.9
  42.4 0.3 fusion.69
  42.7 5.8 %collective-permute-done.2 = f32[516,128]{1,0:T(8,128)S(1)} collective-permute-done((f32[516,128]{1,0:T(8,128)S(1)}, f32[516,128]{1,0:T(8,128)S(1)}, u32[]{:S(2)}, u32[]{:S(2)}) %collective-permute-start.2) | collective-permute-done | bytes 264224 | tf_op jit(solution)/shard_map/ppermute | solution.py:27
  48.5 0.3 bitcast_reduce_fusion.1
  48.9 30.9 %all-gather.4 = f32[12,41,128]{2,1,0:T(8,128)S(1)} all-gather(f32[1,41,128]{2,1,0:T(8,128)S(1)} %maximum_bitcast_fusion), channel_id=2, replica_groups=mesh['seq'=16,'grp_z'=12,'grp_y'=2,'grp_c'=2] {'grp_z'}, dimensions={0}, use_global_device_ids=true | all-gather | bytes 272896 | tf_op jit(solution)/shard_map/all_gather | solution.py:111
  79.7 12.7 %all-gather.1 = f32[24,41,128]{2,1,0:T(8,128)S(1)} all-gather(f32[12,41,128]{2,1,0:T(8,128)S(1)} %all-gather.4), channel_id=3, replica_groups=mesh['seq'=16,'grp_z'=12,'grp_y'=2,'grp_c'=2] {'grp_y'}, dimensions={0}, use_global_device_ids=true | all-gather | bytes 755712 | tf_op jit(solution)/shard_map/all_gather | solution.py:111
  92.4 2.6 %all-gather.2 = f32[4,12,41,128]{3,2,1,0:T(8,128)S(1)} all-gather(f32[2,12,41,128]{3,2,1,0:T(8,128)S(1)} %bitcast.120), channel_id=4, replica_groups=mesh['seq'=16,'grp_z'=12,'grp_y'=2,'grp_c'=2] {'grp_c'}, dimensions={0}, use_global_device_ids=true | all-gather | bytes 1511424 | tf_op jit(solution)/shard_map/all_gather | solution.py:111
  95.1 0.7 copy.39
  95.7 0.5 copy.40
  96.2 0.1 copy.44
  96.4 0.3 fusion.23
  96.7 0.1 convert_reduce_fusion.6
  96.8 0.5 fusion.35
  97.4 0.1 fusion.42
  97.4 0.3 fusion.71
  97.8 0.3 fusion.72
  98.1 4.1 %collective-permute-start.3 = (bf16[512,128]{1,0:T(8,128)(2,1)S(1)}, bf16[512,128]{1,0:T(8,128)(2,1)S(1)}, u32[]{:S(2)}, u32[]{:S(2)}) collective-permute-start(bf16[512,128]{1,0:T(8,128)(2,1)S(1)} %fusion.42), channel_id=1, source_target_pairs={{48,0},{96,48},{144,96},{192,144},{240,192},{288,240},{336,288},{3... | collective-permute-start | bytes 393224 | tf_op jit(solution)/shard_map/ppermute | solution.py:22
  102.2 1.9 %collective-permute-start.4 = (f32[512,128]{1,0:T(8,128)S(1)}, f32[512,128]{1,0:T(8,128)S(1)}, u32[]{:S(2)}, u32[]{:S(2)}) collective-permute-start(f32[512,128]{1,0:T(8,128)S(1)} %fusion.72), channel_id=1, source_target_pairs={{0,48},{48,96},{96,144},{144,192},{192,240},{240,288},{288,336},{3... | collective-permute-start | bytes 786440 | tf_op jit(solution)/shard_map/ppermute | solution.py:27
  104.1 0.1 convert_reduce_fusion.5
  104.2 0.6 fusion.29
  104.8 0.1 convert_reduce_fusion.4
  104.9 1.2 collective-permute-done.3
  106.1 10.0 %collective-permute-done.4 = f32[512,128]{1,0:T(8,128)S(1)} collective-permute-done((f32[512,128]{1,0:T(8,128)S(1)}, f32[512,128]{1,0:T(8,128)S(1)}, u32[]{:S(2)}, u32[]{:S(2)}) %collective-permute-start.4) | collective-permute-done | bytes 262176 | tf_op jit(solution)/shard_map/ppermute | solution.py:27
  116.1 0.4 bitcast_reduce_fusion
  116.5 0.3 fusion.74
  116.8 1.9 %collective-permute-start.5 = (bf16[512,128]{1,0:T(8,128)(2,1)S(1)}, bf16[512,128]{1,0:T(8,128)(2,1)S(1)}, u32[]{:S(2)}, u32[]{:S(2)}) collective-permute-start(bf16[512,128]{1,0:T(8,128)(2,1)S(1)} %fusion.39), channel_id=1, source_target_pairs={{48,0},{96,48},{144,96},{192,144},{240,192},{288,240},{336,288},{3... | collective-permute-start | bytes 393224 | tf_op jit(solution)/shard_map/ppermute | solution.py:22
  118.7 3.9 %collective-permute-start.6 = (f32[512,128]{1,0:T(8,128)S(1)}, f32[512,128]{1,0:T(8,128)S(1)}, u32[]{:S(2)}, u32[]{:S(2)}) collective-permute-start(f32[512,128]{1,0:T(8,128)S(1)} %fusion.74), channel_id=1, source_target_pairs={{0,48},{48,96},{96,144},{144,192},{192,240},{240,288},{288,336},{3... | collective-permute-start | bytes 786440 | tf_op jit(solution)/shard_map/ppermute | solution.py:27
  122.7 1.8 %all-gather.3 = f32[32,128]{1,0:T(8,128)S(1)} all-gather(f32[16,128]{1,0:T(8,128)S(1)} %broadcast_multiply_fusion), channel_id=5, replica_groups=mesh['seq'=16,'grp_z'=12,'grp_y'=2,'grp_c'=2] {'grp_c'}, dimensions={0}, use_global_device_ids=true | all-gather | bytes 24576 | tf_op jit(solution)/shard_map/all_gather | solution.py:32
  124.5 8.4 %all_gather.34 = f32[4,16,128]{2,1,0:T(8,128)S(1)} all-gather(f32[2,16,128]{2,1,0:T(8,128)S(1)} %bitcast.124), channel_id=1, replica_groups=mesh['seq'=16,'grp_z'=12,'grp_y'=2,'grp_c'=2] {'grp_y'}, dimensions={0}, use_global_device_ids=true | all-gather | bytes 49152 | tf_op jit(solution)/shard_map/all_gather | solution.py:32
  132.8 24.4 %all_gather.35 = f32[48,16,128]{2,1,0:T(8,128)S(1)} all-gather(f32[4,16,128]{2,1,0:T(8,128)S(1)} %all_gather.34), channel_id=1, replica_groups=mesh['seq'=16,'grp_z'=12,'grp_y'=2,'grp_c'=2] {'grp_z'}, dimensions={0}, use_global_device_ids=true | all-gather | bytes 425984 | tf_op jit(solution)/shard_map/all_gather | solution.py:32
  157.2 0.7 fusion.33
  157.9 0.3 fusion.73
  158.3 1.1 fusion.19
  (30 shorter events, 0.3 us)
Async XLA Ops:
  0.0 1.6 %copy-start.1 = (bf16[1,1,512,1024]{3,2,1,0:T(8,128)(2,1)S(1)}, bf16[1,1,512,1024]{3,2,1,0:T(8,128)(2,1)}, u32[]{:S(2)}) copy-start(bf16[1,1,512,1024]{3,2,1,0:T(8,128)(2,1)} %param.8) | copy-start | bytes 3145732
  1.6 8.1 %copy-start = (f32[1,1,512,128]{3,2,1,0:T(8,128)S(1)}, f32[1,1,512,128]{3,2,1,0:T(8,128)}, u32[]{:S(2)}) copy-start(f32[1,1,512,128]{3,2,1,0:T(8,128)} %param.9) | copy-start | bytes 786436
  1.6 12.5 %copy-start.2 = (s32[1,1,3,4]{3,1,2,0:T(1,128)S(1)}, s32[1,1,3,4]{3,1,2,0:T(1,128)}, u32[]{:S(2)}) copy-start(s32[1,1,3,4]{3,1,2,0:T(1,128)} %param.10) | copy-start | bytes 148
  2.0 31.3 %collective-permute-start = (bf16[512,1024]{1,0:T(8,128)(2,1)S(1)}, bf16[512,1024]{1,0:T(8,128)(2,1)}, u32[]{:S(2)}, u32[]{:S(2)}) collective-permute-start(bf16[512,1024]{1,0:T(8,128)(2,1)S(1)} %get-tuple-element.32), channel_id=1, source_target_pairs={{48,0},{96,48},{144,96},{192,144},{240,192},{288,240},{336,288},{3... | collective-permute-start | bytes 3145736 | tf_op jit(solution)/shard_map/ppermute | solution.py:22
  9.7 38.8 %collective-permute-start.1 = (bf16[512,128]{1,0:T(8,128)(2,1)S(1)}, bf16[512,128]{1,0:T(8,128)(2,1)S(1)}, u32[]{:S(2)}, u32[]{:S(2)}) collective-permute-start(bf16[512,128]{1,0:T(8,128)(2,1)S(1)} %convert_bitcast_fusion.1), channel_id=1, source_target_pairs={{48,0},{96,48},{144,96},{192,144},{240,192},{288,240},{336,288},{3... | collective-permute-start | bytes 393224 | tf_op jit(solution)/shard_map/ppermute | solution.py:22
  35.7 12.8 %collective-permute-start.2 = (f32[516,128]{1,0:T(8,128)S(1)}, f32[516,128]{1,0:T(8,128)S(1)}, u32[]{:S(2)}, u32[]{:S(2)}) collective-permute-start(f32[516,128]{1,0:T(8,128)S(1)} %pad_maximum_fusion), channel_id=1, source_target_pairs={{0,48},{48,96},{96,144},{144,192},{192,240},{240,288},{288,336},{3... | collective-permute-start | bytes 792584 | tf_op jit(solution)/shard_map/ppermute | solution.py:27
  98.1 8.0 %collective-permute-start.3 = (bf16[512,128]{1,0:T(8,128)(2,1)S(1)}, bf16[512,128]{1,0:T(8,128)(2,1)S(1)}, u32[]{:S(2)}, u32[]{:S(2)}) collective-permute-start(bf16[512,128]{1,0:T(8,128)(2,1)S(1)} %fusion.42), channel_id=1, source_target_pairs={{48,0},{96,48},{144,96},{192,144},{240,192},{288,240},{336,288},{3... | collective-permute-start | bytes 393224 | tf_op jit(solution)/shard_map/ppermute | solution.py:22
  102.2 13.9 %collective-permute-start.4 = (f32[512,128]{1,0:T(8,128)S(1)}, f32[512,128]{1,0:T(8,128)S(1)}, u32[]{:S(2)}, u32[]{:S(2)}) collective-permute-start(f32[512,128]{1,0:T(8,128)S(1)} %fusion.72), channel_id=1, source_target_pairs={{0,48},{48,96},{96,144},{144,192},{192,240},{240,288},{288,336},{3... | collective-permute-start | bytes 786440 | tf_op jit(solution)/shard_map/ppermute | solution.py:27
  116.8 41.5 %collective-permute-start.5 = (bf16[512,128]{1,0:T(8,128)(2,1)S(1)}, bf16[512,128]{1,0:T(8,128)(2,1)S(1)}, u32[]{:S(2)}, u32[]{:S(2)}) collective-permute-start(bf16[512,128]{1,0:T(8,128)(2,1)S(1)} %fusion.39), channel_id=1, source_target_pairs={{48,0},{96,48},{144,96},{192,144},{240,192},{288,240},{336,288},{3... | collective-permute-start | bytes 393224 | tf_op jit(solution)/shard_map/ppermute | solution.py:22
  118.7 39.6 %collective-permute-start.6 = (f32[512,128]{1,0:T(8,128)S(1)}, f32[512,128]{1,0:T(8,128)S(1)}, u32[]{:S(2)}, u32[]{:S(2)}) collective-permute-start(f32[512,128]{1,0:T(8,128)S(1)} %fusion.74), channel_id=1, source_target_pairs={{0,48},{48,96},{96,144},{144,192},{192,240},{240,288},{288,336},{3... | collective-permute-start | bytes 786440 | tf_op jit(solution)/shard_map/ppermute | solution.py:27

commit v7 on v6

--- a/solution.py
+++ b/solution.py
@@ -28,9 +28,8 @@
 
 
 def gather_groups(value):
-    for axis in reversed(GRP_PARTS):
-        value = lax.all_gather(value, axis, axis=0, tiled=True)
-    return value
+    value = lax.all_gather(value, GRP_PARTS[1:], axis=0, tiled=True)
+    return lax.all_gather(value, GRP_PARTS[0], axis=0, tiled=True)
 
 
 def normalized(values):
@@ -106,10 +105,9 @@
     payload = jnp.concatenate(
         [centre_unit.reshape(centre_rows, classes), seed_mean, summarize(spread), info]
     )
-    table_a = payload
-    for axis in GRP_PARTS:
-        table_a = lax.all_gather(table_a, axis, axis=0, tiled=False)
-    table_a = jnp.transpose(table_a, (2, 1, 0, 3, 4)).reshape((groups,) + payload.shape)
+    table_a = lax.all_gather(payload, GRP_PARTS[0], axis=0, tiled=False)
+    table_a = lax.all_gather(table_a, GRP_PARTS[1:], axis=0, tiled=False)
+    table_a = jnp.swapaxes(table_a, 0, 1).reshape((groups,) + payload.shape)
     table = table_a[:, :centre_rows].reshape(groups, width)
     seed_means = table_a[:, centre_rows : centre_rows + coarse_count]
     spread_means = table_a[:, centre_rows + coarse_count : centre_rows + 2 * coarse_count]

time: 160 us -> 160 us (level)
  the two profiles are of different devices: /device:TPU:64 before, /device:TPU:8 now
where the time goes in v7:
time: 160 us
  blocking collectives  80.2 us (50%)
  starting transfers between devices  39.3 us (25%)
  waiting for transfers between devices  20.5 us (13%)
  matrix products  8.8 us (6%)
  other arithmetic  6.34 us (4%)
  local copies, waits for them, and re-layouts  2.95 us (2%)
  between operations  1.72 us (1%)
    all_gather x1, blocking collectives, body(): table_a = lax.all_gather(payload, GRP_PARTS[0], axis=0, tiled=False)  33.6 us
    ppermute x4, starting transfers between devices, from_next(): lax.ppermute(block, 'seq', [((i + 1) % count, i) for i in range(count)])  31.9 us
    all_gather x1, blocking collectives, gather_groups(): return lax.all_gather(value, GRP_PARTS[0], axis=0, tiled=True)  21.7 us
    all_gather x1, blocking collectives, body(): table_a = lax.all_gather(table_a, GRP_PARTS[1:], axis=0, tiled=False)  12.9 us
    all_gather x1, blocking collectives, gather_groups(): value = lax.all_gather(value, GRP_PARTS[1:], axis=0, tiled=True)  11.9 us
    ppermute x4, waiting for transfers between devices, from_next(): lax.ppermute(block, 'seq', [((i + 1) % count, i) for i in range(count)])  11.6 us
    ppermute x3, waiting for transfers between devices, from_prev(): lax.ppermute(block, 'seq', [(i, (i + 1) % count) for i in range(count)])  8.9 us
    ppermute x3, starting transfers between devices, from_prev(): lax.ppermute(block, 'seq', [(i, (i + 1) % count) for i in range(count)])  7.33 us
  transfers between devices with their start and end apart: 7, of which 4 were waited for; matrix products, arithmetic and copies ran while one was open for 7% of the time, Pallas kernels for 0%

profile of v7, /device:TPU:8, one launch (start us, length us, event | category | flops | bytes accessed | tf_op | source)
XLA Modules:
  0.0 159.8 jit_solution(16882702083093069342)
XLA Ops:
  0.0 1.6 fusion.2
  1.6 0.0 copy-start.2
  1.6 0.3 convert_reduce_fusion
  2.0 11.4 %collective-permute-start = (bf16[512,1024]{1,0:T(8,128)(2,1)S(1)}, bf16[512,1024]{1,0:T(8,128)(2,1)}, u32[]{:S(2)}, u32[]{:S(2)}) collective-permute-start(bf16[512,1024]{1,0:T(8,128)(2,1)S(1)} %get-tuple-element.32), channel_id=1, source_target_pairs={{48,0},{96,48},{144,96},{192,144},{240,192},{288,240},{336,288},{3... | collective-permute-start | bytes 3145736 | tf_op jit(solution)/shard_map/ppermute | solution.py:22
  13.4 1.9 %collective-permute-start.1 = (bf16[512,128]{1,0:T(8,128)(2,1)S(1)}, bf16[512,128]{1,0:T(8,128)(2,1)S(1)}, u32[]{:S(2)}, u32[]{:S(2)}) collective-permute-start(bf16[512,128]{1,0:T(8,128)(2,1)S(1)} %convert_bitcast_fusion.1), channel_id=1, source_target_pairs={{48,0},{96,48},{144,96},{192,144},{240,192},{288,240},{336,288},{3... | collective-permute-start | bytes 393224 | tf_op jit(solution)/shard_map/ppermute | solution.py:22
  15.3 0.6 multiply_reduce_fusion
  16.6 0.7 and_reduce_fusion
  17.3 0.7 fusion.62
  18.0 0.9 convert_reduce_fusion.3
  19.0 11.0 %collective-permute-done = bf16[512,1024]{1,0:T(8,128)(2,1)} collective-permute-done((bf16[512,1024]{1,0:T(8,128)(2,1)S(1)}, bf16[512,1024]{1,0:T(8,128)(2,1)}, u32[]{:S(2)}, u32[]{:S(2)}) %collective-permute-start) | collective-permute-done | bytes 1048608 | tf_op jit(solution)/shard_map/ppermute | solution.py:22
  30.0 2.1 %convert_reduce_fusion.1 = (f32[512]{0:T(512)S(1)}, f32[512]{0:T(512)S(1)}, bf16[512,512]{0,1:T(8,128)(2,1)S(1)}) fusion(bf16[512,1024]{1,0:T(8,128)(2,1)S(1)} %get-tuple-element.32, bf16[512,1024]{1,0:T(8,128)(2,1)} %collective-permute-done), kind=kOutput, calls=%fused_computation.15 | convolution fusion | flops 538442752 | bytes 2625536 | tf_op jit(solution)/shard_map/dot_general | solution.py:43
  32.1 0.3 fusion.70
  32.5 3.5 %collective-permute-start.2 = (f32[516,128]{1,0:T(8,128)S(1)}, f32[516,128]{1,0:T(8,128)S(1)}, u32[]{:S(2)}, u32[]{:S(2)}) collective-permute-start(f32[516,128]{1,0:T(8,128)S(1)} %pad_maximum_fusion), channel_id=1, source_target_pairs={{0,48},{48,96},{96,144},{144,192},{192,240},{240,288},{288,336},{3... | collective-permute-start | bytes 792584 | tf_op jit(solution)/shard_map/ppermute | solution.py:27
  36.0 0.1 reshape.168
  36.1 0.7 slice.71
  37.4 1.9 %fusion.68 = f32[1,1]{1,0:T(1,128)} fusion(pred[1,1]{1,0:T(4,128)(4,1)} %bitcast.9, f32[1,1]{1,0:T(1,128)S(6)} %convert_element_type.90, s32[]{:T(128)} %bitcast.10, f32[1,12]{1,0:T(1,128)S(1)} %reshape.168), kind=kLoop, calls=%fused_computation.113 | loop fusion | flops 1 | bytes 61 | tf_op jit(solution)/shard_map/select.3
  39.4 1.4 scatter.9
  40.7 0.3 fusion.69
  41.1 1.6 %collective-permute-done.2 = f32[516,128]{1,0:T(8,128)S(1)} collective-permute-done((f32[516,128]{1,0:T(8,128)S(1)}, f32[516,128]{1,0:T(8,128)S(1)}, u32[]{:S(2)}, u32[]{:S(2)}) %collective-permute-start.2) | collective-permute-done | bytes 264224 | tf_op jit(solution)/shard_map/ppermute | solution.py:27
  42.7 0.0 collective-permute-done.1
  42.7 0.3 bitcast_reduce_fusion.1
  43.1 33.6 %all-gather.3 = f32[12,41,128]{2,1,0:T(8,128)S(1)} all-gather(f32[1,41,128]{2,1,0:T(8,128)S(1)} %maximum_bitcast_fusion), channel_id=2, replica_groups=mesh['seq'=16,'grp_z'=12,'grp_y'=2,'grp_c'=2] {'grp_z'}, dimensions={0}, use_global_device_ids=true | all-gather | bytes 272896 | tf_op jit(solution)/shard_map/all_gather | solution.py:108
  76.7 12.9 %all-gather.1 = f32[48,41,128]{2,1,0:T(8,128)S(1)} all-gather(f32[12,41,128]{2,1,0:T(8,128)S(1)} %all-gather.3), channel_id=3, replica_groups=mesh['seq'=16,'grp_z'=12,'grp_y'=2,'grp_c'=2] {'grp_y','grp_c'}, dimensions={0}, use_global_device_ids=true | all-gather | bytes 1259520 | tf_op jit(solution)/shard_map/all_gather | solution.py:109
  89.6 0.7 copy.35
  90.3 0.1 copy.39
  90.4 0.3 fusion.23
  90.8 0.1 convert_reduce_fusion.6
  90.9 0.5 fusion.35
  91.4 0.1 fusion.42
  91.5 0.3 fusion.71
  91.8 0.3 fusion.72
  92.1 12.0 %collective-permute-start.3 = (bf16[512,128]{1,0:T(8,128)(2,1)S(1)}, bf16[512,128]{1,0:T(8,128)(2,1)S(1)}, u32[]{:S(2)}, u32[]{:S(2)}) collective-permute-start(bf16[512,128]{1,0:T(8,128)(2,1)S(1)} %fusion.42), channel_id=1, source_target_pairs={{48,0},{96,48},{144,96},{192,144},{240,192},{288,240},{336,288},{3... | collective-permute-start | bytes 393224 | tf_op jit(solution)/shard_map/ppermute | solution.py:22
  104.1 1.9 %collective-permute-start.4 = (f32[512,128]{1,0:T(8,128)S(1)}, f32[512,128]{1,0:T(8,128)S(1)}, u32[]{:S(2)}, u32[]{:S(2)}) collective-permute-start(f32[512,128]{1,0:T(8,128)S(1)} %fusion.72), channel_id=1, source_target_pairs={{0,48},{48,96},{96,144},{144,192},{192,240},{240,288},{288,336},{3... | collective-permute-start | bytes 786440 | tf_op jit(solution)/shard_map/ppermute | solution.py:27
  106.1 0.1 convert_reduce_fusion.5
  106.2 0.6 fusion.29
  106.7 0.1 convert_reduce_fusion.4
  106.8 0.5 collective-permute-done.3
  107.4 7.3 %collective-permute-done.4 = f32[512,128]{1,0:T(8,128)S(1)} collective-permute-done((f32[512,128]{1,0:T(8,128)S(1)}, f32[512,128]{1,0:T(8,128)S(1)}, u32[]{:S(2)}, u32[]{:S(2)}) %collective-permute-start.4) | collective-permute-done | bytes 262176 | tf_op jit(solution)/shard_map/ppermute | solution.py:27
  114.7 0.4 bitcast_reduce_fusion
  115.0 0.1 fusion.39
  115.1 0.3 fusion.74
  115.4 6.6 %collective-permute-start.5 = (bf16[512,128]{1,0:T(8,128)(2,1)S(1)}, bf16[512,128]{1,0:T(8,128)(2,1)S(1)}, u32[]{:S(2)}, u32[]{:S(2)}) collective-permute-start(bf16[512,128]{1,0:T(8,128)(2,1)S(1)} %fusion.39), channel_id=1, source_target_pairs={{48,0},{96,48},{144,96},{192,144},{240,192},{288,240},{336,288},{3... | collective-permute-start | bytes 393224 | tf_op jit(solution)/shard_map/ppermute | solution.py:22
  122.0 1.9 %collective-permute-start.6 = (f32[512,128]{1,0:T(8,128)S(1)}, f32[512,128]{1,0:T(8,128)S(1)}, u32[]{:S(2)}, u32[]{:S(2)}) collective-permute-start(f32[512,128]{1,0:T(8,128)S(1)} %fusion.74), channel_id=1, source_target_pairs={{0,48},{48,96},{96,144},{144,192},{192,240},{240,288},{288,336},{3... | collective-permute-start | bytes 786440 | tf_op jit(solution)/shard_map/ppermute | solution.py:27
  124.0 11.9 %all-gather.2 = f32[64,128]{1,0:T(8,128)S(1)} all-gather(f32[16,128]{1,0:T(8,128)S(1)} %broadcast_multiply_fusion), channel_id=4, replica_groups=mesh['seq'=16,'grp_z'=12,'grp_y'=2,'grp_c'=2] {'grp_y','grp_c'}, dimensions={0}, use_global_device_ids=true | all-gather | bytes 40960 | tf_op jit(solution)/shard_map/all_gather | solution.py:31
  135.9 21.7 %all_gather.23 = f32[48,16,128]{2,1,0:T(8,128)S(1)} all-gather(f32[4,16,128]{2,1,0:T(8,128)S(1)} %bitcast.120), channel_id=1, replica_groups=mesh['seq'=16,'grp_z'=12,'grp_y'=2,'grp_c'=2] {'grp_z'}, dimensions={0}, use_global_device_ids=true | all-gather | bytes 425984 | tf_op jit(solution)/shard_map/all_gather | solution.py:32
  157.6 0.7 fusion.33
  158.3 0.3 fusion.73
  158.7 1.1 fusion.19
  (27 shorter events, 0.2 us)
Async XLA Ops:
  0.0 1.6 %copy-start.1 = (bf16[1,1,512,1024]{3,2,1,0:T(8,128)(2,1)S(1)}, bf16[1,1,512,1024]{3,2,1,0:T(8,128)(2,1)}, u32[]{:S(2)}) copy-start(bf16[1,1,512,1024]{3,2,1,0:T(8,128)(2,1)} %param.8) | copy-start | bytes 3145732
  1.6 11.7 %copy-start = (f32[1,1,512,128]{3,2,1,0:T(8,128)S(1)}, f32[1,1,512,128]{3,2,1,0:T(8,128)}, u32[]{:S(2)}) copy-start(f32[1,1,512,128]{3,2,1,0:T(8,128)} %param.9) | copy-start | bytes 786436
  1.6 15.7 %copy-start.2 = (s32[1,1,3,4]{3,1,2,0:T(1,128)S(1)}, s32[1,1,3,4]{3,1,2,0:T(1,128)}, u32[]{:S(2)}) copy-start(s32[1,1,3,4]{3,1,2,0:T(1,128)} %param.10) | copy-start | bytes 148
  2.0 28.0 %collective-permute-start = (bf16[512,1024]{1,0:T(8,128)(2,1)S(1)}, bf16[512,1024]{1,0:T(8,128)(2,1)}, u32[]{:S(2)}, u32[]{:S(2)}) collective-permute-start(bf16[512,1024]{1,0:T(8,128)(2,1)S(1)} %get-tuple-element.32), channel_id=1, source_target_pairs={{48,0},{96,48},{144,96},{192,144},{240,192},{288,240},{336,288},{3... | collective-permute-start | bytes 3145736 | tf_op jit(solution)/shard_map/ppermute | solution.py:22
  13.4 29.3 %collective-permute-start.1 = (bf16[512,128]{1,0:T(8,128)(2,1)S(1)}, bf16[512,128]{1,0:T(8,128)(2,1)S(1)}, u32[]{:S(2)}, u32[]{:S(2)}) collective-permute-start(bf16[512,128]{1,0:T(8,128)(2,1)S(1)} %convert_bitcast_fusion.1), channel_id=1, source_target_pairs={{48,0},{96,48},{144,96},{192,144},{240,192},{288,240},{336,288},{3... | collective-permute-start | bytes 393224 | tf_op jit(solution)/shard_map/ppermute | solution.py:22
  32.5 10.2 %collective-permute-start.2 = (f32[516,128]{1,0:T(8,128)S(1)}, f32[516,128]{1,0:T(8,128)S(1)}, u32[]{:S(2)}, u32[]{:S(2)}) collective-permute-start(f32[516,128]{1,0:T(8,128)S(1)} %pad_maximum_fusion), channel_id=1, source_target_pairs={{0,48},{48,96},{96,144},{144,192},{192,240},{240,288},{288,336},{3... | collective-permute-start | bytes 792584 | tf_op jit(solution)/shard_map/ppermute | solution.py:27
  92.1 15.3 %collective-permute-start.3 = (bf16[512,128]{1,0:T(8,128)(2,1)S(1)}, bf16[512,128]{1,0:T(8,128)(2,1)S(1)}, u32[]{:S(2)}, u32[]{:S(2)}) collective-permute-start(bf16[512,128]{1,0:T(8,128)(2,1)S(1)} %fusion.42), channel_id=1, source_target_pairs={{48,0},{96,48},{144,96},{192,144},{240,192},{288,240},{336,288},{3... | collective-permute-start | bytes 393224 | tf_op jit(solution)/shard_map/ppermute | solution.py:22
  104.1 10.5 %collective-permute-start.4 = (f32[512,128]{1,0:T(8,128)S(1)}, f32[512,128]{1,0:T(8,128)S(1)}, u32[]{:S(2)}, u32[]{:S(2)}) collective-permute-start(f32[512,128]{1,0:T(8,128)S(1)} %fusion.72), channel_id=1, source_target_pairs={{0,48},{48,96},{96,144},{144,192},{192,240},{240,288},{288,336},{3... | collective-permute-start | bytes 786440 | tf_op jit(solution)/shard_map/ppermute | solution.py:27
  115.4 43.3 %collective-permute-start.5 = (bf16[512,128]{1,0:T(8,128)(2,1)S(1)}, bf16[512,128]{1,0:T(8,128)(2,1)S(1)}, u32[]{:S(2)}, u32[]{:S(2)}) collective-permute-start(bf16[512,128]{1,0:T(8,128)(2,1)S(1)} %fusion.39), channel_id=1, source_target_pairs={{48,0},{96,48},{144,96},{192,144},{240,192},{288,240},{336,288},{3... | collective-permute-start | bytes 393224 | tf_op jit(solution)/shard_map/ppermute | solution.py:22
  122.0 36.6 %collective-permute-start.6 = (f32[512,128]{1,0:T(8,128)S(1)}, f32[512,128]{1,0:T(8,128)S(1)}, u32[]{:S(2)}, u32[]{:S(2)}) collective-permute-start(f32[512,128]{1,0:T(8,128)S(1)} %fusion.74), channel_id=1, source_target_pairs={{0,48},{48,96},{96,144},{144,192},{192,240},{240,288},{288,336},{3... | collective-permute-start | bytes 786440 | tf_op jit(solution)/shard_map/ppermute | solution.py:27

commit v8 on v6

--- a/solution.py
+++ b/solution.py
@@ -81,16 +81,18 @@
 
     def spread_of(labels, first):
         label_bf = labels.astype(jnp.bfloat16)
-        ahead = from_next(label_bf)
         back = lax.dot_general(
             next_tile, label_bf, (((0,), (0,)), ((), ())), preferred_element_type=jnp.float32
         )
         if first:
+            ahead = from_next(label_bf)
             packet = from_prev(jnp.concatenate([back, next_cols.reshape(col_rows, classes)]))
             back_in = packet[:row_count]
             degree = self_rows + next_rows + packet[row_count:].reshape(row_count)
         else:
+            label_send, back = lax.optimization_barrier((label_bf, back))
             back_in, degree = from_prev(back), None
+            ahead = from_next(label_send)
         local = jnp.dot(self_tile, label_bf, preferred_element_type=jnp.float32) + jnp.dot(
             next_tile, ahead, preferred_element_type=jnp.float32
         )

time: 160 us -> 161 us (level)
  starting transfers between devices: 23.9 us -> 31.5 us
  waiting for transfers between devices: 34.4 us -> 27.7 us
    ppermute x4, starting transfers between devices: 16.1 us -> 25.7 us  [from_next(): lax.ppermute(block, 'seq', [((i + 1) % count, i) for i in range(count)])]
    ppermute x3, waiting for transfers between devices: 15.8 us -> 6.51 us  [from_prev(): lax.ppermute(block, 'seq', [(i, (i + 1) % count) for i in range(count)])]
    ppermute x4, waiting for transfers between devices: 18.6 us -> 21.2 us  [from_next(): lax.ppermute(block, 'seq', [((i + 1) % count, i) for i in range(count)])]
    ppermute x3, starting transfers between devices: 7.76 us -> 5.76 us  [from_prev(): lax.ppermute(block, 'seq', [(i, (i + 1) % count) for i in range(count)])]
where the time goes in v8:
time: 161 us; the launch traced here: 160 us
  blocking collectives  80.6 us (50%)
  starting transfers between devices  31.5 us (20%)
  waiting for transfers between devices  27.7 us (17%)
  matrix products  8.81 us (5%)
  other arithmetic  6.34 us (4%)
  local copies, waits for them, and re-layouts  3.47 us (2%)
  between operations  1.73 us (1%)
    all_gather x3, blocking collectives, body(): table_a = lax.all_gather(table_a, axis, axis=0, tiled=False)  46.2 us
    all_gather x3, blocking collectives, gather_groups(): value = lax.all_gather(value, axis, axis=0, tiled=True)  34.4 us
    ppermute x4, starting transfers between devices, from_next(): lax.ppermute(block, 'seq', [((i + 1) % count, i) for i in range(count)])  25.7 us
    ppermute x4, waiting for transfers between devices, from_next(): lax.ppermute(block, 'seq', [((i + 1) % count, i) for i in range(count)])  21.2 us
    ppermute x3, waiting for transfers between devices, from_prev(): lax.ppermute(block, 'seq', [(i, (i + 1) % count) for i in range(count)])  6.51 us
    ppermute x3, starting transfers between devices, from_prev(): lax.ppermute(block, 'seq', [(i, (i + 1) % count) for i in range(count)])  5.76 us
    another operation x4, other arithmetic  3.35 us
  transfers between devices with their start and end apart: 7, of which 4 were waited for; matrix products, arithmetic and copies ran while one was open for 7% of the time, Pallas kernels for 0%

profile of v8, /device:TPU:64, one launch (start us, length us, event | category | flops | bytes accessed | tf_op | source)
XLA Modules:
  0.0 160.2 jit_solution(13793047885587117500)
XLA Ops:
  0.0 1.6 fusion.2
  1.6 0.3 convert_reduce_fusion
  2.0 7.7 %collective-permute-start = (bf16[512,1024]{1,0:T(8,128)(2,1)S(1)}, bf16[512,1024]{1,0:T(8,128)(2,1)}, u32[]{:S(2)}, u32[]{:S(2)}) collective-permute-start(bf16[512,1024]{1,0:T(8,128)(2,1)S(1)} %get-tuple-element.40), channel_id=1, source_target_pairs={{48,0},{96,48},{144,96},{192,144},{240,192},{288,240},{336,288},{3... | collective-permute-start | bytes 3145736 | tf_op jit(solution)/shard_map/ppermute | solution.py:22
  9.7 2.4 %collective-permute-start.1 = (bf16[512,128]{1,0:T(8,128)(2,1)S(1)}, bf16[512,128]{1,0:T(8,128)(2,1)S(1)}, u32[]{:S(2)}, u32[]{:S(2)}) collective-permute-start(bf16[512,128]{1,0:T(8,128)(2,1)S(1)} %convert_bitcast_fusion.1), channel_id=1, source_target_pairs={{48,0},{96,48},{144,96},{192,144},{240,192},{288,240},{336,288},{3... | collective-permute-start | bytes 393224 | tf_op jit(solution)/shard_map/ppermute | solution.py:22
  12.1 0.6 multiply_reduce_fusion
  13.4 0.7 and_reduce_fusion
  14.1 0.7 fusion.62
  14.8 0.9 convert_reduce_fusion.3
  15.7 17.5 %collective-permute-done = bf16[512,1024]{1,0:T(8,128)(2,1)} collective-permute-done((bf16[512,1024]{1,0:T(8,128)(2,1)S(1)}, bf16[512,1024]{1,0:T(8,128)(2,1)}, u32[]{:S(2)}, u32[]{:S(2)}) %collective-permute-start) | collective-permute-done | bytes 1048608 | tf_op jit(solution)/shard_map/ppermute | solution.py:22
  33.2 2.1 %convert_reduce_fusion.1 = (f32[512]{0:T(512)S(1)}, f32[512]{0:T(512)S(1)}, bf16[512,512]{0,1:T(8,128)(2,1)S(1)}) fusion(bf16[512,1024]{1,0:T(8,128)(2,1)S(1)} %get-tuple-element.40, bf16[512,1024]{1,0:T(8,128)(2,1)} %collective-permute-done), kind=kOutput, calls=%fused_computation.15 | convolution fusion | flops 538442752 | bytes 2625536 | tf_op jit(solution)/shard_map/dot_general | solution.py:44
  35.3 0.3 fusion.70
  35.7 1.9 %collective-permute-start.2 = (f32[516,128]{1,0:T(8,128)S(1)}, f32[516,128]{1,0:T(8,128)S(1)}, u32[]{:S(2)}, u32[]{:S(2)}) collective-permute-start(f32[516,128]{1,0:T(8,128)S(1)} %pad_maximum_fusion), channel_id=1, source_target_pairs={{0,48},{48,96},{96,144},{144,192},{192,240},{240,288},{288,336},{3... | collective-permute-start | bytes 792584 | tf_op jit(solution)/shard_map/ppermute | solution.py:27
  37.6 0.1 reshape.168
  37.7 0.7 slice.71
  39.1 1.9 %fusion.68 = f32[1,1]{1,0:T(1,128)} fusion(pred[1,1]{1,0:T(4,128)(4,1)} %bitcast.9, f32[1,1]{1,0:T(1,128)S(6)} %convert_element_type.90, s32[]{:T(128)} %bitcast.10, f32[1,12]{1,0:T(1,128)S(1)} %reshape.168), kind=kLoop, calls=%fused_computation.113 | loop fusion | flops 1 | bytes 61 | tf_op jit(solution)/shard_map/select.3
  41.0 1.4 scatter.9
  42.4 0.3 fusion.69
  42.7 5.8 %collective-permute-done.2 = f32[516,128]{1,0:T(8,128)S(1)} collective-permute-done((f32[516,128]{1,0:T(8,128)S(1)}, f32[516,128]{1,0:T(8,128)S(1)}, u32[]{:S(2)}, u32[]{:S(2)}) %collective-permute-start.2) | collective-permute-done | bytes 264224 | tf_op jit(solution)/shard_map/ppermute | solution.py:27
  48.5 0.3 bitcast_reduce_fusion.1
  48.9 30.9 %all-gather.4 = f32[12,41,128]{2,1,0:T(8,128)S(1)} all-gather(f32[1,41,128]{2,1,0:T(8,128)S(1)} %maximum_bitcast_fusion), channel_id=2, replica_groups=mesh['seq'=16,'grp_z'=12,'grp_y'=2,'grp_c'=2] {'grp_z'}, dimensions={0}, use_global_device_ids=true | all-gather | bytes 272896 | tf_op jit(solution)/shard_map/all_gather | solution.py:113
  79.7 12.7 %all-gather.1 = f32[24,41,128]{2,1,0:T(8,128)S(1)} all-gather(f32[12,41,128]{2,1,0:T(8,128)S(1)} %all-gather.4), channel_id=3, replica_groups=mesh['seq'=16,'grp_z'=12,'grp_y'=2,'grp_c'=2] {'grp_y'}, dimensions={0}, use_global_device_ids=true | all-gather | bytes 755712 | tf_op jit(solution)/shard_map/all_gather | solution.py:113
  92.4 2.6 %all-gather.2 = f32[4,12,41,128]{3,2,1,0:T(8,128)S(1)} all-gather(f32[2,12,41,128]{3,2,1,0:T(8,128)S(1)} %bitcast.120), channel_id=4, replica_groups=mesh['seq'=16,'grp_z'=12,'grp_y'=2,'grp_c'=2] {'grp_c'}, dimensions={0}, use_global_device_ids=true | all-gather | bytes 1511424 | tf_op jit(solution)/shard_map/all_gather | solution.py:113
  95.1 0.7 copy.39
  95.7 0.5 copy.40
  96.2 0.1 copy.44
  96.4 0.3 fusion.23
  96.7 0.1 convert_reduce_fusion.6
  96.8 0.5 fusion.35
  97.4 0.1 fusion.42
  97.4 0.3 fusion.71
  97.8 0.3 fusion.72
  98.1 1.9 %collective-permute-start.4 = (f32[512,128]{1,0:T(8,128)S(1)}, f32[512,128]{1,0:T(8,128)S(1)}, u32[]{:S(2)}, u32[]{:S(2)}) collective-permute-start(f32[512,128]{1,0:T(8,128)S(1)} %fusion.72), channel_id=1, source_target_pairs={{0,48},{48,96},{96,144},{144,192},{192,240},{240,288},{288,336},{3... | collective-permute-start | bytes 786440 | tf_op jit(solution)/shard_map/ppermute | solution.py:27
  100.0 7.8 %collective-permute-start.3 = (bf16[512,128]{1,0:T(8,128)(2,1)S(1)}, bf16[512,128]{1,0:T(8,128)(2,1)S(1)}, u32[]{:S(2)}, u32[]{:S(2)}) collective-permute-start(bf16[512,128]{1,0:T(8,128)(2,1)S(1)} %fusion.42), channel_id=1, source_target_pairs={{48,0},{96,48},{144,96},{192,144},{240,192},{288,240},{336,288},{3... | collective-permute-start | bytes 393224 | tf_op jit(solution)/shard_map/ppermute | solution.py:22
  107.8 0.1 convert_reduce_fusion.5
  107.9 0.6 fusion.29
  108.5 0.1 convert_reduce_fusion.4
  108.6 3.7 %collective-permute-done.3 = bf16[512,128]{1,0:T(8,128)(2,1)S(1)} collective-permute-done((bf16[512,128]{1,0:T(8,128)(2,1)S(1)}, bf16[512,128]{1,0:T(8,128)(2,1)S(1)}, u32[]{:S(2)}, u32[]{:S(2)}) %collective-permute-start.3) | collective-permute-done | bytes 131104 | tf_op jit(solution)/shard_map/ppermute | solution.py:22
  112.3 0.7 collective-permute-done.4
  113.1 0.4 bitcast_reduce_fusion
  113.5 0.3 fusion.74
  113.8 1.9 %collective-permute-start.6 = (f32[512,128]{1,0:T(8,128)S(1)}, f32[512,128]{1,0:T(8,128)S(1)}, u32[]{:S(2)}, u32[]{:S(2)}) collective-permute-start(f32[512,128]{1,0:T(8,128)S(1)} %fusion.74), channel_id=1, source_target_pairs={{0,48},{48,96},{96,144},{144,192},{192,240},{240,288},{288,336},{3... | collective-permute-start | bytes 786440 | tf_op jit(solution)/shard_map/ppermute | solution.py:27
  115.7 7.8 %collective-permute-start.5 = (bf16[512,128]{1,0:T(8,128)(2,1)S(1)}, bf16[512,128]{1,0:T(8,128)(2,1)S(1)}, u32[]{:S(2)}, u32[]{:S(2)}) collective-permute-start(bf16[512,128]{1,0:T(8,128)(2,1)S(1)} %fusion.39), channel_id=1, source_target_pairs={{48,0},{96,48},{144,96},{192,144},{240,192},{288,240},{336,288},{3... | collective-permute-start | bytes 393224 | tf_op jit(solution)/shard_map/ppermute | solution.py:22
  123.6 1.8 %all-gather.3 = f32[32,128]{1,0:T(8,128)S(1)} all-gather(f32[16,128]{1,0:T(8,128)S(1)} %broadcast_multiply_fusion), channel_id=5, replica_groups=mesh['seq'=16,'grp_z'=12,'grp_y'=2,'grp_c'=2] {'grp_c'}, dimensions={0}, use_global_device_ids=true | all-gather | bytes 24576 | tf_op jit(solution)/shard_map/all_gather | solution.py:32
  125.4 8.3 %all_gather.34 = f32[4,16,128]{2,1,0:T(8,128)S(1)} all-gather(f32[2,16,128]{2,1,0:T(8,128)S(1)} %bitcast.124), channel_id=1, replica_groups=mesh['seq'=16,'grp_z'=12,'grp_y'=2,'grp_c'=2] {'grp_y'}, dimensions={0}, use_global_device_ids=true | all-gather | bytes 49152 | tf_op jit(solution)/shard_map/all_gather | solution.py:32
  133.7 24.3 %all_gather.35 = f32[48,16,128]{2,1,0:T(8,128)S(1)} all-gather(f32[4,16,128]{2,1,0:T(8,128)S(1)} %all_gather.34), channel_id=1, replica_groups=mesh['seq'=16,'grp_z'=12,'grp_y'=2,'grp_c'=2] {'grp_z'}, dimensions={0}, use_global_device_ids=true | all-gather | bytes 425984 | tf_op jit(solution)/shard_map/all_gather | solution.py:32
  158.0 0.7 fusion.33
  158.7 0.3 fusion.73
  159.1 1.1 fusion.19
  (30 shorter events, 0.3 us)
Async XLA Ops:
  0.0 1.6 %copy-start.1 = (bf16[1,1,512,1024]{3,2,1,0:T(8,128)(2,1)S(1)}, bf16[1,1,512,1024]{3,2,1,0:T(8,128)(2,1)}, u32[]{:S(2)}) copy-start(bf16[1,1,512,1024]{3,2,1,0:T(8,128)(2,1)} %param.8) | copy-start | bytes 3145732
  1.6 8.1 %copy-start = (f32[1,1,512,128]{3,2,1,0:T(8,128)S(1)}, f32[1,1,512,128]{3,2,1,0:T(8,128)}, u32[]{:S(2)}) copy-start(f32[1,1,512,128]{3,2,1,0:T(8,128)} %param.9) | copy-start | bytes 786436
  1.6 12.5 %copy-start.2 = (s32[1,1,3,4]{3,1,2,0:T(1,128)S(1)}, s32[1,1,3,4]{3,1,2,0:T(1,128)}, u32[]{:S(2)}) copy-start(s32[1,1,3,4]{3,1,2,0:T(1,128)} %param.10) | copy-start | bytes 148
  2.0 31.3 %collective-permute-start = (bf16[512,1024]{1,0:T(8,128)(2,1)S(1)}, bf16[512,1024]{1,0:T(8,128)(2,1)}, u32[]{:S(2)}, u32[]{:S(2)}) collective-permute-start(bf16[512,1024]{1,0:T(8,128)(2,1)S(1)} %get-tuple-element.40), channel_id=1, source_target_pairs={{48,0},{96,48},{144,96},{192,144},{240,192},{288,240},{336,288},{3... | collective-permute-start | bytes 3145736 | tf_op jit(solution)/shard_map/ppermute | solution.py:22
  9.7 38.8 %collective-permute-start.1 = (bf16[512,128]{1,0:T(8,128)(2,1)S(1)}, bf16[512,128]{1,0:T(8,128)(2,1)S(1)}, u32[]{:S(2)}, u32[]{:S(2)}) collective-permute-start(bf16[512,128]{1,0:T(8,128)(2,1)S(1)} %convert_bitcast_fusion.1), channel_id=1, source_target_pairs={{48,0},{96,48},{144,96},{192,144},{240,192},{288,240},{336,288},{3... | collective-permute-start | bytes 393224 | tf_op jit(solution)/shard_map/ppermute | solution.py:22
  35.7 12.8 %collective-permute-start.2 = (f32[516,128]{1,0:T(8,128)S(1)}, f32[516,128]{1,0:T(8,128)S(1)}, u32[]{:S(2)}, u32[]{:S(2)}) collective-permute-start(f32[516,128]{1,0:T(8,128)S(1)} %pad_maximum_fusion), channel_id=1, source_target_pairs={{0,48},{48,96},{96,144},{144,192},{192,240},{240,288},{288,336},{3... | collective-permute-start | bytes 792584 | tf_op jit(solution)/shard_map/ppermute | solution.py:27
  98.1 15.0 %collective-permute-start.4 = (f32[512,128]{1,0:T(8,128)S(1)}, f32[512,128]{1,0:T(8,128)S(1)}, u32[]{:S(2)}, u32[]{:S(2)}) collective-permute-start(f32[512,128]{1,0:T(8,128)S(1)} %fusion.72), channel_id=1, source_target_pairs={{0,48},{48,96},{96,144},{144,192},{192,240},{240,288},{288,336},{3... | collective-permute-start | bytes 786440 | tf_op jit(solution)/shard_map/ppermute | solution.py:27
  100.0 12.3 %collective-permute-start.3 = (bf16[512,128]{1,0:T(8,128)(2,1)S(1)}, bf16[512,128]{1,0:T(8,128)(2,1)S(1)}, u32[]{:S(2)}, u32[]{:S(2)}) collective-permute-start(bf16[512,128]{1,0:T(8,128)(2,1)S(1)} %fusion.42), channel_id=1, source_target_pairs={{48,0},{96,48},{144,96},{192,144},{240,192},{288,240},{336,288},{3... | collective-permute-start | bytes 393224 | tf_op jit(solution)/shard_map/ppermute | solution.py:22
  113.8 45.3 %collective-permute-start.6 = (f32[512,128]{1,0:T(8,128)S(1)}, f32[512,128]{1,0:T(8,128)S(1)}, u32[]{:S(2)}, u32[]{:S(2)}) collective-permute-start(f32[512,128]{1,0:T(8,128)S(1)} %fusion.74), channel_id=1, source_target_pairs={{0,48},{48,96},{96,144},{144,192},{192,240},{240,288},{288,336},{3... | collective-permute-start | bytes 786440 | tf_op jit(solution)/shard_map/ppermute | solution.py:27
  115.7 43.3 %collective-permute-start.5 = (bf16[512,128]{1,0:T(8,128)(2,1)S(1)}, bf16[512,128]{1,0:T(8,128)(2,1)S(1)}, u32[]{:S(2)}, u32[]{:S(2)}) collective-permute-start(bf16[512,128]{1,0:T(8,128)(2,1)S(1)} %fusion.39), channel_id=1, source_target_pairs={{48,0},{96,48},{144,96},{192,144},{240,192},{288,240},{336,288},{3... | collective-permute-start | bytes 393224 | tf_op jit(solution)/shard_map/ppermute | solution.py:22

commit v9 on v8

--- a/solution.py
+++ b/solution.py
@@ -79,7 +79,7 @@
     next_rows = jnp.sum(next_tile, axis=1, dtype=jnp.float32)
     next_cols = jnp.sum(next_tile, axis=0, dtype=jnp.float32)
 
-    def spread_of(labels, first):
+    def spread_of(labels, first, product_first=False):
         label_bf = labels.astype(jnp.bfloat16)
         back = lax.dot_general(
             next_tile, label_bf, (((0,), (0,)), ((), ())), preferred_element_type=jnp.float32
@@ -89,10 +89,13 @@
             packet = from_prev(jnp.concatenate([back, next_cols.reshape(col_rows, classes)]))
             back_in = packet[:row_count]
             degree = self_rows + next_rows + packet[row_count:].reshape(row_count)
-        else:
+        elif product_first:
             label_send, back = lax.optimization_barrier((label_bf, back))
             back_in, degree = from_prev(back), None
             ahead = from_next(label_send)
+        else:
+            ahead = from_next(label_bf)
+            back_in, degree = from_prev(back), None
         local = jnp.dot(self_tile, label_bf, preferred_element_type=jnp.float32) + jnp.dot(
             next_tile, ahead, preferred_element_type=jnp.float32
         )
@@ -138,7 +141,7 @@
     far_1 = far_all(1, next_summary(spread_means, far_0))
     labels = keep_share * seed + (1.0 - keep_share) * (spread + rows_of(own(far_0)))
 
-    local, _ = spread_of(labels, False)
+    local, _ = spread_of(labels, False, True)
     spread = local / degree[:, None]
     labels = keep_share * seed + (1.0 - keep_share) * (spread + rows_of(own(far_1)))
     spread_means = gather_groups(summarize(spread)[None])

time: 161 us -> 159 us (0.988)
  the two profiles are of different devices: /device:TPU:64 before, /device:TPU:14 now
where the time goes in v9:
time: 159 us
  blocking collectives  84.2 us (53%)
  starting transfers between devices  29 us (18%)
  waiting for transfers between devices  25.3 us (16%)
  matrix products  8.8 us (6%)
  other arithmetic  6.34 us (4%)
  local copies, waits for them, and re-layouts  3.47 us (2%)
  between operations  1.75 us (1%)
    all_gather x3, blocking collectives, body(): table_a = lax.all_gather(table_a, axis, axis=0, tiled=False)  48.8 us
    all_gather x3, blocking collectives, gather_groups(): value = lax.all_gather(value, axis, axis=0, tiled=True)  35.4 us
    ppermute x4, waiting for transfers between devices, from_next(): lax.ppermute(block, 'seq', [((i + 1) % count, i) for i in range(count)])  25.3 us
    ppermute x3, starting transfers between devices, from_prev(): lax.ppermute(block, 'seq', [(i, (i + 1) % count) for i in range(count)])  15.8 us
    ppermute x4, starting transfers between devices, from_next(): lax.ppermute(block, 'seq', [((i + 1) % count, i) for i in range(count)])  13.2 us
    another operation x4, other arithmetic  3.35 us
  transfers between devices with their start and end apart: 7, of which 2 were waited for; matrix products, arithmetic and copies ran while one was open for 7% of the time, Pallas kernels for 0%

profile of v9, /device:TPU:14, one launch (start us, length us, event | category | flops | bytes accessed | tf_op | source)
XLA Modules:
  0.0 158.9 jit_solution(3996443017029541683)
XLA Ops:
  0.0 1.6 %fusion.2 = f32[512]{0:T(512)S(1)} fusion(bf16[1,1,512,1024]{3,2,1,0:T(8,128)(2,1)} %param.8), kind=kLoop, calls=%fused_computation.4 | loop fusion | flops 1572352 | bytes 1050624 | tf_op jit(solution)/shard_map/reduce_sum | solution.py:38
  1.6 0.0 copy-start.2
  1.6 0.3 convert_reduce_fusion
  2.0 2.4 %collective-permute-start = (bf16[512,1024]{1,0:T(8,128)(2,1)S(1)}, bf16[512,1024]{1,0:T(8,128)(2,1)}, u32[]{:S(2)}, u32[]{:S(2)}) collective-permute-start(bf16[512,1024]{1,0:T(8,128)(2,1)S(1)} %get-tuple-element.36), channel_id=1, source_target_pairs={{48,0},{96,48},{144,96},{192,144},{240,192},{288,240},{336,288},{3... | collective-permute-start | bytes 3145736 | tf_op jit(solution)/shard_map/ppermute | solution.py:22
  4.4 5.8 %collective-permute-start.1 = (bf16[512,128]{1,0:T(8,128)(2,1)S(1)}, bf16[512,128]{1,0:T(8,128)(2,1)S(1)}, u32[]{:S(2)}, u32[]{:S(2)}) collective-permute-start(bf16[512,128]{1,0:T(8,128)(2,1)S(1)} %convert_bitcast_fusion.1), channel_id=1, source_target_pairs={{48,0},{96,48},{144,96},{192,144},{240,192},{288,240},{336,288},{3... | collective-permute-start | bytes 393224 | tf_op jit(solution)/shard_map/ppermute | solution.py:22
  10.1 0.6 multiply_reduce_fusion
  11.4 0.7 and_reduce_fusion
  12.2 0.7 fusion.62
  12.9 0.9 convert_reduce_fusion.3
  13.8 16.2 %collective-permute-done = bf16[512,1024]{1,0:T(8,128)(2,1)} collective-permute-done((bf16[512,1024]{1,0:T(8,128)(2,1)S(1)}, bf16[512,1024]{1,0:T(8,128)(2,1)}, u32[]{:S(2)}, u32[]{:S(2)}) %collective-permute-start) | collective-permute-done | bytes 1048608 | tf_op jit(solution)/shard_map/ppermute | solution.py:22
  30.0 2.1 %convert_reduce_fusion.1 = (f32[512]{0:T(512)S(1)}, f32[512]{0:T(512)S(1)}, bf16[512,512]{0,1:T(8,128)(2,1)S(1)}) fusion(bf16[512,1024]{1,0:T(8,128)(2,1)S(1)} %get-tuple-element.36, bf16[512,1024]{1,0:T(8,128)(2,1)} %collective-permute-done), kind=kOutput, calls=%fused_computation.15 | convolution fusion | flops 538442752 | bytes 2625536 | tf_op jit(solution)/shard_map/dot_general | solution.py:44
  32.1 0.3 fusion.70
  32.5 3.5 %collective-permute-start.2 = (f32[516,128]{1,0:T(8,128)S(1)}, f32[516,128]{1,0:T(8,128)S(1)}, u32[]{:S(2)}, u32[]{:S(2)}) collective-permute-start(f32[516,128]{1,0:T(8,128)S(1)} %pad_maximum_fusion), channel_id=1, source_target_pairs={{0,48},{48,96},{96,144},{144,192},{192,240},{240,288},{288,336},{3... | collective-permute-start | bytes 792584 | tf_op jit(solution)/shard_map/ppermute | solution.py:27
  36.0 0.1 reshape.168
  36.1 0.7 slice.71
  37.4 1.9 %fusion.68 = f32[1,1]{1,0:T(1,128)} fusion(pred[1,1]{1,0:T(4,128)(4,1)} %bitcast.9, f32[1,1]{1,0:T(1,128)S(6)} %convert_element_type.90, s32[]{:T(128)} %bitcast.10, f32[1,12]{1,0:T(1,128)S(1)} %reshape.168), kind=kLoop, calls=%fused_computation.113 | loop fusion | flops 1 | bytes 61 | tf_op jit(solution)/shard_map/select.3
  39.4 1.4 scatter.9
  40.7 0.3 fusion.69
  41.1 0.4 bitcast_reduce_fusion.1
  41.5 34.0 %all-gather.4 = f32[12,41,128]{2,1,0:T(8,128)S(1)} all-gather(f32[1,41,128]{2,1,0:T(8,128)S(1)} %maximum_bitcast_fusion), channel_id=2, replica_groups=mesh['seq'=16,'grp_z'=12,'grp_y'=2,'grp_c'=2] {'grp_z'}, dimensions={0}, use_global_device_ids=true | all-gather | bytes 272896 | tf_op jit(solution)/shard_map/all_gather | solution.py:116
  75.5 12.2 %all-gather.1 = f32[24,41,128]{2,1,0:T(8,128)S(1)} all-gather(f32[12,41,128]{2,1,0:T(8,128)S(1)} %all-gather.4), channel_id=3, replica_groups=mesh['seq'=16,'grp_z'=12,'grp_y'=2,'grp_c'=2] {'grp_y'}, dimensions={0}, use_global_device_ids=true | all-gather | bytes 755712 | tf_op jit(solution)/shard_map/all_gather | solution.py:116
  87.7 2.6 %all-gather.2 = f32[4,12,41,128]{3,2,1,0:T(8,128)S(1)} all-gather(f32[2,12,41,128]{3,2,1,0:T(8,128)S(1)} %bitcast.120), channel_id=4, replica_groups=mesh['seq'=16,'grp_z'=12,'grp_y'=2,'grp_c'=2] {'grp_c'}, dimensions={0}, use_global_device_ids=true | all-gather | bytes 1511424 | tf_op jit(solution)/shard_map/all_gather | solution.py:116
  90.3 0.7 copy.39
  91.0 0.5 copy.40
  91.5 0.1 copy.44
  91.6 0.3 fusion.23
  92.0 0.1 convert_reduce_fusion.6
  92.1 0.5 fusion.35
  92.6 0.1 fusion.42
  92.7 0.3 fusion.71
  93.0 0.3 fusion.72
  93.3 9.6 %collective-permute-start.4 = (f32[512,128]{1,0:T(8,128)S(1)}, f32[512,128]{1,0:T(8,128)S(1)}, u32[]{:S(2)}, u32[]{:S(2)}) collective-permute-start(f32[512,128]{1,0:T(8,128)S(1)} %fusion.72), channel_id=1, source_target_pairs={{0,48},{48,96},{96,144},{144,192},{192,240},{240,288},{288,336},{3... | collective-permute-start | bytes 786440 | tf_op jit(solution)/shard_map/ppermute | solution.py:27
  103.0 1.9 %collective-permute-start.3 = (bf16[512,128]{1,0:T(8,128)(2,1)S(1)}, bf16[512,128]{1,0:T(8,128)(2,1)S(1)}, u32[]{:S(2)}, u32[]{:S(2)}) collective-permute-start(bf16[512,128]{1,0:T(8,128)(2,1)S(1)} %fusion.42), channel_id=1, source_target_pairs={{48,0},{96,48},{144,96},{192,144},{240,192},{288,240},{336,288},{3... | collective-permute-start | bytes 393224 | tf_op jit(solution)/shard_map/ppermute | solution.py:22
  104.9 0.1 convert_reduce_fusion.5
  105.0 0.6 fusion.29
  105.6 0.1 convert_reduce_fusion.4
  105.7 9.1 %collective-permute-done.3 = bf16[512,128]{1,0:T(8,128)(2,1)S(1)} collective-permute-done((bf16[512,128]{1,0:T(8,128)(2,1)S(1)}, bf16[512,128]{1,0:T(8,128)(2,1)S(1)}, u32[]{:S(2)}, u32[]{:S(2)}) %collective-permute-start.3) | collective-permute-done | bytes 131104 | tf_op jit(solution)/shard_map/ppermute | solution.py:22
  114.8 0.4 bitcast_reduce_fusion
  115.1 0.1 fusion.39
  115.2 0.3 fusion.74
  115.5 3.1 %collective-permute-start.5 = (bf16[512,128]{1,0:T(8,128)(2,1)S(1)}, bf16[512,128]{1,0:T(8,128)(2,1)S(1)}, u32[]{:S(2)}, u32[]{:S(2)}) collective-permute-start(bf16[512,128]{1,0:T(8,128)(2,1)S(1)} %fusion.39), channel_id=1, source_target_pairs={{48,0},{96,48},{144,96},{192,144},{240,192},{288,240},{336,288},{3... | collective-permute-start | bytes 393224 | tf_op jit(solution)/shard_map/ppermute | solution.py:22
  118.7 2.7 %collective-permute-start.6 = (f32[512,128]{1,0:T(8,128)S(1)}, f32[512,128]{1,0:T(8,128)S(1)}, u32[]{:S(2)}, u32[]{:S(2)}) collective-permute-start(f32[512,128]{1,0:T(8,128)S(1)} %fusion.74), channel_id=1, source_target_pairs={{0,48},{48,96},{96,144},{144,192},{192,240},{240,288},{288,336},{3... | collective-permute-start | bytes 786440 | tf_op jit(solution)/shard_map/ppermute | solution.py:27
  121.4 1.8 %all-gather.3 = f32[32,128]{1,0:T(8,128)S(1)} all-gather(f32[16,128]{1,0:T(8,128)S(1)} %broadcast_multiply_fusion), channel_id=5, replica_groups=mesh['seq'=16,'grp_z'=12,'grp_y'=2,'grp_c'=2] {'grp_c'}, dimensions={0}, use_global_device_ids=true | all-gather | bytes 24576 | tf_op jit(solution)/shard_map/all_gather | solution.py:32
  123.2 11.8 %all_gather.34 = f32[4,16,128]{2,1,0:T(8,128)S(1)} all-gather(f32[2,16,128]{2,1,0:T(8,128)S(1)} %bitcast.124), channel_id=1, replica_groups=mesh['seq'=16,'grp_z'=12,'grp_y'=2,'grp_c'=2] {'grp_y'}, dimensions={0}, use_global_device_ids=true | all-gather | bytes 49152 | tf_op jit(solution)/shard_map/all_gather | solution.py:32
  135.0 21.7 %all_gather.35 = f32[48,16,128]{2,1,0:T(8,128)S(1)} all-gather(f32[4,16,128]{2,1,0:T(8,128)S(1)} %all_gather.34), channel_id=1, replica_groups=mesh['seq'=16,'grp_z'=12,'grp_y'=2,'grp_c'=2] {'grp_z'}, dimensions={0}, use_global_device_ids=true | all-gather | bytes 425984 | tf_op jit(solution)/shard_map/all_gather | solution.py:32
  156.7 0.7 fusion.33
  157.4 0.3 fusion.73
  157.8 1.1 fusion.19
  (30 shorter events, 0.2 us)
Async XLA Ops:
  0.0 1.6 %copy-start.1 = (bf16[1,1,512,1024]{3,2,1,0:T(8,128)(2,1)S(1)}, bf16[1,1,512,1024]{3,2,1,0:T(8,128)(2,1)}, u32[]{:S(2)}) copy-start(bf16[1,1,512,1024]{3,2,1,0:T(8,128)(2,1)} %param.8) | copy-start | bytes 3145732
  1.6 2.7 %copy-start = (f32[1,1,512,128]{3,2,1,0:T(8,128)S(1)}, f32[1,1,512,128]{3,2,1,0:T(8,128)}, u32[]{:S(2)}) copy-start(f32[1,1,512,128]{3,2,1,0:T(8,128)} %param.9) | copy-start | bytes 786436
  1.6 10.5 %copy-start.2 = (s32[1,1,3,4]{3,1,2,0:T(1,128)S(1)}, s32[1,1,3,4]{3,1,2,0:T(1,128)}, u32[]{:S(2)}) copy-start(s32[1,1,3,4]{3,1,2,0:T(1,128)} %param.10) | copy-start | bytes 148
  2.0 28.0 %collective-permute-start = (bf16[512,1024]{1,0:T(8,128)(2,1)S(1)}, bf16[512,1024]{1,0:T(8,128)(2,1)}, u32[]{:S(2)}, u32[]{:S(2)}) collective-permute-start(bf16[512,1024]{1,0:T(8,128)(2,1)S(1)} %get-tuple-element.36), channel_id=1, source_target_pairs={{48,0},{96,48},{144,96},{192,144},{240,192},{288,240},{336,288},{3... | collective-permute-start | bytes 3145736 | tf_op jit(solution)/shard_map/ppermute | solution.py:22
  4.4 36.7 %collective-permute-start.1 = (bf16[512,128]{1,0:T(8,128)(2,1)S(1)}, bf16[512,128]{1,0:T(8,128)(2,1)S(1)}, u32[]{:S(2)}, u32[]{:S(2)}) collective-permute-start(bf16[512,128]{1,0:T(8,128)(2,1)S(1)} %convert_bitcast_fusion.1), channel_id=1, source_target_pairs={{48,0},{96,48},{144,96},{192,144},{240,192},{288,240},{336,288},{3... | collective-permute-start | bytes 393224 | tf_op jit(solution)/shard_map/ppermute | solution.py:22
  32.5 8.6 %collective-permute-start.2 = (f32[516,128]{1,0:T(8,128)S(1)}, f32[516,128]{1,0:T(8,128)S(1)}, u32[]{:S(2)}, u32[]{:S(2)}) collective-permute-start(f32[516,128]{1,0:T(8,128)S(1)} %pad_maximum_fusion), channel_id=1, source_target_pairs={{0,48},{48,96},{96,144},{144,192},{192,240},{240,288},{288,336},{3... | collective-permute-start | bytes 792584 | tf_op jit(solution)/shard_map/ppermute | solution.py:27
  93.3 21.5 %collective-permute-start.4 = (f32[512,128]{1,0:T(8,128)S(1)}, f32[512,128]{1,0:T(8,128)S(1)}, u32[]{:S(2)}, u32[]{:S(2)}) collective-permute-start(f32[512,128]{1,0:T(8,128)S(1)} %fusion.72), channel_id=1, source_target_pairs={{0,48},{48,96},{96,144},{144,192},{192,240},{240,288},{288,336},{3... | collective-permute-start | bytes 786440 | tf_op jit(solution)/shard_map/ppermute | solution.py:27
  103.0 11.8 %collective-permute-start.3 = (bf16[512,128]{1,0:T(8,128)(2,1)S(1)}, bf16[512,128]{1,0:T(8,128)(2,1)S(1)}, u32[]{:S(2)}, u32[]{:S(2)}) collective-permute-start(bf16[512,128]{1,0:T(8,128)(2,1)S(1)} %fusion.42), channel_id=1, source_target_pairs={{48,0},{96,48},{144,96},{192,144},{240,192},{288,240},{336,288},{3... | collective-permute-start | bytes 393224 | tf_op jit(solution)/shard_map/ppermute | solution.py:22
  115.5 42.3 %collective-permute-start.5 = (bf16[512,128]{1,0:T(8,128)(2,1)S(1)}, bf16[512,128]{1,0:T(8,128)(2,1)S(1)}, u32[]{:S(2)}, u32[]{:S(2)}) collective-permute-start(bf16[512,128]{1,0:T(8,128)(2,1)S(1)} %fusion.39), channel_id=1, source_target_pairs={{48,0},{96,48},{144,96},{192,144},{240,192},{288,240},{336,288},{3... | collective-permute-start | bytes 393224 | tf_op jit(solution)/shard_map/ppermute | solution.py:22
  118.7 39.1 %collective-permute-start.6 = (f32[512,128]{1,0:T(8,128)S(1)}, f32[512,128]{1,0:T(8,128)S(1)}, u32[]{:S(2)}, u32[]{:S(2)}) collective-permute-start(f32[512,128]{1,0:T(8,128)S(1)} %fusion.74), channel_id=1, source_target_pairs={{0,48},{48,96},{96,144},{144,192},{192,240},{240,288},{288,336},{3... | collective-permute-start | bytes 786440 | tf_op jit(solution)/shard_map/ppermute | solution.py:27

commit v10 on v9

--- a/solution.py
+++ b/solution.py
@@ -27,10 +27,24 @@
     return lax.ppermute(block, "seq", [(i, (i + 1) % count) for i in range(count)])
 
 
+def gather_z(value):
+    count = lax.axis_size(GRP_PARTS[0])
+    block = value.shape[0]
+    held, have = value, 1
+    while have < count:
+        take = min(have, count - have)
+        pairs = [(i, (i - have) % count) for i in range(count)]
+        got = lax.ppermute(held[: take * block], GRP_PARTS[0], pairs)
+        held = jnp.concatenate([held, got])
+        have += take
+    start = (count - lax.axis_index(GRP_PARTS[0])) % count * block
+    return lax.dynamic_slice_in_dim(jnp.concatenate([held, held]), start, count * block, axis=0)
+
+
 def gather_groups(value):
-    for axis in reversed(GRP_PARTS):
+    for axis in reversed(GRP_PARTS[1:]):
         value = lax.all_gather(value, axis, axis=0, tiled=True)
-    return value
+    return gather_z(value)
 
 
 def normalized(values):
@@ -111,8 +125,8 @@
     payload = jnp.concatenate(
         [centre_unit.reshape(centre_rows, classes), seed_mean, summarize(spread), info]
     )
-    table_a = payload
-    for axis in GRP_PARTS:
+    table_a = gather_z(payload[None])
+    for axis in GRP_PARTS[1:]:
         table_a = lax.all_gather(table_a, axis, axis=0, tiled=False)
     table_a = jnp.transpose(table_a, (2, 1, 0, 3, 4)).reshape((groups,) + payload.shape)
     table = table_a[:, :centre_rows].reshape(groups, width)

time: 159 us -> 181 us (1.14)
  the two profiles are of different devices: /device:TPU:14 before, /device:TPU:9 now
where the time goes in v10:
time: 181 us; the launch traced here: 180 us
  starting transfers between devices  78.6 us (43%)
  waiting for transfers between devices  42.5 us (23%)
  blocking collectives  32.3 us (18%)
  matrix products  11.3 us (6%)
  local copies, waits for them, and re-layouts  7.31 us (4%)
  other arithmetic  6.32 us (3%)
  between operations  1.96 us (1%)
    ppermute x8, starting transfers between devices, gather_z(): got = lax.ppermute(held[:take * block], GRP_PARTS[0], pairs)  46.4 us
    ppermute x4, starting transfers between devices, from_next(): lax.ppermute(block, 'seq', [((i + 1) % count, i) for i in range(count)])  25.2 us
    all_gather x2, blocking collectives, body(): table_a = lax.all_gather(table_a, axis, axis=0, tiled=False)  22.4 us
    ppermute x8, waiting for transfers between devices, gather_z(): got = lax.ppermute(held[:take * block], GRP_PARTS[0], pairs)  21 us
    ppermute x4, waiting for transfers between devices, from_next(): lax.ppermute(block, 'seq', [((i + 1) % count, i) for i in range(count)])  13 us
    all_gather x2, blocking collectives, gather_groups(): value = lax.all_gather(value, axis, axis=0, tiled=True)  9.86 us
    ppermute x3, waiting for transfers between devices, from_prev(): lax.ppermute(block, 'seq', [(i, (i + 1) % count) for i in range(count)])  8.45 us
    ppermute x3, starting transfers between devices, from_prev(): lax.ppermute(block, 'seq', [(i, (i + 1) % count) for i in range(count)])  7.04 us
  transfers between devices with their start and end apart: 15, of which 9 were waited for; matrix products, arithmetic and copies ran while one was open for 9% of the time, Pallas kernels for 0%

profile of v10, /device:TPU:9, one launch (start us, length us, event | category | flops | bytes accessed | tf_op | source)
XLA Modules:
  0.0 180.1 jit_solution(11720728625488982388)
XLA Ops:
  0.0 1.6 fusion.2
  2.0 1.9 %collective-permute-start = (bf16[512,1024]{1,0:T(8,128)(2,1)S(1)}, bf16[512,1024]{1,0:T(8,128)(2,1)}, u32[]{:S(2)}, u32[]{:S(2)}) collective-permute-start(bf16[512,1024]{1,0:T(8,128)(2,1)S(1)} %get-tuple-element.36), channel_id=1, source_target_pairs={{48,0},{96,48},{144,96},{192,144},{240,192},{288,240},{336,288},{3... | collective-permute-start | bytes 3145736 | tf_op jit(solution)/shard_map/ppermute | solution.py:22
  3.9 7.6 %collective-permute-start.1 = (bf16[512,128]{1,0:T(8,128)(2,1)S(1)}, bf16[512,128]{1,0:T(8,128)(2,1)}, u32[]{:S(2)}, u32[]{:S(2)}) collective-permute-start(bf16[512,128]{1,0:T(8,128)(2,1)S(1)} %convert_bitcast_fusion.1), channel_id=1, source_target_pairs={{48,0},{96,48},{144,96},{192,144},{240,192},{288,240},{336,288},{3... | collective-permute-start | bytes 393224 | tf_op jit(solution)/shard_map/ppermute | solution.py:22
  11.5 0.6 multiply_reduce_fusion
  12.8 0.7 and_reduce_fusion
  13.5 0.6 fusion.63
  14.2 0.9 convert_reduce_fusion.3
  15.1 12.9 %collective-permute-done = bf16[512,1024]{1,0:T(8,128)(2,1)} collective-permute-done((bf16[512,1024]{1,0:T(8,128)(2,1)S(1)}, bf16[512,1024]{1,0:T(8,128)(2,1)}, u32[]{:S(2)}, u32[]{:S(2)}) %collective-permute-start) | collective-permute-done | bytes 1048608 | tf_op jit(solution)/shard_map/ppermute | solution.py:22
  28.0 2.1 %convert_reduce_fusion.1 = (f32[512]{0:T(512)S(1)}, f32[512]{0:T(512)S(1)}, bf16[512,512]{0,1:T(8,128)(2,1)S(1)}) fusion(bf16[512,1024]{1,0:T(8,128)(2,1)S(1)} %get-tuple-element.36, bf16[512,1024]{1,0:T(8,128)(2,1)} %collective-permute-done), kind=kOutput, calls=%fused_computation.15 | convolution fusion | flops 538442752 | bytes 2625536 | tf_op jit(solution)/shard_map/dot_general | solution.py:58
  30.4 3.2 %collective-permute-start.2 = (f32[516,128]{1,0:T(8,128)S(1)}, f32[516,128]{1,0:T(8,128)S(1)}, u32[]{:S(2)}, u32[]{:S(2)}) collective-permute-start(f32[516,128]{1,0:T(8,128)S(1)} %pad_maximum_fusion), channel_id=1, source_target_pairs={{0,48},{48,96},{96,144},{144,192},{192,240},{240,288},{288,336},{3... | collective-permute-start | bytes 792584 | tf_op jit(solution)/shard_map/ppermute | solution.py:27
  34.4 0.7 slice.71
  35.2 1.9 %fusion.70 = f32[1,1]{1,0:T(1,128)} fusion(pred[1,1]{1,0:T(4,128)(4,1)} %bitcast.9, f32[1,1]{1,0:T(1,128)S(6)} %convert_element_type.90, s32[]{:T(128)} %bitcast.10, f32[1,12]{1,0:T(1,128)S(1)} %reshape.168), kind=kLoop, calls=%fused_computation.130 | loop fusion | flops 1 | bytes 61 | tf_op jit(solution)/shard_map/select.3
  37.1 1.4 scatter.9
  38.4 0.3 fusion.71
  38.8 1.2 bitcast_reduce_fusion.1
  40.1 15.0 %collective-permute-start.3 = (f32[1,41,128]{2,1,0:T(8,128)S(1)}, f32[1,41,128]{2,1,0:T(8,128)S(1)}, u32[]{:S(2)}, u32[]{:S(2)}) collective-permute-start(f32[1,41,128]{2,1,0:T(8,128)S(1)} %maximum_bitcast_fusion), channel_id=1, source_target_pairs={{0,44},{4,0},{8,4},{12,8},{16,12},{20,16},{24,20},{28,24},{32,28},... | collective-permute-start | bytes 62984 | tf_op jit(solution)/shard_map/ppermute | solution.py:37
  55.2 0.9 collective-permute-done.3
  56.1 3.6 %collective-permute-start.4 = (f32[2,41,128]{2,1,0:T(8,128)S(1)}, f32[2,41,128]{2,1,0:T(8,128)S(1)}, u32[]{:S(2)}, u32[]{:S(2)}) collective-permute-start(f32[2,41,128]{2,1,0:T(8,128)S(1)} %pad_maximum_fusion.4), channel_id=1, source_target_pairs={{0,40},{4,44},{8,0},{12,4},{16,8},{20,12},{24,16},{28,20},{32,24},... | collective-permute-start | bytes 125960 | tf_op jit(solution)/shard_map/ppermute | solution.py:37
  59.7 2.1 %collective-permute-done.4 = f32[2,41,128]{2,1,0:T(8,128)S(1)} collective-permute-done((f32[2,41,128]{2,1,0:T(8,128)S(1)}, f32[2,41,128]{2,1,0:T(8,128)S(1)}, u32[]{:S(2)}, u32[]{:S(2)}) %collective-permute-start.4) | collective-permute-done | bytes 42016 | tf_op jit(solution)/shard_map/ppermute | solution.py:37
  61.8 1.9 %collective-permute-start.6 = (f32[4,41,128]{2,1,0:T(8,128)S(1)}, f32[4,41,128]{2,1,0:T(8,128)S(1)}, u32[]{:S(2)}, u32[]{:S(2)}) collective-permute-start(f32[4,41,128]{2,1,0:T(8,128)S(1)} %pad_maximum_fusion.2), channel_id=1, source_target_pairs={{0,16},{4,20},{8,24},{12,28},{16,32},{20,36},{24,40},{28,44},{32,0... | collective-permute-start | bytes 251912 | tf_op jit(solution)/shard_map/ppermute | solution.py:37
  63.7 7.3 %collective-permute-start.5 = (f32[4,41,128]{2,1,0:T(8,128)S(1)}, f32[4,41,128]{2,1,0:T(8,128)S(1)}, u32[]{:S(2)}, u32[]{:S(2)}) collective-permute-start(f32[4,41,128]{2,1,0:T(8,128)S(1)} %pad_maximum_fusion.2), channel_id=1, source_target_pairs={{0,32},{4,36},{8,40},{12,44},{16,0},{20,4},{24,8},{28,12},{32,16},... | collective-permute-start | bytes 251912 | tf_op jit(solution)/shard_map/ppermute | solution.py:37
  71.0 2.1 %collective-permute-done.5 = f32[4,41,128]{2,1,0:T(8,128)S(1)} collective-permute-done((f32[4,41,128]{2,1,0:T(8,128)S(1)}, f32[4,41,128]{2,1,0:T(8,128)S(1)}, u32[]{:S(2)}, u32[]{:S(2)}) %collective-permute-start.5) | collective-permute-done | bytes 84000 | tf_op jit(solution)/shard_map/ppermute | solution.py:37
  73.3 10.3 %all-gather = f32[24,41,128]{2,1,0:T(8,128)S(1)} all-gather(f32[12,41,128]{2,1,0:T(8,128)S(1)} %constant_dynamic-slice_fusion.3), channel_id=2, replica_groups=mesh['seq'=16,'grp_z'=12,'grp_y'=2,'grp_c'=2] {'grp_y'}, dimensions={0}, use_global_device_ids=true | all-gather | bytes 755712 | tf_op jit(solution)/shard_map/all_gather | solution.py:130
  83.5 12.1 %all-gather.1 = f32[4,12,41,128]{3,2,1,0:T(8,128)S(1)} all-gather(f32[2,12,41,128]{3,2,1,0:T(8,128)S(1)} %bitcast.124), channel_id=3, replica_groups=mesh['seq'=16,'grp_z'=12,'grp_y'=2,'grp_c'=2] {'grp_c'}, dimensions={0}, use_global_device_ids=true | all-gather | bytes 1511424 | tf_op jit(solution)/shard_map/all_gather | solution.py:130
  95.7 0.7 copy.51
  96.3 0.5 copy.52
  97.5 0.5 fusion.36
  98.1 0.6 fusion.29
  99.0 9.3 %collective-permute-start.7 = (bf16[512,128]{1,0:T(8,128)(2,1)S(1)}, bf16[512,128]{1,0:T(8,128)(2,1)S(1)}, u32[]{:S(2)}, u32[]{:S(2)}) collective-permute-start(bf16[512,128]{1,0:T(8,128)(2,1)S(1)} %fusion.43), channel_id=1, source_target_pairs={{48,0},{96,48},{144,96},{192,144},{240,192},{288,240},{336,288},{3... | collective-permute-start | bytes 393224 | tf_op jit(solution)/shard_map/ppermute | solution.py:22
  108.3 1.9 %collective-permute-start.8 = (f32[512,128]{1,0:T(8,128)S(1)}, f32[512,128]{1,0:T(8,128)S(1)}, u32[]{:S(2)}, u32[]{:S(2)}) collective-permute-start(f32[512,128]{1,0:T(8,128)S(1)} %fusion.74), channel_id=1, source_target_pairs={{0,48},{48,96},{96,144},{144,192},{192,240},{240,288},{288,336},{3... | collective-permute-start | bytes 786440 | tf_op jit(solution)/shard_map/ppermute | solution.py:27
  110.2 0.3 fusion.73
  110.7 8.4 %collective-permute-done.8 = f32[512,128]{1,0:T(8,128)S(1)} collective-permute-done((f32[512,128]{1,0:T(8,128)S(1)}, f32[512,128]{1,0:T(8,128)S(1)}, u32[]{:S(2)}, u32[]{:S(2)}) %collective-permute-start.8) | collective-permute-done | bytes 262176 | tf_op jit(solution)/shard_map/ppermute | solution.py:27
  119.2 0.4 bitcast_reduce_fusion
  119.6 2.7 %all-gather.2 = f32[32,128]{1,0:T(8,128)S(1)} all-gather(f32[16,128]{1,0:T(8,128)S(1)} %broadcast_multiply_fusion), channel_id=4, replica_groups=mesh['seq'=16,'grp_z'=12,'grp_y'=2,'grp_c'=2] {'grp_c'}, dimensions={0}, use_global_device_ids=true | all-gather | bytes 24576 | tf_op jit(solution)/shard_map/all_gather | solution.py:46
  122.3 7.2 %all_gather.23 = f32[4,16,128]{2,1,0:T(8,128)S(1)} all-gather(f32[2,16,128]{2,1,0:T(8,128)S(1)} %bitcast.128), channel_id=1, replica_groups=mesh['seq'=16,'grp_z'=12,'grp_y'=2,'grp_c'=2] {'grp_y'}, dimensions={0}, use_global_device_ids=true | all-gather | bytes 49152 | tf_op jit(solution)/shard_map/all_gather | solution.py:46
  129.4 6.6 %collective-permute-start.11 = (f32[4,16,128]{2,0,1:T(4,128)S(1)}, f32[4,16,128]{2,0,1:T(4,128)S(1)}, u32[]{:S(2)}, u32[]{:S(2)}) collective-permute-start(f32[4,16,128]{2,0,1:T(4,128)S(1)} %copy.57), channel_id=1, source_target_pairs={{0,44},{4,0},{8,4},{12,8},{16,12},{20,16},{24,20},{28,24},{32,28},... | collective-permute-start | bytes 98312 | tf_op jit(solution)/shard_map/ppermute | solution.py:37
  136.1 6.4 %collective-permute-start.9 = (bf16[512,128]{1,0:T(8,128)(2,1)S(1)}, bf16[512,128]{1,0:T(8,128)(2,1)}, u32[]{:S(2)}, u32[]{:S(2)}) collective-permute-start(bf16[512,128]{1,0:T(8,128)(2,1)S(1)} %fusion.40), channel_id=1, source_target_pairs={{48,0},{96,48},{144,96},{192,144},{240,192},{288,240},{336,288},{3... | collective-permute-start | bytes 393224 | tf_op jit(solution)/shard_map/ppermute | solution.py:22
  142.5 2.8 %collective-permute-start.12 = (f32[8,16,128]{2,0,1:T(8,128)S(1)}, f32[8,16,128]{2,0,1:T(8,128)S(1)}, u32[]{:S(2)}, u32[]{:S(2)}) collective-permute-start(f32[8,16,128]{2,0,1:T(8,128)S(1)} %pad_maximum_fusion.3), channel_id=1, source_target_pairs={{0,40},{4,44},{8,0},{12,4},{16,8},{20,12},{24,16},{28,20},{32,24},... | collective-permute-start | bytes 196616 | tf_op jit(solution)/shard_map/ppermute | solution.py:37
  145.3 1.0 fusion.76
  146.3 1.9 %collective-permute-start.10 = (f32[512,128]{1,0:T(8,128)}, f32[512,128]{1,0:T(8,128)}, u32[]{:S(2)}, u32[]{:S(2)}) collective-permute-start(f32[512,128]{1,0:T(8,128)} %fusion.76), channel_id=1, source_target_pairs={{0,48},{48,96},{96,144},{144,192},{192,240},{240,288},{288,336},{3... | collective-permute-start | bytes 786440 | tf_op jit(solution)/shard_map/ppermute | solution.py:27
  148.5 5.6 %collective-permute-start.14 = (f32[16,16,128]{2,0,1:T(8,128)S(1)}, f32[16,16,128]{2,0,1:T(8,128)}, u32[]{:S(2)}, u32[]{:S(2)}) collective-permute-start(f32[16,16,128]{2,0,1:T(8,128)S(1)} %pad_maximum_fusion.1), channel_id=1, source_target_pairs={{0,16},{4,20},{8,24},{12,28},{16,32},{20,36},{24,40},{28,44},{32,0... | collective-permute-start | bytes 393224 | tf_op jit(solution)/shard_map/ppermute | solution.py:37
  154.1 3.6 %collective-permute-start.13 = (f32[16,16,128]{2,0,1:T(8,128)S(1)}, f32[16,16,128]{2,0,1:T(8,128)}, u32[]{:S(2)}, u32[]{:S(2)}) collective-permute-start(f32[16,16,128]{2,0,1:T(8,128)S(1)} %pad_maximum_fusion.1), channel_id=1, source_target_pairs={{0,32},{4,36},{8,40},{12,44},{16,0},{20,4},{24,8},{28,12},{32,16},... | collective-permute-start | bytes 393224 | tf_op jit(solution)/shard_map/ppermute | solution.py:37
  157.7 0.3 fusion.75
  158.0 1.9 %collective-permute-done.14 = f32[16,16,128]{2,0,1:T(8,128)} collective-permute-done((f32[16,16,128]{2,0,1:T(8,128)S(1)}, f32[16,16,128]{2,0,1:T(8,128)}, u32[]{:S(2)}, u32[]{:S(2)}) %collective-permute-start.14) | collective-permute-done | bytes 131104 | tf_op jit(solution)/shard_map/ppermute | solution.py:37
  159.9 13.8 %collective-permute-done.13 = f32[16,16,128]{2,0,1:T(8,128)} collective-permute-done((f32[16,16,128]{2,0,1:T(8,128)S(1)}, f32[16,16,128]{2,0,1:T(8,128)}, u32[]{:S(2)}, u32[]{:S(2)}) %collective-permute-start.13) | collective-permute-done | bytes 131104 | tf_op jit(solution)/shard_map/ppermute | solution.py:37
  173.7 3.7 %concatenate.43 = f32[96,16,128]{2,0,1:T(8,128)S(1)} concatenate(f32[4,16,128]{2,0,1:T(4,128)S(1)} %copy.57, f32[4,16,128]{2,0,1:T(4,128)S(1)} %collective-permute-done.11, f32[8,16,128]{2,0,1:T(8,128)S(1)} %collective-permute-done.12, f32[16,16,128]{2,0,1:T(8,128)} %collective-permute-done.13, f32[16,16,128]{2,0,1:T(8,128)} %collective-permute-done.14, f32[4,16,128]{2,0,1:T(4,128)S(1)} %copy.57, ...), dimensions={0} | concatenate | bytes 1572864 | tf_op jit(solution)/shard_map/concatenate | solution.py:41
  177.5 0.5 fusion.31
  178.1 2.1 %fusion.19 = f32[1,1,512,128]{3,2,1,0:T(8,128)} fusion(f32[512,128]{1,0:T(8,128)S(1)} %bitcast.125, f32[512,128]{1,0:T(8,128)} %collective-permute-done.10, f32[512,128]{1,0:T(8,128)S(1)} %fusion.75, bf16[512,512]{0,1:T(8,128)(2,1)S(1)} %get-tuple-element.40, bf16[512,128]{1,0:T(8,128)(2,1)} %collective-permute-done.9, f32[1,1,512,128]{3,2,1,0:T(8,128)S(1)} %copy-done, ...), kind=kOutput, calls=%fused_computation.29 | convolution fusion | flops 67567616 | bytes 1968128 | tf_op jit(solution)/shard_map/dot_general | solution.py:113
  (61 shorter events, 2.5 us)
Async XLA Ops:
  0.0 1.6 copy-start.1
  1.6 2.3 %copy-start = (f32[1,1,512,128]{3,2,1,0:T(8,128)S(1)}, f32[1,1,512,128]{3,2,1,0:T(8,128)}, u32[]{:S(2)}) copy-start(f32[1,1,512,128]{3,2,1,0:T(8,128)} %param.9) | copy-start | bytes 786436
  1.6 11.9 %copy-start.2 = (s32[1,1,3,4]{3,1,2,0:T(1,128)S(1)}, s32[1,1,3,4]{3,1,2,0:T(1,128)}, u32[]{:S(2)}) copy-start(s32[1,1,3,4]{3,1,2,0:T(1,128)} %param.10) | copy-start | bytes 148
  2.0 26.0 %collective-permute-start = (bf16[512,1024]{1,0:T(8,128)(2,1)S(1)}, bf16[512,1024]{1,0:T(8,128)(2,1)}, u32[]{:S(2)}, u32[]{:S(2)}) collective-permute-start(bf16[512,1024]{1,0:T(8,128)(2,1)S(1)} %get-tuple-element.36), channel_id=1, source_target_pairs={{48,0},{96,48},{144,96},{192,144},{240,192},{288,240},{336,288},{3... | collective-permute-start | bytes 3145736 | tf_op jit(solution)/shard_map/ppermute | solution.py:22
  3.9 34.9 %collective-permute-start.1 = (bf16[512,128]{1,0:T(8,128)(2,1)S(1)}, bf16[512,128]{1,0:T(8,128)(2,1)}, u32[]{:S(2)}, u32[]{:S(2)}) collective-permute-start(bf16[512,128]{1,0:T(8,128)(2,1)S(1)} %convert_bitcast_fusion.1), channel_id=1, source_target_pairs={{48,0},{96,48},{144,96},{192,144},{240,192},{288,240},{336,288},{3... | collective-permute-start | bytes 393224 | tf_op jit(solution)/shard_map/ppermute | solution.py:22
  30.4 8.3 %collective-permute-start.2 = (f32[516,128]{1,0:T(8,128)S(1)}, f32[516,128]{1,0:T(8,128)S(1)}, u32[]{:S(2)}, u32[]{:S(2)}) collective-permute-start(f32[516,128]{1,0:T(8,128)S(1)} %pad_maximum_fusion), channel_id=1, source_target_pairs={{0,48},{48,96},{96,144},{144,192},{192,240},{240,288},{288,336},{3... | collective-permute-start | bytes 792584 | tf_op jit(solution)/shard_map/ppermute | solution.py:27
  40.1 16.0 %collective-permute-start.3 = (f32[1,41,128]{2,1,0:T(8,128)S(1)}, f32[1,41,128]{2,1,0:T(8,128)S(1)}, u32[]{:S(2)}, u32[]{:S(2)}) collective-permute-start(f32[1,41,128]{2,1,0:T(8,128)S(1)} %maximum_bitcast_fusion), channel_id=1, source_target_pairs={{0,44},{4,0},{8,4},{12,8},{16,12},{20,16},{24,20},{28,24},{32,28},... | collective-permute-start | bytes 62984 | tf_op jit(solution)/shard_map/ppermute | solution.py:37
  56.1 5.7 %collective-permute-start.4 = (f32[2,41,128]{2,1,0:T(8,128)S(1)}, f32[2,41,128]{2,1,0:T(8,128)S(1)}, u32[]{:S(2)}, u32[]{:S(2)}) collective-permute-start(f32[2,41,128]{2,1,0:T(8,128)S(1)} %pad_maximum_fusion.4), channel_id=1, source_target_pairs={{0,40},{4,44},{8,0},{12,4},{16,8},{20,12},{24,16},{28,20},{32,24},... | collective-permute-start | bytes 125960 | tf_op jit(solution)/shard_map/ppermute | solution.py:37
  61.8 11.3 %collective-permute-start.6 = (f32[4,41,128]{2,1,0:T(8,128)S(1)}, f32[4,41,128]{2,1,0:T(8,128)S(1)}, u32[]{:S(2)}, u32[]{:S(2)}) collective-permute-start(f32[4,41,128]{2,1,0:T(8,128)S(1)} %pad_maximum_fusion.2), channel_id=1, source_target_pairs={{0,16},{4,20},{8,24},{12,28},{16,32},{20,36},{24,40},{28,44},{32,0... | collective-permute-start | bytes 251912 | tf_op jit(solution)/shard_map/ppermute | solution.py:37
  63.7 9.4 %collective-permute-start.5 = (f32[4,41,128]{2,1,0:T(8,128)S(1)}, f32[4,41,128]{2,1,0:T(8,128)S(1)}, u32[]{:S(2)}, u32[]{:S(2)}) collective-permute-start(f32[4,41,128]{2,1,0:T(8,128)S(1)} %pad_maximum_fusion.2), channel_id=1, source_target_pairs={{0,32},{4,36},{8,40},{12,44},{16,0},{20,4},{24,8},{28,12},{32,16},... | collective-permute-start | bytes 251912 | tf_op jit(solution)/shard_map/ppermute | solution.py:37
  99.0 11.8 %collective-permute-start.7 = (bf16[512,128]{1,0:T(8,128)(2,1)S(1)}, bf16[512,128]{1,0:T(8,128)(2,1)S(1)}, u32[]{:S(2)}, u32[]{:S(2)}) collective-permute-start(bf16[512,128]{1,0:T(8,128)(2,1)S(1)} %fusion.43), channel_id=1, source_target_pairs={{48,0},{96,48},{144,96},{192,144},{240,192},{288,240},{336,288},{3... | collective-permute-start | bytes 393224 | tf_op jit(solution)/shard_map/ppermute | solution.py:22
  108.3 10.9 %collective-permute-start.8 = (f32[512,128]{1,0:T(8,128)S(1)}, f32[512,128]{1,0:T(8,128)S(1)}, u32[]{:S(2)}, u32[]{:S(2)}) collective-permute-start(f32[512,128]{1,0:T(8,128)S(1)} %fusion.74), channel_id=1, source_target_pairs={{0,48},{48,96},{96,144},{144,192},{192,240},{240,288},{288,336},{3... | collective-permute-start | bytes 786440 | tf_op jit(solution)/shard_map/ppermute | solution.py:27
  129.4 13.1 %collective-permute-start.11 = (f32[4,16,128]{2,0,1:T(4,128)S(1)}, f32[4,16,128]{2,0,1:T(4,128)S(1)}, u32[]{:S(2)}, u32[]{:S(2)}) collective-permute-start(f32[4,16,128]{2,0,1:T(4,128)S(1)} %copy.57), channel_id=1, source_target_pairs={{0,44},{4,0},{8,4},{12,8},{16,12},{20,16},{24,20},{28,24},{32,28},... | collective-permute-start | bytes 98312 | tf_op jit(solution)/shard_map/ppermute | solution.py:37
  136.1 41.9 %collective-permute-start.9 = (bf16[512,128]{1,0:T(8,128)(2,1)S(1)}, bf16[512,128]{1,0:T(8,128)(2,1)}, u32[]{:S(2)}, u32[]{:S(2)}) collective-permute-start(bf16[512,128]{1,0:T(8,128)(2,1)S(1)} %fusion.40), channel_id=1, source_target_pairs={{48,0},{96,48},{144,96},{192,144},{240,192},{288,240},{336,288},{3... | collective-permute-start | bytes 393224 | tf_op jit(solution)/shard_map/ppermute | solution.py:22
  142.5 5.9 %collective-permute-start.12 = (f32[8,16,128]{2,0,1:T(8,128)S(1)}, f32[8,16,128]{2,0,1:T(8,128)S(1)}, u32[]{:S(2)}, u32[]{:S(2)}) collective-permute-start(f32[8,16,128]{2,0,1:T(8,128)S(1)} %pad_maximum_fusion.3), channel_id=1, source_target_pairs={{0,40},{4,44},{8,0},{12,4},{16,8},{20,12},{24,16},{28,20},{32,24},... | collective-permute-start | bytes 196616 | tf_op jit(solution)/shard_map/ppermute | solution.py:37
  146.3 31.7 %collective-permute-start.10 = (f32[512,128]{1,0:T(8,128)}, f32[512,128]{1,0:T(8,128)}, u32[]{:S(2)}, u32[]{:S(2)}) collective-permute-start(f32[512,128]{1,0:T(8,128)} %fusion.76), channel_id=1, source_target_pairs={{0,48},{48,96},{96,144},{144,192},{192,240},{240,288},{288,336},{3... | collective-permute-start | bytes 786440 | tf_op jit(solution)/shard_map/ppermute | solution.py:27
  148.5 11.5 %collective-permute-start.14 = (f32[16,16,128]{2,0,1:T(8,128)S(1)}, f32[16,16,128]{2,0,1:T(8,128)}, u32[]{:S(2)}, u32[]{:S(2)}) collective-permute-start(f32[16,16,128]{2,0,1:T(8,128)S(1)} %pad_maximum_fusion.1), channel_id=1, source_target_pairs={{0,16},{4,20},{8,24},{12,28},{16,32},{20,36},{24,40},{28,44},{32,0... | collective-permute-start | bytes 393224 | tf_op jit(solution)/shard_map/ppermute | solution.py:37
  154.1 19.7 %collective-permute-start.13 = (f32[16,16,128]{2,0,1:T(8,128)S(1)}, f32[16,16,128]{2,0,1:T(8,128)}, u32[]{:S(2)}, u32[]{:S(2)}) collective-permute-start(f32[16,16,128]{2,0,1:T(8,128)S(1)} %pad_maximum_fusion.1), channel_id=1, source_target_pairs={{0,32},{4,36},{8,40},{12,44},{16,0},{20,4},{24,8},{28,12},{32,16},... | collective-permute-start | bytes 393224 | tf_op jit(solution)/shard_map/ppermute | solution.py:37

commit v11 on v9

--- a/solution.py
+++ b/solution.py
@@ -74,10 +74,11 @@
             row_count, classes
         )
 
-    after_unit = from_next(unit_emb)
-    next_tile = kernel_tile(unit_emb, after_unit, False)
+    half = row_count // 2
+    tiles = [kernel_tile(unit_emb, from_next(unit_emb[:half]), False)]
+    tiles.append(kernel_tile(unit_emb, from_next(unit_emb[half:]), False))
+    next_tile = jnp.concatenate(tiles, axis=1)
     next_rows = jnp.sum(next_tile, axis=1, dtype=jnp.float32)
-    next_cols = jnp.sum(next_tile, axis=0, dtype=jnp.float32)
 
     def spread_of(labels, first, product_first=False):
         label_bf = labels.astype(jnp.bfloat16)
@@ -86,9 +87,17 @@
         )
         if first:
             ahead = from_next(label_bf)
-            packet = from_prev(jnp.concatenate([back, next_cols.reshape(col_rows, classes)]))
-            back_in = packet[:row_count]
-            degree = self_rows + next_rows + packet[row_count:].reshape(row_count)
+            back_in, prior_cols = [], []
+            for tile in tiles:
+                part = lax.dot_general(
+                    tile, label_bf, (((0,), (0,)), ((), ())), preferred_element_type=jnp.float32
+                )
+                cols = jnp.sum(tile, axis=0, dtype=jnp.float32).reshape(-1, classes)
+                packet = from_prev(jnp.concatenate([part, cols]))
+                back_in.append(packet[: tile.shape[1]])
+                prior_cols.append(packet[tile.shape[1] :].reshape(-1))
+            back_in = jnp.concatenate(back_in)
+            degree = self_rows + next_rows + jnp.concatenate(prior_cols)
         elif product_first:
             label_send, back = lax.optimization_barrier((label_bf, back))
             back_in, degree = from_prev(back), None

time: 159 us -> 159 us (level)
  waiting for transfers between devices: 25.3 us -> 15.6 us
  starting transfers between devices: 29 us -> 35 us
  matrix products: 8.8 us -> 10.6 us
    ppermute x4 -> x5, waiting for transfers between devices: 25.3 us -> 12.7 us  [from_next(): lax.ppermute(block, 'seq', [((i + 1) % count, i) for i in range(count)])]
    ppermute x4 -> x5, starting transfers between devices: 13.2 us -> 18.1 us  [from_next(): lax.ppermute(block, 'seq', [((i + 1) % count, i) for i in range(count)])]
    ppermute x3 -> x4, waiting for transfers between devices: 0.01 us -> 2.88 us  [from_prev(): lax.ppermute(block, 'seq', [(i, (i + 1) % count) for i in range(count)])]
    ppermute x3 -> x4, starting transfers between devices: 15.8 us -> 16.9 us  [from_prev(): lax.ppermute(block, 'seq', [(i, (i + 1) % count) for i in range(count)])]
    dot_general x2 -> x3, matrix products: 3.07 us -> 4.03 us  [kernel_tile(): score = jnp.dot(left, right.T, preferred_element_type=jnp.float32)]
  transfers between devices with their start and end apart: 7 -> 9, of which waited for: 2 -> 4; matrix products, arithmetic and copies ran while one was open for 7% -> 8% of each run, Pallas kernels for 0% -> 0%
where the time goes in v11:
time: 159 us
  blocking collectives  85.7 us (54%)
  starting transfers between devices  35 us (22%)
  waiting for transfers between devices  15.6 us (10%)
  matrix products  10.6 us (7%)
  other arithmetic  6.35 us (4%)
  local copies, waits for them, and re-layouts  3.48 us (2%)
  between operations  1.81 us (1%)
    all_gather x3, blocking collectives, body(): table_a = lax.all_gather(table_a, axis, axis=0, tiled=False)  49.2 us
    all_gather x3, blocking collectives, gather_groups(): value = lax.all_gather(value, axis, axis=0, tiled=True)  36.5 us
    ppermute x5, starting transfers between devices, from_next(): lax.ppermute(block, 'seq', [((i + 1) % count, i) for i in range(count)])  18.1 us
    ppermute x4, starting transfers between devices, from_prev(): lax.ppermute(block, 'seq', [(i, (i + 1) % count) for i in range(count)])  16.9 us
    ppermute x5, waiting for transfers between devices, from_next(): lax.ppermute(block, 'seq', [((i + 1) % count, i) for i in range(count)])  12.7 us
    dot_general x3, matrix products, kernel_tile(): score = jnp.dot(left, right.T, preferred_element_type=jnp.float32)  4.03 us
  transfers between devices with their start and end apart: 9, of which 4 were waited for; matrix products, arithmetic and copies ran while one was open for 8% of the time, Pallas kernels for 0%

profile of v11, /device:TPU:14, one launch (start us, length us, event | category | flops | bytes accessed | tf_op | source)
XLA Modules:
  0.0 158.6 jit_solution(17816685394759255276)
XLA Ops:
  0.0 1.6 %fusion.2 = f32[512]{0:T(512)S(1)} fusion(bf16[1,1,512,1024]{3,2,1,0:T(8,128)(2,1)} %param.8), kind=kLoop, calls=%fused_computation.4 | loop fusion | flops 1572352 | bytes 1050624 | tf_op jit(solution)/shard_map/reduce_sum | solution.py:38
  1.6 0.3 convert_reduce_fusion
  2.0 2.5 %collective-permute-start = (bf16[256,1024]{1,0:T(8,128)(2,1)S(1)}, bf16[256,1024]{1,0:T(8,128)(2,1)}, u32[]{:S(2)}, u32[]{:S(2)}) collective-permute-start(bf16[256,1024]{1,0:T(8,128)(2,1)S(1)} %get-tuple-element.35), channel_id=1, source_target_pairs={{48,0},{96,48},{144,96},{192,144},{240,192},{288,240},{336,288},{3... | collective-permute-start | bytes 1572872 | tf_op jit(solution)/shard_map/ppermute | solution.py:22
  4.5 5.8 %collective-permute-start.1 = (bf16[256,1024]{1,0:T(8,128)(2,1)S(1)}, bf16[256,1024]{1,0:T(8,128)(2,1)}, u32[]{:S(2)}, u32[]{:S(2)}) collective-permute-start(bf16[256,1024]{1,0:T(8,128)(2,1)S(1)} %get-tuple-element.36), channel_id=1, source_target_pairs={{48,0},{96,48},{144,96},{192,144},{240,192},{288,240},{336,288},{3... | collective-permute-start | bytes 1572872 | tf_op jit(solution)/shard_map/ppermute | solution.py:22
  10.4 2.4 %collective-permute-start.2 = (bf16[512,128]{1,0:T(8,128)(2,1)S(1)}, bf16[512,128]{1,0:T(8,128)(2,1)S(1)}, u32[]{:S(2)}, u32[]{:S(2)}) collective-permute-start(bf16[512,128]{1,0:T(8,128)(2,1)S(1)} %convert_bitcast_fusion.1), channel_id=1, source_target_pairs={{48,0},{96,48},{144,96},{192,144},{240,192},{288,240},{336,288},{3... | collective-permute-start | bytes 393224 | tf_op jit(solution)/shard_map/ppermute | solution.py:22
  12.7 0.6 and_reduce_fusion
  13.4 0.6 multiply_reduce_fusion
  14.7 0.6 fusion.64
  15.4 0.6 slice.87
  16.7 1.9 %fusion.73 = f32[1,1]{1,0:T(1,128)} fusion(pred[1,1]{1,0:T(4,128)(4,1)} %bitcast.11, f32[1,1]{1,0:T(1,128)S(6)} %convert_element_type.101, s32[]{:T(128)} %bitcast.12, f32[1,12]{1,0:T(1,128)S(1)} %reshape.182), kind=kLoop, calls=%fused_computation.124 | loop fusion | flops 1 | bytes 61 | tf_op jit(solution)/shard_map/select.3
  18.6 1.3 scatter.9
  19.9 0.9 convert_reduce_fusion.2
  20.9 0.3 fusion.74
  21.3 1.5 convert_reduce_fusion.4
  22.8 0.3 fusion.75
  23.1 3.5 %collective-permute-start.3 = (f32[258,128]{1,0:T(8,128)S(1)}, f32[258,128]{1,0:T(8,128)S(1)}, u32[]{:S(2)}, u32[]{:S(2)}) collective-permute-start(f32[258,128]{1,0:T(8,128)S(1)} %pad_maximum_fusion.1), channel_id=1, source_target_pairs={{0,48},{48,96},{96,144},{144,192},{192,240},{240,288},{288,336},{3... | collective-permute-start | bytes 396296 | tf_op jit(solution)/shard_map/ppermute | solution.py:27
  26.6 3.6 %collective-permute-done.1 = bf16[256,1024]{1,0:T(8,128)(2,1)} collective-permute-done((bf16[256,1024]{1,0:T(8,128)(2,1)S(1)}, bf16[256,1024]{1,0:T(8,128)(2,1)}, u32[]{:S(2)}, u32[]{:S(2)}) %collective-permute-start.1) | collective-permute-done | bytes 524320 | tf_op jit(solution)/shard_map/ppermute | solution.py:22
  30.2 1.5 convert_reduce_fusion.3
  31.8 0.3 fusion.76
  32.1 4.8 %collective-permute-start.4 = (f32[258,128]{1,0:T(8,128)S(1)}, f32[258,128]{1,0:T(8,128)S(1)}, u32[]{:S(2)}, u32[]{:S(2)}) collective-permute-start(f32[258,128]{1,0:T(8,128)S(1)} %pad_maximum_fusion.2), channel_id=1, source_target_pairs={{0,48},{48,96},{96,144},{144,192},{192,240},{240,288},{288,336},{3... | collective-permute-start | bytes 396296 | tf_op jit(solution)/shard_map/ppermute | solution.py:27
  36.9 0.1 convert_reduce_fusion.1
  37.0 1.1 collective-permute-done.3
  38.2 1.7 %collective-permute-done.4 = f32[258,128]{1,0:T(8,128)S(1)} collective-permute-done((f32[258,128]{1,0:T(8,128)S(1)}, f32[258,128]{1,0:T(8,128)S(1)}, u32[]{:S(2)}, u32[]{:S(2)}) %collective-permute-start.4) | collective-permute-done | bytes 132128 | tf_op jit(solution)/shard_map/ppermute | solution.py:27
  39.9 1.0 bitcast_reduce_fusion.1
  41.0 33.8 %all-gather.4 = f32[12,41,128]{2,1,0:T(8,128)S(1)} all-gather(f32[1,41,128]{2,1,0:T(8,128)S(1)} %maximum_bitcast_fusion), channel_id=2, replica_groups=mesh['seq'=16,'grp_z'=12,'grp_y'=2,'grp_c'=2] {'grp_z'}, dimensions={0}, use_global_device_ids=true | all-gather | bytes 272896 | tf_op jit(solution)/shard_map/all_gather | solution.py:125
  74.8 12.7 %all-gather.1 = f32[24,41,128]{2,1,0:T(8,128)S(1)} all-gather(f32[12,41,128]{2,1,0:T(8,128)S(1)} %all-gather.4), channel_id=3, replica_groups=mesh['seq'=16,'grp_z'=12,'grp_y'=2,'grp_c'=2] {'grp_y'}, dimensions={0}, use_global_device_ids=true | all-gather | bytes 755712 | tf_op jit(solution)/shard_map/all_gather | solution.py:125
  87.5 2.6 %all-gather.2 = f32[4,12,41,128]{3,2,1,0:T(8,128)S(1)} all-gather(f32[2,12,41,128]{3,2,1,0:T(8,128)S(1)} %bitcast.120), channel_id=4, replica_groups=mesh['seq'=16,'grp_z'=12,'grp_y'=2,'grp_c'=2] {'grp_c'}, dimensions={0}, use_global_device_ids=true | all-gather | bytes 1511424 | tf_op jit(solution)/shard_map/all_gather | solution.py:125
  90.1 0.7 copy.33
  90.8 0.5 copy.34
  91.3 0.1 copy.37
  91.5 0.3 fusion.26
  91.9 0.5 fusion.38
  92.5 0.3 fusion.77
  92.9 0.3 fusion.70
  93.2 5.8 %collective-permute-start.6 = (f32[512,128]{1,0:T(8,128)S(1)}, f32[512,128]{1,0:T(8,128)S(1)}, u32[]{:S(2)}, u32[]{:S(2)}) collective-permute-start(f32[512,128]{1,0:T(8,128)S(1)} %fusion.70), channel_id=1, source_target_pairs={{0,48},{48,96},{96,144},{144,192},{192,240},{240,288},{288,336},{3... | collective-permute-start | bytes 786440 | tf_op jit(solution)/shard_map/ppermute | solution.py:27
  99.0 4.2 %collective-permute-start.5 = (bf16[512,128]{1,0:T(8,128)(2,1)S(1)}, bf16[512,128]{1,0:T(8,128)(2,1)S(1)}, u32[]{:S(2)}, u32[]{:S(2)}) collective-permute-start(bf16[512,128]{1,0:T(8,128)(2,1)S(1)} %fusion.45), channel_id=1, source_target_pairs={{48,0},{96,48},{144,96},{192,144},{240,192},{288,240},{336,288},{3... | collective-permute-start | bytes 393224 | tf_op jit(solution)/shard_map/ppermute | solution.py:22
  103.3 0.5 fusion.32
  104.0 9.1 %collective-permute-done.5 = bf16[512,128]{1,0:T(8,128)(2,1)S(1)} collective-permute-done((bf16[512,128]{1,0:T(8,128)(2,1)S(1)}, bf16[512,128]{1,0:T(8,128)(2,1)S(1)}, u32[]{:S(2)}, u32[]{:S(2)}) %collective-permute-start.5) | collective-permute-done | bytes 131104 | tf_op jit(solution)/shard_map/ppermute | solution.py:22
  113.1 0.3 bitcast_reduce_fusion
  113.5 0.3 fusion.69
  113.8 3.2 %collective-permute-start.7 = (bf16[512,128]{1,0:T(8,128)(2,1)S(1)}, bf16[512,128]{1,0:T(8,128)(2,1)S(1)}, u32[]{:S(2)}, u32[]{:S(2)}) collective-permute-start(bf16[512,128]{1,0:T(8,128)(2,1)S(1)} %fusion.42), channel_id=1, source_target_pairs={{48,0},{96,48},{144,96},{192,144},{240,192},{288,240},{336,288},{3... | collective-permute-start | bytes 393224 | tf_op jit(solution)/shard_map/ppermute | solution.py:22
  117.0 2.9 %collective-permute-start.8 = (f32[512,128]{1,0:T(8,128)S(1)}, f32[512,128]{1,0:T(8,128)S(1)}, u32[]{:S(2)}, u32[]{:S(2)}) collective-permute-start(f32[512,128]{1,0:T(8,128)S(1)} %fusion.69), channel_id=1, source_target_pairs={{0,48},{48,96},{96,144},{144,192},{192,240},{240,288},{288,336},{3... | collective-permute-start | bytes 786440 | tf_op jit(solution)/shard_map/ppermute | solution.py:27
  119.9 1.8 %all-gather.3 = f32[32,128]{1,0:T(8,128)S(1)} all-gather(f32[16,128]{1,0:T(8,128)S(1)} %broadcast_multiply_fusion), channel_id=5, replica_groups=mesh['seq'=16,'grp_z'=12,'grp_y'=2,'grp_c'=2] {'grp_c'}, dimensions={0}, use_global_device_ids=true | all-gather | bytes 24576 | tf_op jit(solution)/shard_map/all_gather | solution.py:32
  121.7 12.9 %all_gather.34 = f32[4,16,128]{2,1,0:T(8,128)S(1)} all-gather(f32[2,16,128]{2,1,0:T(8,128)S(1)} %bitcast.124), channel_id=1, replica_groups=mesh['seq'=16,'grp_z'=12,'grp_y'=2,'grp_c'=2] {'grp_y'}, dimensions={0}, use_global_device_ids=true | all-gather | bytes 49152 | tf_op jit(solution)/shard_map/all_gather | solution.py:32
  134.6 21.8 %all_gather.35 = f32[48,16,128]{2,1,0:T(8,128)S(1)} all-gather(f32[4,16,128]{2,1,0:T(8,128)S(1)} %all_gather.34), channel_id=1, replica_groups=mesh['seq'=16,'grp_z'=12,'grp_y'=2,'grp_c'=2] {'grp_z'}, dimensions={0}, use_global_device_ids=true | all-gather | bytes 425984 | tf_op jit(solution)/shard_map/all_gather | solution.py:32
  156.5 0.7 fusion.36
  157.1 0.3 fusion.78
  157.5 1.0 fusion.22
  (49 shorter events, 0.8 us)
Async XLA Ops:
  0.0 1.6 %copy-start = (bf16[1,1,512,1024]{3,2,1,0:T(8,128)(2,1)S(1)}, bf16[1,1,512,1024]{3,2,1,0:T(8,128)(2,1)}, u32[]{:S(2)}) copy-start(bf16[1,1,512,1024]{3,2,1,0:T(8,128)(2,1)} %param.8) | copy-start | bytes 3145732
  1.9 8.4 %copy-start.1 = (bf16[512,1024]{1,0:T(8,128)(2,1)}, bf16[512,1024]{1,0:T(8,128)(2,1)S(1)}, u32[]{:S(2)}) copy-start(bf16[512,1024]{1,0:T(8,128)(2,1)S(1)} %get-tuple-element.34) | copy-start | bytes 3145732
  1.9 8.4 %copy-start.3 = (f32[1,1,512,128]{3,2,1,0:T(8,128)S(1)}, f32[1,1,512,128]{3,2,1,0:T(8,128)}, u32[]{:S(2)}) copy-start(f32[1,1,512,128]{3,2,1,0:T(8,128)} %param.9) | copy-start | bytes 786436
  2.0 12.7 %copy-start.5 = (s32[1,1,3,4]{3,1,2,0:T(1,128)S(1)}, s32[1,1,3,4]{3,1,2,0:T(1,128)}, u32[]{:S(2)}) copy-start(s32[1,1,3,4]{3,1,2,0:T(1,128)} %param.10) | copy-start | bytes 148
  2.0 19.2 %collective-permute-start = (bf16[256,1024]{1,0:T(8,128)(2,1)S(1)}, bf16[256,1024]{1,0:T(8,128)(2,1)}, u32[]{:S(2)}, u32[]{:S(2)}) collective-permute-start(bf16[256,1024]{1,0:T(8,128)(2,1)S(1)} %get-tuple-element.35), channel_id=1, source_target_pairs={{48,0},{96,48},{144,96},{192,144},{240,192},{288,240},{336,288},{3... | collective-permute-start | bytes 1572872 | tf_op jit(solution)/shard_map/ppermute | solution.py:22
  4.5 25.7 %collective-permute-start.1 = (bf16[256,1024]{1,0:T(8,128)(2,1)S(1)}, bf16[256,1024]{1,0:T(8,128)(2,1)}, u32[]{:S(2)}, u32[]{:S(2)}) collective-permute-start(bf16[256,1024]{1,0:T(8,128)(2,1)S(1)} %get-tuple-element.36), channel_id=1, source_target_pairs={{48,0},{96,48},{144,96},{192,144},{240,192},{288,240},{336,288},{3... | collective-permute-start | bytes 1572872 | tf_op jit(solution)/shard_map/ppermute | solution.py:22
  10.4 29.6 %collective-permute-start.2 = (bf16[512,128]{1,0:T(8,128)(2,1)S(1)}, bf16[512,128]{1,0:T(8,128)(2,1)S(1)}, u32[]{:S(2)}, u32[]{:S(2)}) collective-permute-start(bf16[512,128]{1,0:T(8,128)(2,1)S(1)} %convert_bitcast_fusion.1), channel_id=1, source_target_pairs={{48,0},{96,48},{144,96},{192,144},{240,192},{288,240},{336,288},{3... | collective-permute-start | bytes 393224 | tf_op jit(solution)/shard_map/ppermute | solution.py:22
  19.9 1.3 copy-start.2
  23.1 15.1 %collective-permute-start.3 = (f32[258,128]{1,0:T(8,128)S(1)}, f32[258,128]{1,0:T(8,128)S(1)}, u32[]{:S(2)}, u32[]{:S(2)}) collective-permute-start(f32[258,128]{1,0:T(8,128)S(1)} %pad_maximum_fusion.1), channel_id=1, source_target_pairs={{0,48},{48,96},{96,144},{144,192},{192,240},{240,288},{288,336},{3... | collective-permute-start | bytes 396296 | tf_op jit(solution)/shard_map/ppermute | solution.py:27
  32.1 7.8 %collective-permute-start.4 = (f32[258,128]{1,0:T(8,128)S(1)}, f32[258,128]{1,0:T(8,128)S(1)}, u32[]{:S(2)}, u32[]{:S(2)}) collective-permute-start(f32[258,128]{1,0:T(8,128)S(1)} %pad_maximum_fusion.2), channel_id=1, source_target_pairs={{0,48},{48,96},{96,144},{144,192},{192,240},{240,288},{288,336},{3... | collective-permute-start | bytes 396296 | tf_op jit(solution)/shard_map/ppermute | solution.py:27
  91.3 1.1 copy-start.4
  93.2 19.9 %collective-permute-start.6 = (f32[512,128]{1,0:T(8,128)S(1)}, f32[512,128]{1,0:T(8,128)S(1)}, u32[]{:S(2)}, u32[]{:S(2)}) collective-permute-start(f32[512,128]{1,0:T(8,128)S(1)} %fusion.70), channel_id=1, source_target_pairs={{0,48},{48,96},{96,144},{144,192},{192,240},{240,288},{288,336},{3... | collective-permute-start | bytes 786440 | tf_op jit(solution)/shard_map/ppermute | solution.py:27
  99.0 14.1 %collective-permute-start.5 = (bf16[512,128]{1,0:T(8,128)(2,1)S(1)}, bf16[512,128]{1,0:T(8,128)(2,1)S(1)}, u32[]{:S(2)}, u32[]{:S(2)}) collective-permute-start(bf16[512,128]{1,0:T(8,128)(2,1)S(1)} %fusion.45), channel_id=1, source_target_pairs={{48,0},{96,48},{144,96},{192,144},{240,192},{288,240},{336,288},{3... | collective-permute-start | bytes 393224 | tf_op jit(solution)/shard_map/ppermute | solution.py:22
  113.8 43.7 %collective-permute-start.7 = (bf16[512,128]{1,0:T(8,128)(2,1)S(1)}, bf16[512,128]{1,0:T(8,128)(2,1)S(1)}, u32[]{:S(2)}, u32[]{:S(2)}) collective-permute-start(bf16[512,128]{1,0:T(8,128)(2,1)S(1)} %fusion.42), channel_id=1, source_target_pairs={{48,0},{96,48},{144,96},{192,144},{240,192},{288,240},{336,288},{3... | collective-permute-start | bytes 393224 | tf_op jit(solution)/shard_map/ppermute | solution.py:22
  117.0 40.5 %collective-permute-start.8 = (f32[512,128]{1,0:T(8,128)S(1)}, f32[512,128]{1,0:T(8,128)S(1)}, u32[]{:S(2)}, u32[]{:S(2)}) collective-permute-start(f32[512,128]{1,0:T(8,128)S(1)} %fusion.69), channel_id=1, source_target_pairs={{0,48},{48,96},{96,144},{144,192},{192,240},{240,288},{288,336},{3... | collective-permute-start | bytes 786440 | tf_op jit(solution)/shard_map/ppermute | solution.py:27

commit v12 on v9

--- a/solution.py
+++ b/solution.py
@@ -74,7 +74,9 @@
             row_count, classes
         )
 
-    after_unit = from_next(unit_emb)
+    seed_bf = seed.astype(jnp.bfloat16)
+    arrived = from_next(jnp.concatenate([unit_emb, seed_bf], axis=1))
+    after_unit, seed_ahead = arrived[:, :width], arrived[:, width:]
     next_tile = kernel_tile(unit_emb, after_unit, False)
     next_rows = jnp.sum(next_tile, axis=1, dtype=jnp.float32)
     next_cols = jnp.sum(next_tile, axis=0, dtype=jnp.float32)
@@ -85,7 +87,7 @@
             next_tile, label_bf, (((0,), (0,)), ((), ())), preferred_element_type=jnp.float32
         )
         if first:
-            ahead = from_next(label_bf)
+            ahead = seed_ahead
             packet = from_prev(jnp.concatenate([back, next_cols.reshape(col_rows, classes)]))
             back_in = packet[:row_count]
             degree = self_rows + next_rows + packet[row_count:].reshape(row_count)

time: 159 us -> 165 us (1.038)
  the two profiles are of different devices: /device:TPU:14 before, /device:TPU:30 now
where the time goes in v12:
time: 165 us; the launch traced here: 164 us
  blocking collectives  82.3 us (50%)
  waiting for transfers between devices  37.7 us (23%)
  starting transfers between devices  21.5 us (13%)
  matrix products  9.7 us (6%)
  other arithmetic  7.22 us (4%)
  local copies, waits for them, and re-layouts  4.04 us (2%)
  between operations  1.72 us (1%)
    all_gather x3, blocking collectives, body(): table_a = lax.all_gather(table_a, axis, axis=0, tiled=False)  50.4 us
    ppermute x3, waiting for transfers between devices, from_next(): lax.ppermute(block, 'seq', [((i + 1) % count, i) for i in range(count)])  36.4 us
    all_gather x3, blocking collectives, gather_groups(): value = lax.all_gather(value, axis, axis=0, tiled=True)  31.9 us
    ppermute x3, starting transfers between devices, from_prev(): lax.ppermute(block, 'seq', [(i, (i + 1) % count) for i in range(count)])  15.2 us
    ppermute x3, starting transfers between devices, from_next(): lax.ppermute(block, 'seq', [((i + 1) % count, i) for i in range(count)])  6.3 us
  transfers between devices with their start and end apart: 6, of which 3 were waited for; matrix products, arithmetic and copies ran while one was open for 5% of the time, Pallas kernels for 0%

profile of v12, /device:TPU:30, one launch (start us, length us, event | category | flops | bytes accessed | tf_op | source)
XLA Modules:
  0.0 164.2 jit_solution(1009249537580255028)
XLA Ops:
  0.0 1.6 fusion.2
  1.6 0.3 convert_reduce_fusion
  1.9 0.6 copy-done
  2.6 1.1 pad_maximum_fusion
  3.7 2.3 %collective-permute-start = (bf16[512,1152]{1,0:T(8,128)(2,1)}, bf16[512,1152]{1,0:T(8,128)(2,1)}, u32[]{:S(2)}, u32[]{:S(2)}) collective-permute-start(bf16[512,1152]{1,0:T(8,128)(2,1)} %pad_maximum_fusion), channel_id=1, source_target_pairs={{48,0},{96,48},{144,96},{192,144},{240,192},{288,240},{336,288},{3... | collective-permute-start | bytes 3538952 | tf_op jit(solution)/shard_map/ppermute | solution.py:22
  6.1 0.6 multiply_reduce_fusion
  7.4 0.6 and_reduce_fusion
  8.0 0.6 fusion.64
  8.6 0.9 convert_reduce_fusion.3
  9.5 28.0 %collective-permute-done = bf16[512,1152]{1,0:T(8,128)(2,1)} collective-permute-done((bf16[512,1152]{1,0:T(8,128)(2,1)}, bf16[512,1152]{1,0:T(8,128)(2,1)}, u32[]{:S(2)}, u32[]{:S(2)}) %collective-permute-start) | collective-permute-done | bytes 1179680 | tf_op jit(solution)/shard_map/ppermute | solution.py:22
  37.5 2.1 %convert_reduce_fusion.1 = (f32[512]{0:T(512)S(1)}, f32[512]{0:T(512)S(1)}, bf16[512,512]{0,1:T(8,128)(2,1)S(1)}) fusion(bf16[512,1024]{1,0:T(8,128)(2,1)S(1)} %get-tuple-element.36, bf16[512,1152]{1,0:T(8,128)(2,1)} %collective-permute-done), kind=kOutput, calls=%fused_computation.15 | convolution fusion | flops 538442752 | bytes 2625536 | tf_op jit(solution)/shard_map/dot_general | solution.py:44
  39.7 0.3 fusion.72
  40.0 1.9 %collective-permute-start.1 = (f32[516,128]{1,0:T(8,128)S(1)}, f32[516,128]{1,0:T(8,128)S(1)}, u32[]{:S(2)}, u32[]{:S(2)}) collective-permute-start(f32[516,128]{1,0:T(8,128)S(1)} %pad_maximum_fusion.1), channel_id=1, source_target_pairs={{0,48},{48,96},{96,144},{144,192},{192,240},{240,288},{288,336},{3... | collective-permute-start | bytes 792584 | tf_op jit(solution)/shard_map/ppermute | solution.py:27
  41.9 0.1 reshape.168
  42.0 0.6 slice.79
  43.4 1.9 %fusion.70 = f32[1,1]{1,0:T(1,128)} fusion(pred[1,1]{1,0:T(4,128)(4,1)} %bitcast.9, f32[1,1]{1,0:T(1,128)S(6)} %convert_element_type.91, s32[]{:T(128)} %bitcast.10, f32[1,12]{1,0:T(1,128)S(1)} %reshape.168), kind=kLoop, calls=%fused_computation.116 | loop fusion | flops 1 | bytes 61 | tf_op jit(solution)/shard_map/select.3
  45.3 1.3 scatter.9
  46.6 0.3 fusion.71
  46.9 1.4 collective-permute-done.1
  48.3 1.2 bitcast_reduce_fusion.1
  49.6 34.9 %all-gather.4 = f32[12,41,128]{2,1,0:T(8,128)S(1)} all-gather(f32[1,41,128]{2,1,0:T(8,128)S(1)} %maximum_bitcast_fusion), channel_id=2, replica_groups=mesh['seq'=16,'grp_z'=12,'grp_y'=2,'grp_c'=2] {'grp_z'}, dimensions={0}, use_global_device_ids=true | all-gather | bytes 272896 | tf_op jit(solution)/shard_map/all_gather | solution.py:118
  84.5 12.9 %all-gather.1 = f32[24,41,128]{2,1,0:T(8,128)S(1)} all-gather(f32[12,41,128]{2,1,0:T(8,128)S(1)} %all-gather.4), channel_id=3, replica_groups=mesh['seq'=16,'grp_z'=12,'grp_y'=2,'grp_c'=2] {'grp_y'}, dimensions={0}, use_global_device_ids=true | all-gather | bytes 755712 | tf_op jit(solution)/shard_map/all_gather | solution.py:118
  97.4 2.6 %all-gather.2 = f32[4,12,41,128]{3,2,1,0:T(8,128)S(1)} all-gather(f32[2,12,41,128]{3,2,1,0:T(8,128)S(1)} %bitcast.118), channel_id=4, replica_groups=mesh['seq'=16,'grp_z'=12,'grp_y'=2,'grp_c'=2] {'grp_c'}, dimensions={0}, use_global_device_ids=true | all-gather | bytes 1511424 | tf_op jit(solution)/shard_map/all_gather | solution.py:118
  100.0 0.7 copy.39
  100.7 0.5 copy.40
  101.2 0.1 copy.44
  101.3 0.3 fusion.23
  101.7 0.1 convert_reduce_fusion.6
  101.8 0.5 fusion.36
  102.3 0.1 fusion.43
  102.4 0.3 fusion.73
  102.7 0.3 fusion.74
  103.0 5.6 %collective-permute-start.3 = (f32[512,128]{1,0:T(8,128)S(1)}, f32[512,128]{1,0:T(8,128)S(1)}, u32[]{:S(2)}, u32[]{:S(2)}) collective-permute-start(f32[512,128]{1,0:T(8,128)S(1)} %fusion.74), channel_id=1, source_target_pairs={{0,48},{48,96},{96,144},{144,192},{192,240},{240,288},{288,336},{3... | collective-permute-start | bytes 786440 | tf_op jit(solution)/shard_map/ppermute | solution.py:27
  108.6 1.9 %collective-permute-start.2 = (bf16[512,128]{1,0:T(8,128)(2,1)S(1)}, bf16[512,128]{1,0:T(8,128)(2,1)S(1)}, u32[]{:S(2)}, u32[]{:S(2)}) collective-permute-start(bf16[512,128]{1,0:T(8,128)(2,1)S(1)} %fusion.43), channel_id=1, source_target_pairs={{48,0},{96,48},{144,96},{192,144},{240,192},{288,240},{336,288},{3... | collective-permute-start | bytes 393224 | tf_op jit(solution)/shard_map/ppermute | solution.py:22
  110.5 0.1 convert_reduce_fusion.5
  110.6 0.6 fusion.30
  111.2 0.1 convert_reduce_fusion.4
  111.3 8.4 %collective-permute-done.2 = bf16[512,128]{1,0:T(8,128)(2,1)S(1)} collective-permute-done((bf16[512,128]{1,0:T(8,128)(2,1)S(1)}, bf16[512,128]{1,0:T(8,128)(2,1)S(1)}, u32[]{:S(2)}, u32[]{:S(2)}) %collective-permute-start.2) | collective-permute-done | bytes 131104 | tf_op jit(solution)/shard_map/ppermute | solution.py:22
  119.7 0.4 bitcast_reduce_fusion
  120.1 0.3 fusion.76
  120.4 2.0 %collective-permute-start.4 = (bf16[512,128]{1,0:T(8,128)(2,1)S(1)}, bf16[512,128]{1,0:T(8,128)(2,1)S(1)}, u32[]{:S(2)}, u32[]{:S(2)}) collective-permute-start(bf16[512,128]{1,0:T(8,128)(2,1)S(1)} %fusion.40), channel_id=1, source_target_pairs={{48,0},{96,48},{144,96},{192,144},{240,192},{288,240},{336,288},{3... | collective-permute-start | bytes 393224 | tf_op jit(solution)/shard_map/ppermute | solution.py:22
  122.4 7.7 %collective-permute-start.5 = (f32[512,128]{1,0:T(8,128)S(1)}, f32[512,128]{1,0:T(8,128)S(1)}, u32[]{:S(2)}, u32[]{:S(2)}) collective-permute-start(f32[512,128]{1,0:T(8,128)S(1)} %fusion.76), channel_id=1, source_target_pairs={{0,48},{48,96},{96,144},{144,192},{192,240},{240,288},{288,336},{3... | collective-permute-start | bytes 786440 | tf_op jit(solution)/shard_map/ppermute | solution.py:27
  130.2 1.8 %all-gather.3 = f32[32,128]{1,0:T(8,128)S(1)} all-gather(f32[16,128]{1,0:T(8,128)S(1)} %broadcast_multiply_fusion), channel_id=5, replica_groups=mesh['seq'=16,'grp_z'=12,'grp_y'=2,'grp_c'=2] {'grp_c'}, dimensions={0}, use_global_device_ids=true | all-gather | bytes 24576 | tf_op jit(solution)/shard_map/all_gather | solution.py:32
  132.0 8.3 %all_gather.34 = f32[4,16,128]{2,1,0:T(8,128)S(1)} all-gather(f32[2,16,128]{2,1,0:T(8,128)S(1)} %bitcast.122), channel_id=1, replica_groups=mesh['seq'=16,'grp_z'=12,'grp_y'=2,'grp_c'=2] {'grp_y'}, dimensions={0}, use_global_device_ids=true | all-gather | bytes 49152 | tf_op jit(solution)/shard_map/all_gather | solution.py:32
  140.3 21.7 %all_gather.35 = f32[48,16,128]{2,1,0:T(8,128)S(1)} all-gather(f32[4,16,128]{2,1,0:T(8,128)S(1)} %all_gather.34), channel_id=1, replica_groups=mesh['seq'=16,'grp_z'=12,'grp_y'=2,'grp_c'=2] {'grp_z'}, dimensions={0}, use_global_device_ids=true | all-gather | bytes 425984 | tf_op jit(solution)/shard_map/all_gather | solution.py:32
  162.0 0.7 fusion.34
  162.7 0.3 fusion.75
  163.1 1.1 fusion.19
  (29 shorter events, 0.3 us)
Async XLA Ops:
  0.0 1.6 copy-start.1
  1.6 1.0 copy-start
  2.6 5.4 %copy-start.2 = (s32[1,1,3,4]{3,1,2,0:T(1,128)S(1)}, s32[1,1,3,4]{3,1,2,0:T(1,128)}, u32[]{:S(2)}) copy-start(s32[1,1,3,4]{3,1,2,0:T(1,128)} %param.10) | copy-start | bytes 148
  3.7 33.8 %collective-permute-start = (bf16[512,1152]{1,0:T(8,128)(2,1)}, bf16[512,1152]{1,0:T(8,128)(2,1)}, u32[]{:S(2)}, u32[]{:S(2)}) collective-permute-start(bf16[512,1152]{1,0:T(8,128)(2,1)} %pad_maximum_fusion), channel_id=1, source_target_pairs={{48,0},{96,48},{144,96},{192,144},{240,192},{288,240},{336,288},{3... | collective-permute-start | bytes 3538952 | tf_op jit(solution)/shard_map/ppermute | solution.py:22
  40.0 8.3 %collective-permute-start.1 = (f32[516,128]{1,0:T(8,128)S(1)}, f32[516,128]{1,0:T(8,128)S(1)}, u32[]{:S(2)}, u32[]{:S(2)}) collective-permute-start(f32[516,128]{1,0:T(8,128)S(1)} %pad_maximum_fusion.1), channel_id=1, source_target_pairs={{0,48},{48,96},{96,144},{144,192},{192,240},{240,288},{288,336},{3... | collective-permute-start | bytes 792584 | tf_op jit(solution)/shard_map/ppermute | solution.py:27
  103.0 16.6 %collective-permute-start.3 = (f32[512,128]{1,0:T(8,128)S(1)}, f32[512,128]{1,0:T(8,128)S(1)}, u32[]{:S(2)}, u32[]{:S(2)}) collective-permute-start(f32[512,128]{1,0:T(8,128)S(1)} %fusion.74), channel_id=1, source_target_pairs={{0,48},{48,96},{96,144},{144,192},{192,240},{240,288},{288,336},{3... | collective-permute-start | bytes 786440 | tf_op jit(solution)/shard_map/ppermute | solution.py:27
  108.6 11.1 %collective-permute-start.2 = (bf16[512,128]{1,0:T(8,128)(2,1)S(1)}, bf16[512,128]{1,0:T(8,128)(2,1)S(1)}, u32[]{:S(2)}, u32[]{:S(2)}) collective-permute-start(bf16[512,128]{1,0:T(8,128)(2,1)S(1)} %fusion.43), channel_id=1, source_target_pairs={{48,0},{96,48},{144,96},{192,144},{240,192},{288,240},{336,288},{3... | collective-permute-start | bytes 393224 | tf_op jit(solution)/shard_map/ppermute | solution.py:22
  120.4 42.7 %collective-permute-start.4 = (bf16[512,128]{1,0:T(8,128)(2,1)S(1)}, bf16[512,128]{1,0:T(8,128)(2,1)S(1)}, u32[]{:S(2)}, u32[]{:S(2)}) collective-permute-start(bf16[512,128]{1,0:T(8,128)(2,1)S(1)} %fusion.40), channel_id=1, source_target_pairs={{48,0},{96,48},{144,96},{192,144},{240,192},{288,240},{336,288},{3... | collective-permute-start | bytes 393224 | tf_op jit(solution)/shard_map/ppermute | solution.py:22
  122.4 40.7 %collective-permute-start.5 = (f32[512,128]{1,0:T(8,128)S(1)}, f32[512,128]{1,0:T(8,128)S(1)}, u32[]{:S(2)}, u32[]{:S(2)}) collective-permute-start(f32[512,128]{1,0:T(8,128)S(1)} %fusion.76), channel_id=1, source_target_pairs={{0,48},{48,96},{96,144},{144,192},{192,240},{240,288},{288,336},{3... | collective-permute-start | bytes 786440 | tf_op jit(solution)/shard_map/ppermute | solution.py:27

commit v13 on v9

--- a/solution.py
+++ b/solution.py
@@ -79,8 +79,10 @@
     next_rows = jnp.sum(next_tile, axis=1, dtype=jnp.float32)
     next_cols = jnp.sum(next_tile, axis=0, dtype=jnp.float32)
 
-    def spread_of(labels, first, product_first=False):
+    def spread_of(labels, first, product_first=False, after=None):
         label_bf = labels.astype(jnp.bfloat16)
+        if after is not None:
+            label_bf, after = lax.optimization_barrier((label_bf, after))
         back = lax.dot_general(
             next_tile, label_bf, (((0,), (0,)), ((), ())), preferred_element_type=jnp.float32
         )
@@ -147,7 +149,7 @@
     spread_means = gather_groups(summarize(spread)[None])
     far_2 = far_all(2, next_summary(spread_means, far_1))
 
-    local, _ = spread_of(labels, False)
+    local, _ = spread_of(labels, False, after=spread_means)
     spread = local / degree[:, None]
     labels = keep_share * seed + (1.0 - keep_share) * (spread + rows_of(own(far_2)))
     return labels[None, None]

time: 159 us -> 168 us (1.057)
  the two profiles are of different devices: /device:TPU:14 before, /device:TPU:64 now
where the time goes in v13:
time: 168 us; the launch traced here: 167 us
  blocking collectives  80.6 us (48%)
  waiting for transfers between devices  36.9 us (22%)
  starting transfers between devices  29.5 us (18%)
  matrix products  8.82 us (5%)
  other arithmetic  6.34 us (4%)
  local copies, waits for them, and re-layouts  3.47 us (2%)
  between operations  1.72 us (1%)
    all_gather x3, blocking collectives, body(): table_a = lax.all_gather(table_a, axis, axis=0, tiled=False)  46.2 us
    all_gather x3, blocking collectives, gather_groups(): value = lax.all_gather(value, axis, axis=0, tiled=True)  34.4 us
    ppermute x4, starting transfers between devices, from_next(): lax.ppermute(block, 'seq', [((i + 1) % count, i) for i in range(count)])  23.7 us
    ppermute x4, waiting for transfers between devices, from_next(): lax.ppermute(block, 'seq', [((i + 1) % count, i) for i in range(count)])  21.2 us
    ppermute x3, waiting for transfers between devices, from_prev(): lax.ppermute(block, 'seq', [(i, (i + 1) % count) for i in range(count)])  15.7 us
    ppermute x3, starting transfers between devices, from_prev(): lax.ppermute(block, 'seq', [(i, (i + 1) % count) for i in range(count)])  5.76 us
  transfers between devices with their start and end apart: 7, of which 5 were waited for; matrix products, arithmetic and copies ran while one was open for 7% of the time, Pallas kernels for 0%

profile of v13, /device:TPU:64, one launch (start us, length us, event | category | flops | bytes accessed | tf_op | source)
XLA Modules:
  0.0 167.3 jit_solution(5268924689193856548)
XLA Ops:
  0.0 1.6 fusion.2
  1.6 0.3 convert_reduce_fusion
  2.0 7.7 %collective-permute-start = (bf16[512,1024]{1,0:T(8,128)(2,1)S(1)}, bf16[512,1024]{1,0:T(8,128)(2,1)}, u32[]{:S(2)}, u32[]{:S(2)}) collective-permute-start(bf16[512,1024]{1,0:T(8,128)(2,1)S(1)} %get-tuple-element.38), channel_id=1, source_target_pairs={{48,0},{96,48},{144,96},{192,144},{240,192},{288,240},{336,288},{3... | collective-permute-start | bytes 3145736 | tf_op jit(solution)/shard_map/ppermute | solution.py:22
  9.7 2.4 %collective-permute-start.1 = (bf16[512,128]{1,0:T(8,128)(2,1)S(1)}, bf16[512,128]{1,0:T(8,128)(2,1)S(1)}, u32[]{:S(2)}, u32[]{:S(2)}) collective-permute-start(bf16[512,128]{1,0:T(8,128)(2,1)S(1)} %convert_bitcast_fusion.1), channel_id=1, source_target_pairs={{48,0},{96,48},{144,96},{192,144},{240,192},{288,240},{336,288},{3... | collective-permute-start | bytes 393224 | tf_op jit(solution)/shard_map/ppermute | solution.py:22
  12.1 0.6 multiply_reduce_fusion
  13.4 0.7 and_reduce_fusion
  14.1 0.7 fusion.62
  14.8 0.9 convert_reduce_fusion.3
  15.7 17.5 %collective-permute-done = bf16[512,1024]{1,0:T(8,128)(2,1)} collective-permute-done((bf16[512,1024]{1,0:T(8,128)(2,1)S(1)}, bf16[512,1024]{1,0:T(8,128)(2,1)}, u32[]{:S(2)}, u32[]{:S(2)}) %collective-permute-start) | collective-permute-done | bytes 1048608 | tf_op jit(solution)/shard_map/ppermute | solution.py:22
  33.2 2.1 %convert_reduce_fusion.1 = (f32[512]{0:T(512)S(1)}, f32[512]{0:T(512)S(1)}, bf16[512,512]{0,1:T(8,128)(2,1)S(1)}) fusion(bf16[512,1024]{1,0:T(8,128)(2,1)S(1)} %get-tuple-element.38, bf16[512,1024]{1,0:T(8,128)(2,1)} %collective-permute-done), kind=kOutput, calls=%fused_computation.15 | convolution fusion | flops 538442752 | bytes 2625536 | tf_op jit(solution)/shard_map/dot_general | solution.py:44
  35.3 0.3 fusion.70
  35.7 1.9 %collective-permute-start.2 = (f32[516,128]{1,0:T(8,128)S(1)}, f32[516,128]{1,0:T(8,128)S(1)}, u32[]{:S(2)}, u32[]{:S(2)}) collective-permute-start(f32[516,128]{1,0:T(8,128)S(1)} %pad_maximum_fusion), channel_id=1, source_target_pairs={{0,48},{48,96},{96,144},{144,192},{192,240},{240,288},{288,336},{3... | collective-permute-start | bytes 792584 | tf_op jit(solution)/shard_map/ppermute | solution.py:27
  37.6 0.1 reshape.168
  37.7 0.7 slice.71
  39.1 1.9 %fusion.68 = f32[1,1]{1,0:T(1,128)} fusion(pred[1,1]{1,0:T(4,128)(4,1)} %bitcast.9, f32[1,1]{1,0:T(1,128)S(6)} %convert_element_type.90, s32[]{:T(128)} %bitcast.10, f32[1,12]{1,0:T(1,128)S(1)} %reshape.168), kind=kLoop, calls=%fused_computation.113 | loop fusion | flops 1 | bytes 61 | tf_op jit(solution)/shard_map/select.3
  41.0 1.4 scatter.9
  42.4 0.3 fusion.69
  42.7 5.8 %collective-permute-done.2 = f32[516,128]{1,0:T(8,128)S(1)} collective-permute-done((f32[516,128]{1,0:T(8,128)S(1)}, f32[516,128]{1,0:T(8,128)S(1)}, u32[]{:S(2)}, u32[]{:S(2)}) %collective-permute-start.2) | collective-permute-done | bytes 264224 | tf_op jit(solution)/shard_map/ppermute | solution.py:27
  48.5 0.3 bitcast_reduce_fusion.1
  48.9 30.9 %all-gather.4 = f32[12,41,128]{2,1,0:T(8,128)S(1)} all-gather(f32[1,41,128]{2,1,0:T(8,128)S(1)} %maximum_bitcast_fusion), channel_id=2, replica_groups=mesh['seq'=16,'grp_z'=12,'grp_y'=2,'grp_c'=2] {'grp_z'}, dimensions={0}, use_global_device_ids=true | all-gather | bytes 272896 | tf_op jit(solution)/shard_map/all_gather | solution.py:118
  79.7 12.7 %all-gather.1 = f32[24,41,128]{2,1,0:T(8,128)S(1)} all-gather(f32[12,41,128]{2,1,0:T(8,128)S(1)} %all-gather.4), channel_id=3, replica_groups=mesh['seq'=16,'grp_z'=12,'grp_y'=2,'grp_c'=2] {'grp_y'}, dimensions={0}, use_global_device_ids=true | all-gather | bytes 755712 | tf_op jit(solution)/shard_map/all_gather | solution.py:118
  92.4 2.6 %all-gather.2 = f32[4,12,41,128]{3,2,1,0:T(8,128)S(1)} all-gather(f32[2,12,41,128]{3,2,1,0:T(8,128)S(1)} %bitcast.120), channel_id=4, replica_groups=mesh['seq'=16,'grp_z'=12,'grp_y'=2,'grp_c'=2] {'grp_c'}, dimensions={0}, use_global_device_ids=true | all-gather | bytes 1511424 | tf_op jit(solution)/shard_map/all_gather | solution.py:118
  95.1 0.7 copy.39
  95.7 0.5 copy.40
  96.2 0.1 copy.44
  96.4 0.3 fusion.23
  96.7 0.1 convert_reduce_fusion.6
  96.8 0.5 fusion.35
  97.4 0.3 fusion.71
  97.8 0.3 fusion.72
  98.1 1.9 %collective-permute-start.4 = (f32[512,128]{1,0:T(8,128)S(1)}, f32[512,128]{1,0:T(8,128)S(1)}, u32[]{:S(2)}, u32[]{:S(2)}) collective-permute-start(f32[512,128]{1,0:T(8,128)S(1)} %fusion.72), channel_id=1, source_target_pairs={{0,48},{48,96},{96,144},{144,192},{192,240},{240,288},{288,336},{3... | collective-permute-start | bytes 786440 | tf_op jit(solution)/shard_map/ppermute | solution.py:27
  100.0 7.8 %collective-permute-start.3 = (bf16[512,128]{1,0:T(8,128)(2,1)S(1)}, bf16[512,128]{1,0:T(8,128)(2,1)S(1)}, u32[]{:S(2)}, u32[]{:S(2)}) collective-permute-start(bf16[512,128]{1,0:T(8,128)(2,1)S(1)} %fusion.42), channel_id=1, source_target_pairs={{48,0},{96,48},{144,96},{192,144},{240,192},{288,240},{336,288},{3... | collective-permute-start | bytes 393224 | tf_op jit(solution)/shard_map/ppermute | solution.py:22
  107.8 0.1 convert_reduce_fusion.5
  107.9 0.6 fusion.29
  108.5 0.1 convert_reduce_fusion.4
  108.6 3.7 %collective-permute-done.3 = bf16[512,128]{1,0:T(8,128)(2,1)S(1)} collective-permute-done((bf16[512,128]{1,0:T(8,128)(2,1)S(1)}, bf16[512,128]{1,0:T(8,128)(2,1)S(1)}, u32[]{:S(2)}, u32[]{:S(2)}) %collective-permute-start.3) | collective-permute-done | bytes 131104 | tf_op jit(solution)/shard_map/ppermute | solution.py:22
  112.3 0.7 collective-permute-done.4
  113.1 0.4 bitcast_reduce_fusion
  113.4 1.8 %all-gather.3 = f32[32,128]{1,0:T(8,128)S(1)} all-gather(f32[16,128]{1,0:T(8,128)S(1)} %broadcast_multiply_fusion), channel_id=5, replica_groups=mesh['seq'=16,'grp_z'=12,'grp_y'=2,'grp_c'=2] {'grp_c'}, dimensions={0}, use_global_device_ids=true | all-gather | bytes 24576 | tf_op jit(solution)/shard_map/all_gather | solution.py:32
  115.3 8.3 %all_gather.34 = f32[4,16,128]{2,1,0:T(8,128)S(1)} all-gather(f32[2,16,128]{2,1,0:T(8,128)S(1)} %bitcast.124), channel_id=1, replica_groups=mesh['seq'=16,'grp_z'=12,'grp_y'=2,'grp_c'=2] {'grp_y'}, dimensions={0}, use_global_device_ids=true | all-gather | bytes 49152 | tf_op jit(solution)/shard_map/all_gather | solution.py:32
  123.6 24.3 %all_gather.35 = f32[48,16,128]{2,1,0:T(8,128)S(1)} all-gather(f32[4,16,128]{2,1,0:T(8,128)S(1)} %all_gather.34), channel_id=1, replica_groups=mesh['seq'=16,'grp_z'=12,'grp_y'=2,'grp_c'=2] {'grp_z'}, dimensions={0}, use_global_device_ids=true | all-gather | bytes 425984 | tf_op jit(solution)/shard_map/all_gather | solution.py:32
  147.9 0.3 fusion.74
  148.2 5.8 %collective-permute-start.5 = (bf16[512,128]{1,0:T(8,128)(2,1)S(1)}, bf16[512,128]{1,0:T(8,128)(2,1)S(1)}, u32[]{:S(2)}, u32[]{:S(2)}) collective-permute-start(bf16[512,128]{1,0:T(8,128)(2,1)S(1)} %fusion.39), channel_id=1, source_target_pairs={{48,0},{96,48},{144,96},{192,144},{240,192},{288,240},{336,288},{3... | collective-permute-start | bytes 393224 | tf_op jit(solution)/shard_map/ppermute | solution.py:22
  154.0 1.9 %collective-permute-start.6 = (f32[512,128]{1,0:T(8,128)S(1)}, f32[512,128]{1,0:T(8,128)S(1)}, u32[]{:S(2)}, u32[]{:S(2)}) collective-permute-start(f32[512,128]{1,0:T(8,128)S(1)} %fusion.74), channel_id=1, source_target_pairs={{0,48},{48,96},{96,144},{144,192},{192,240},{240,288},{288,336},{3... | collective-permute-start | bytes 786440 | tf_op jit(solution)/shard_map/ppermute | solution.py:27
  156.0 0.7 fusion.33
  156.6 0.3 fusion.73
  157.0 9.2 %collective-permute-done.6 = f32[512,128]{1,0:T(8,128)S(1)} collective-permute-done((f32[512,128]{1,0:T(8,128)S(1)}, f32[512,128]{1,0:T(8,128)S(1)}, u32[]{:S(2)}, u32[]{:S(2)}) %collective-permute-start.6) | collective-permute-done | bytes 262176 | tf_op jit(solution)/shard_map/ppermute | solution.py:27
  166.2 1.1 fusion.19
  (30 shorter events, 0.3 us)
Async XLA Ops:
  0.0 1.6 copy-start.1
  1.6 8.1 %copy-start = (f32[1,1,512,128]{3,2,1,0:T(8,128)S(1)}, f32[1,1,512,128]{3,2,1,0:T(8,128)}, u32[]{:S(2)}) copy-start(f32[1,1,512,128]{3,2,1,0:T(8,128)} %param.9) | copy-start | bytes 786436
  1.6 12.5 %copy-start.2 = (s32[1,1,3,4]{3,1,2,0:T(1,128)S(1)}, s32[1,1,3,4]{3,1,2,0:T(1,128)}, u32[]{:S(2)}) copy-start(s32[1,1,3,4]{3,1,2,0:T(1,128)} %param.10) | copy-start | bytes 148
  2.0 31.3 %collective-permute-start = (bf16[512,1024]{1,0:T(8,128)(2,1)S(1)}, bf16[512,1024]{1,0:T(8,128)(2,1)}, u32[]{:S(2)}, u32[]{:S(2)}) collective-permute-start(bf16[512,1024]{1,0:T(8,128)(2,1)S(1)} %get-tuple-element.38), channel_id=1, source_target_pairs={{48,0},{96,48},{144,96},{192,144},{240,192},{288,240},{336,288},{3... | collective-permute-start | bytes 3145736 | tf_op jit(solution)/shard_map/ppermute | solution.py:22
  9.7 38.8 %collective-permute-start.1 = (bf16[512,128]{1,0:T(8,128)(2,1)S(1)}, bf16[512,128]{1,0:T(8,128)(2,1)S(1)}, u32[]{:S(2)}, u32[]{:S(2)}) collective-permute-start(bf16[512,128]{1,0:T(8,128)(2,1)S(1)} %convert_bitcast_fusion.1), channel_id=1, source_target_pairs={{48,0},{96,48},{144,96},{192,144},{240,192},{288,240},{336,288},{3... | collective-permute-start | bytes 393224 | tf_op jit(solution)/shard_map/ppermute | solution.py:22
  35.7 12.8 %collective-permute-start.2 = (f32[516,128]{1,0:T(8,128)S(1)}, f32[516,128]{1,0:T(8,128)S(1)}, u32[]{:S(2)}, u32[]{:S(2)}) collective-permute-start(f32[516,128]{1,0:T(8,128)S(1)} %pad_maximum_fusion), channel_id=1, source_target_pairs={{0,48},{48,96},{96,144},{144,192},{192,240},{240,288},{288,336},{3... | collective-permute-start | bytes 792584 | tf_op jit(solution)/shard_map/ppermute | solution.py:27
  98.1 15.0 %collective-permute-start.4 = (f32[512,128]{1,0:T(8,128)S(1)}, f32[512,128]{1,0:T(8,128)S(1)}, u32[]{:S(2)}, u32[]{:S(2)}) collective-permute-start(f32[512,128]{1,0:T(8,128)S(1)} %fusion.72), channel_id=1, source_target_pairs={{0,48},{48,96},{96,144},{144,192},{192,240},{240,288},{288,336},{3... | collective-permute-start | bytes 786440 | tf_op jit(solution)/shard_map/ppermute | solution.py:27
  100.0 12.3 %collective-permute-start.3 = (bf16[512,128]{1,0:T(8,128)(2,1)S(1)}, bf16[512,128]{1,0:T(8,128)(2,1)S(1)}, u32[]{:S(2)}, u32[]{:S(2)}) collective-permute-start(bf16[512,128]{1,0:T(8,128)(2,1)S(1)} %fusion.42), channel_id=1, source_target_pairs={{48,0},{96,48},{144,96},{192,144},{240,192},{288,240},{336,288},{3... | collective-permute-start | bytes 393224 | tf_op jit(solution)/shard_map/ppermute | solution.py:22
  148.2 8.8 %collective-permute-start.5 = (bf16[512,128]{1,0:T(8,128)(2,1)S(1)}, bf16[512,128]{1,0:T(8,128)(2,1)S(1)}, u32[]{:S(2)}, u32[]{:S(2)}) collective-permute-start(bf16[512,128]{1,0:T(8,128)(2,1)S(1)} %fusion.39), channel_id=1, source_target_pairs={{48,0},{96,48},{144,96},{192,144},{240,192},{288,240},{336,288},{3... | collective-permute-start | bytes 393224 | tf_op jit(solution)/shard_map/ppermute | solution.py:22
  154.0 12.2 %collective-permute-start.6 = (f32[512,128]{1,0:T(8,128)S(1)}, f32[512,128]{1,0:T(8,128)S(1)}, u32[]{:S(2)}, u32[]{:S(2)}) collective-permute-start(f32[512,128]{1,0:T(8,128)S(1)} %fusion.74), channel_id=1, source_target_pairs={{0,48},{48,96},{96,144},{144,192},{192,240},{240,288},{288,336},{3... | collective-permute-start | bytes 786440 | tf_op jit(solution)/shard_map/ppermute | solution.py:27

commit v14 on v9

--- a/solution.py
+++ b/solution.py
@@ -124,11 +124,13 @@
     pair_weight = jnp.exp(pair_scale * jnp.dot(table, table.T, precision=highest))
     member = jnp.arange(groups, dtype=jnp.int32)
 
-    def far_all(iteration, summary):
+    def far_all(iteration, summary, own_only=False):
         chosen = jnp.sum(
             (source_all[:, iteration, :, None] == member[None, None, :]).astype(jnp.float32), axis=1
         )
         coefficient = chosen * pair_weight / count_all[:, None]
+        if own_only:
+            return jnp.einsum("h,hkc->kc", own(coefficient), summary, precision=highest)[None]
         return jnp.einsum("gh,hkc->gkc", coefficient, summary, precision=highest)
 
     def own(values):
@@ -145,11 +147,11 @@
     spread = local / degree[:, None]
     labels = keep_share * seed + (1.0 - keep_share) * (spread + rows_of(own(far_1)))
     spread_means = gather_groups(summarize(spread)[None])
-    far_2 = far_all(2, next_summary(spread_means, far_1))
+    far_2 = far_all(2, next_summary(spread_means, far_1), own_only=True)
 
     local, _ = spread_of(labels, False)
     spread = local / degree[:, None]
-    labels = keep_share * seed + (1.0 - keep_share) * (spread + rows_of(own(far_2)))
+    labels = keep_share * seed + (1.0 - keep_share) * (spread + rows_of(far_2[0]))
     return labels[None, None]
 
 

time: 159 us -> 160 us (level)
  transfers between devices with their start and end apart: 7 -> 7, of which waited for: 2 -> 2; matrix products, arithmetic and copies ran while one was open for 7% -> 8% of each run, Pallas kernels for 0% -> 0%
where the time goes in v14:
time: 160 us; the launch traced here: 159 us
  blocking collectives  84.2 us (53%)
  starting transfers between devices  29 us (18%)
  waiting for transfers between devices  24.7 us (15%)
  matrix products  9.28 us (6%)
  other arithmetic  6.34 us (4%)
  local copies, waits for them, and re-layouts  4.04 us (3%)
  between operations  1.75 us (1%)
    all_gather x3, blocking collectives, body(): table_a = lax.all_gather(table_a, axis, axis=0, tiled=False)  48.8 us
    all_gather x3, blocking collectives, gather_groups(): value = lax.all_gather(value, axis, axis=0, tiled=True)  35.3 us
    ppermute x4, waiting for transfers between devices, from_next(): lax.ppermute(block, 'seq', [((i + 1) % count, i) for i in range(count)])  24.7 us
    ppermute x3, starting transfers between devices, from_prev(): lax.ppermute(block, 'seq', [(i, (i + 1) % count) for i in range(count)])  15.8 us
    ppermute x4, starting transfers between devices, from_next(): lax.ppermute(block, 'seq', [((i + 1) % count, i) for i in range(count)])  13.2 us
    another operation x4, other arithmetic  3.35 us
  transfers between devices with their start and end apart: 7, of which 2 were waited for; matrix products, arithmetic and copies ran while one was open for 8% of the time, Pallas kernels for 0%

profile of v14, /device:TPU:14, one launch (start us, length us, event | category | flops | bytes accessed | tf_op | source)
XLA Modules:
  0.0 159.3 jit_solution(12504235792407840758)
XLA Ops:
  0.0 1.6 fusion.2
  1.6 0.3 convert_reduce_fusion
  2.0 2.4 %collective-permute-start = (bf16[512,1024]{1,0:T(8,128)(2,1)S(1)}, bf16[512,1024]{1,0:T(8,128)(2,1)}, u32[]{:S(2)}, u32[]{:S(2)}) collective-permute-start(bf16[512,1024]{1,0:T(8,128)(2,1)S(1)} %get-tuple-element.36), channel_id=1, source_target_pairs={{48,0},{96,48},{144,96},{192,144},{240,192},{288,240},{336,288},{3... | collective-permute-start | bytes 3145736 | tf_op jit(solution)/shard_map/ppermute | solution.py:22
  4.4 5.8 %collective-permute-start.1 = (bf16[512,128]{1,0:T(8,128)(2,1)S(1)}, bf16[512,128]{1,0:T(8,128)(2,1)S(1)}, u32[]{:S(2)}, u32[]{:S(2)}) collective-permute-start(bf16[512,128]{1,0:T(8,128)(2,1)S(1)} %convert_bitcast_fusion.1), channel_id=1, source_target_pairs={{48,0},{96,48},{144,96},{192,144},{240,192},{288,240},{336,288},{3... | collective-permute-start | bytes 393224 | tf_op jit(solution)/shard_map/ppermute | solution.py:22
  10.1 0.6 multiply_reduce_fusion
  11.4 0.7 and_reduce_fusion
  12.2 0.7 fusion.58
  12.9 0.9 convert_reduce_fusion.3
  13.8 16.2 %collective-permute-done = bf16[512,1024]{1,0:T(8,128)(2,1)} collective-permute-done((bf16[512,1024]{1,0:T(8,128)(2,1)S(1)}, bf16[512,1024]{1,0:T(8,128)(2,1)}, u32[]{:S(2)}, u32[]{:S(2)}) %collective-permute-start) | collective-permute-done | bytes 1048608 | tf_op jit(solution)/shard_map/ppermute | solution.py:22
  30.0 2.1 %convert_reduce_fusion.1 = (f32[512]{0:T(512)S(1)}, f32[512]{0:T(512)S(1)}, bf16[512,512]{0,1:T(8,128)(2,1)S(1)}) fusion(bf16[512,1024]{1,0:T(8,128)(2,1)S(1)} %get-tuple-element.36, bf16[512,1024]{1,0:T(8,128)(2,1)} %collective-permute-done), kind=kOutput, calls=%fused_computation.15 | convolution fusion | flops 538442752 | bytes 2625536 | tf_op jit(solution)/shard_map/dot_general | solution.py:44
  32.1 0.3 fusion.71
  32.5 3.5 %collective-permute-start.2 = (f32[516,128]{1,0:T(8,128)S(1)}, f32[516,128]{1,0:T(8,128)S(1)}, u32[]{:S(2)}, u32[]{:S(2)}) collective-permute-start(f32[516,128]{1,0:T(8,128)S(1)} %pad_maximum_fusion), channel_id=1, source_target_pairs={{0,48},{48,96},{96,144},{144,192},{192,240},{240,288},{288,336},{3... | collective-permute-start | bytes 792584 | tf_op jit(solution)/shard_map/ppermute | solution.py:27
  36.0 0.1 reshape.167
  36.1 0.7 slice.71
  37.4 1.9 %fusion.69 = f32[1,1]{1,0:T(1,128)} fusion(pred[1,1]{1,0:T(4,128)(4,1)} %bitcast.9, f32[1,1]{1,0:T(1,128)S(6)} %convert_element_type.90, s32[]{:T(128)} %bitcast.10, f32[1,12]{1,0:T(1,128)S(1)} %reshape.167), kind=kLoop, calls=%fused_computation.114 | loop fusion | flops 1 | bytes 61 | tf_op jit(solution)/shard_map/select.3
  39.4 1.4 scatter.9
  40.7 0.3 fusion.70
  41.1 0.4 bitcast_reduce_fusion.1
  41.5 34.0 %all-gather.4 = f32[12,41,128]{2,1,0:T(8,128)S(1)} all-gather(f32[1,41,128]{2,1,0:T(8,128)S(1)} %maximum_bitcast_fusion), channel_id=2, replica_groups=mesh['seq'=16,'grp_z'=12,'grp_y'=2,'grp_c'=2] {'grp_z'}, dimensions={0}, use_global_device_ids=true | all-gather | bytes 272896 | tf_op jit(solution)/shard_map/all_gather | solution.py:116
  75.5 12.2 %all-gather.1 = f32[24,41,128]{2,1,0:T(8,128)S(1)} all-gather(f32[12,41,128]{2,1,0:T(8,128)S(1)} %all-gather.4), channel_id=3, replica_groups=mesh['seq'=16,'grp_z'=12,'grp_y'=2,'grp_c'=2] {'grp_y'}, dimensions={0}, use_global_device_ids=true | all-gather | bytes 755712 | tf_op jit(solution)/shard_map/all_gather | solution.py:116
  87.7 2.6 %all-gather.2 = f32[4,12,41,128]{3,2,1,0:T(8,128)S(1)} all-gather(f32[2,12,41,128]{3,2,1,0:T(8,128)S(1)} %bitcast.123), channel_id=4, replica_groups=mesh['seq'=16,'grp_z'=12,'grp_y'=2,'grp_c'=2] {'grp_c'}, dimensions={0}, use_global_device_ids=true | all-gather | bytes 1511424 | tf_op jit(solution)/shard_map/all_gather | solution.py:116
  90.3 0.7 copy.38
  91.0 0.5 copy.39
  91.5 0.1 copy.44
  91.6 0.3 fusion.23
  92.0 0.1 convert_reduce_fusion.6
  92.1 0.5 fusion.35
  92.6 0.1 fusion.42
  92.7 0.3 fusion.72
  93.0 0.3 fusion.73
  93.3 9.6 %collective-permute-start.4 = (f32[512,128]{1,0:T(8,128)S(1)}, f32[512,128]{1,0:T(8,128)S(1)}, u32[]{:S(2)}, u32[]{:S(2)}) collective-permute-start(f32[512,128]{1,0:T(8,128)S(1)} %fusion.73), channel_id=1, source_target_pairs={{0,48},{48,96},{96,144},{144,192},{192,240},{240,288},{288,336},{3... | collective-permute-start | bytes 786440 | tf_op jit(solution)/shard_map/ppermute | solution.py:27
  102.9 1.9 %collective-permute-start.3 = (bf16[512,128]{1,0:T(8,128)(2,1)S(1)}, bf16[512,128]{1,0:T(8,128)(2,1)S(1)}, u32[]{:S(2)}, u32[]{:S(2)}) collective-permute-start(bf16[512,128]{1,0:T(8,128)(2,1)S(1)} %fusion.42), channel_id=1, source_target_pairs={{48,0},{96,48},{144,96},{192,144},{240,192},{288,240},{336,288},{3... | collective-permute-start | bytes 393224 | tf_op jit(solution)/shard_map/ppermute | solution.py:22
  104.9 0.1 convert_reduce_fusion.5
  105.0 0.6 fusion.29
  105.6 0.6 dynamic-slice.18
  106.2 0.1 convert_reduce_fusion.4
  106.2 8.5 %collective-permute-done.3 = bf16[512,128]{1,0:T(8,128)(2,1)S(1)} collective-permute-done((bf16[512,128]{1,0:T(8,128)(2,1)S(1)}, bf16[512,128]{1,0:T(8,128)(2,1)S(1)}, u32[]{:S(2)}, u32[]{:S(2)}) %collective-permute-start.3) | collective-permute-done | bytes 131104 | tf_op jit(solution)/shard_map/ppermute | solution.py:22
  114.8 0.4 bitcast_reduce_fusion
  115.1 0.1 fusion.39
  115.2 0.3 fusion.75
  115.5 3.1 %collective-permute-start.5 = (bf16[512,128]{1,0:T(8,128)(2,1)S(1)}, bf16[512,128]{1,0:T(8,128)(2,1)S(1)}, u32[]{:S(2)}, u32[]{:S(2)}) collective-permute-start(bf16[512,128]{1,0:T(8,128)(2,1)S(1)} %fusion.39), channel_id=1, source_target_pairs={{48,0},{96,48},{144,96},{192,144},{240,192},{288,240},{336,288},{3... | collective-permute-start | bytes 393224 | tf_op jit(solution)/shard_map/ppermute | solution.py:22
  118.7 2.7 %collective-permute-start.6 = (f32[512,128]{1,0:T(8,128)S(1)}, f32[512,128]{1,0:T(8,128)S(1)}, u32[]{:S(2)}, u32[]{:S(2)}) collective-permute-start(f32[512,128]{1,0:T(8,128)S(1)} %fusion.75), channel_id=1, source_target_pairs={{0,48},{48,96},{96,144},{144,192},{192,240},{240,288},{288,336},{3... | collective-permute-start | bytes 786440 | tf_op jit(solution)/shard_map/ppermute | solution.py:27
  121.4 1.8 %all-gather.3 = f32[32,128]{1,0:T(8,128)S(1)} all-gather(f32[16,128]{1,0:T(8,128)S(1)} %broadcast_multiply_fusion), channel_id=5, replica_groups=mesh['seq'=16,'grp_z'=12,'grp_y'=2,'grp_c'=2] {'grp_c'}, dimensions={0}, use_global_device_ids=true | all-gather | bytes 24576 | tf_op jit(solution)/shard_map/all_gather | solution.py:32
  123.2 11.8 %all_gather.34 = f32[4,16,128]{2,1,0:T(8,128)S(1)} all-gather(f32[2,16,128]{2,1,0:T(8,128)S(1)} %bitcast.127), channel_id=1, replica_groups=mesh['seq'=16,'grp_z'=12,'grp_y'=2,'grp_c'=2] {'grp_y'}, dimensions={0}, use_global_device_ids=true | all-gather | bytes 49152 | tf_op jit(solution)/shard_map/all_gather | solution.py:32
  135.0 21.7 %all_gather.35 = f32[48,16,128]{2,1,0:T(8,128)S(1)} all-gather(f32[4,16,128]{2,1,0:T(8,128)S(1)} %all_gather.34), channel_id=1, replica_groups=mesh['seq'=16,'grp_z'=12,'grp_y'=2,'grp_c'=2] {'grp_z'}, dimensions={0}, use_global_device_ids=true | all-gather | bytes 425984 | tf_op jit(solution)/shard_map/all_gather | solution.py:32
  156.7 1.1 fusion.33
  157.8 0.3 fusion.74
  158.2 1.1 fusion.19
  (30 shorter events, 0.2 us)
Async XLA Ops:
  0.0 1.6 %copy-start.1 = (bf16[1,1,512,1024]{3,2,1,0:T(8,128)(2,1)S(1)}, bf16[1,1,512,1024]{3,2,1,0:T(8,128)(2,1)}, u32[]{:S(2)}) copy-start(bf16[1,1,512,1024]{3,2,1,0:T(8,128)(2,1)} %param.8) | copy-start | bytes 3145732
  1.6 2.7 %copy-start = (f32[1,1,512,128]{3,2,1,0:T(8,128)S(1)}, f32[1,1,512,128]{3,2,1,0:T(8,128)}, u32[]{:S(2)}) copy-start(f32[1,1,512,128]{3,2,1,0:T(8,128)} %param.9) | copy-start | bytes 786436
  1.6 10.5 %copy-start.2 = (s32[1,1,3,4]{3,1,2,0:T(1,128)S(1)}, s32[1,1,3,4]{3,1,2,0:T(1,128)}, u32[]{:S(2)}) copy-start(s32[1,1,3,4]{3,1,2,0:T(1,128)} %param.10) | copy-start | bytes 148
  2.0 28.0 %collective-permute-start = (bf16[512,1024]{1,0:T(8,128)(2,1)S(1)}, bf16[512,1024]{1,0:T(8,128)(2,1)}, u32[]{:S(2)}, u32[]{:S(2)}) collective-permute-start(bf16[512,1024]{1,0:T(8,128)(2,1)S(1)} %get-tuple-element.36), channel_id=1, source_target_pairs={{48,0},{96,48},{144,96},{192,144},{240,192},{288,240},{336,288},{3... | collective-permute-start | bytes 3145736 | tf_op jit(solution)/shard_map/ppermute | solution.py:22
  4.4 36.7 %collective-permute-start.1 = (bf16[512,128]{1,0:T(8,128)(2,1)S(1)}, bf16[512,128]{1,0:T(8,128)(2,1)S(1)}, u32[]{:S(2)}, u32[]{:S(2)}) collective-permute-start(bf16[512,128]{1,0:T(8,128)(2,1)S(1)} %convert_bitcast_fusion.1), channel_id=1, source_target_pairs={{48,0},{96,48},{144,96},{192,144},{240,192},{288,240},{336,288},{3... | collective-permute-start | bytes 393224 | tf_op jit(solution)/shard_map/ppermute | solution.py:22
  32.5 8.6 %collective-permute-start.2 = (f32[516,128]{1,0:T(8,128)S(1)}, f32[516,128]{1,0:T(8,128)S(1)}, u32[]{:S(2)}, u32[]{:S(2)}) collective-permute-start(f32[516,128]{1,0:T(8,128)S(1)} %pad_maximum_fusion), channel_id=1, source_target_pairs={{0,48},{48,96},{96,144},{144,192},{192,240},{240,288},{288,336},{3... | collective-permute-start | bytes 792584 | tf_op jit(solution)/shard_map/ppermute | solution.py:27
  93.3 21.5 %collective-permute-start.4 = (f32[512,128]{1,0:T(8,128)S(1)}, f32[512,128]{1,0:T(8,128)S(1)}, u32[]{:S(2)}, u32[]{:S(2)}) collective-permute-start(f32[512,128]{1,0:T(8,128)S(1)} %fusion.73), channel_id=1, source_target_pairs={{0,48},{48,96},{96,144},{144,192},{192,240},{240,288},{288,336},{3... | collective-permute-start | bytes 786440 | tf_op jit(solution)/shard_map/ppermute | solution.py:27
  102.9 11.8 %collective-permute-start.3 = (bf16[512,128]{1,0:T(8,128)(2,1)S(1)}, bf16[512,128]{1,0:T(8,128)(2,1)S(1)}, u32[]{:S(2)}, u32[]{:S(2)}) collective-permute-start(bf16[512,128]{1,0:T(8,128)(2,1)S(1)} %fusion.42), channel_id=1, source_target_pairs={{48,0},{96,48},{144,96},{192,144},{240,192},{288,240},{336,288},{3... | collective-permute-start | bytes 393224 | tf_op jit(solution)/shard_map/ppermute | solution.py:22
  115.5 42.7 %collective-permute-start.5 = (bf16[512,128]{1,0:T(8,128)(2,1)S(1)}, bf16[512,128]{1,0:T(8,128)(2,1)S(1)}, u32[]{:S(2)}, u32[]{:S(2)}) collective-permute-start(bf16[512,128]{1,0:T(8,128)(2,1)S(1)} %fusion.39), channel_id=1, source_target_pairs={{48,0},{96,48},{144,96},{192,144},{240,192},{288,240},{336,288},{3... | collective-permute-start | bytes 393224 | tf_op jit(solution)/shard_map/ppermute | solution.py:22
  118.7 39.5 %collective-permute-start.6 = (f32[512,128]{1,0:T(8,128)S(1)}, f32[512,128]{1,0:T(8,128)S(1)}, u32[]{:S(2)}, u32[]{:S(2)}) collective-permute-start(f32[512,128]{1,0:T(8,128)S(1)} %fusion.75), channel_id=1, source_target_pairs={{0,48},{48,96},{96,144},{144,192},{192,240},{240,288},{288,336},{3... | collective-permute-start | bytes 786440 | tf_op jit(solution)/shard_map/ppermute | solution.py:27

commit v15 on v9

--- a/solution.py
+++ b/solution.py
@@ -112,9 +112,9 @@
         [centre_unit.reshape(centre_rows, classes), seed_mean, summarize(spread), info]
     )
     table_a = payload
-    for axis in GRP_PARTS:
+    for axis in (GRP_PARTS[2], GRP_PARTS[0], GRP_PARTS[1]):
         table_a = lax.all_gather(table_a, axis, axis=0, tiled=False)
-    table_a = jnp.transpose(table_a, (2, 1, 0, 3, 4)).reshape((groups,) + payload.shape)
+    table_a = jnp.transpose(table_a, (1, 0, 2, 3, 4)).reshape((groups,) + payload.shape)
     table = table_a[:, :centre_rows].reshape(groups, width)
     seed_means = table_a[:, centre_rows : centre_rows + coarse_count]
     spread_means = table_a[:, centre_rows + coarse_count : centre_rows + 2 * coarse_count]

time: 159 us -> 168 us (1.057)
  the two profiles are of different devices: /device:TPU:14 before, /device:TPU:30 now
where the time goes in v15:
time: 168 us
  blocking collectives  91.2 us (54%)
  waiting for transfers between devices  33.1 us (20%)
  starting transfers between devices  23.9 us (14%)
  matrix products  8.81 us (5%)
  other arithmetic  6.34 us (4%)
  local copies, waits for them, and re-layouts  2.91 us (2%)
  between operations  1.73 us (1%)
    all_gather x3, blocking collectives, body(): table_a = lax.all_gather(table_a, axis, axis=0, tiled=False)  59.4 us
    all_gather x3, blocking collectives, gather_groups(): value = lax.all_gather(value, axis, axis=0, tiled=True)  31.9 us
    ppermute x4, waiting for transfers between devices, from_next(): lax.ppermute(block, 'seq', [((i + 1) % count, i) for i in range(count)])  31.8 us
    ppermute x3, starting transfers between devices, from_prev(): lax.ppermute(block, 'seq', [(i, (i + 1) % count) for i in range(count)])  15.3 us
    ppermute x4, starting transfers between devices, from_next(): lax.ppermute(block, 'seq', [((i + 1) % count, i) for i in range(count)])  8.56 us
  transfers between devices with their start and end apart: 7, of which 3 were waited for; matrix products, arithmetic and copies ran while one was open for 7% of the time, Pallas kernels for 0%

profile of v15, /device:TPU:30, one launch (start us, length us, event | category | flops | bytes accessed | tf_op | source)
XLA Modules:
  0.0 168.0 jit_solution(18237149001614419306)
XLA Ops:
  0.0 1.6 fusion.2
  1.6 0.3 convert_reduce_fusion
  2.0 2.4 %collective-permute-start = (bf16[512,1024]{1,0:T(8,128)(2,1)S(1)}, bf16[512,1024]{1,0:T(8,128)(2,1)}, u32[]{:S(2)}, u32[]{:S(2)}) collective-permute-start(bf16[512,1024]{1,0:T(8,128)(2,1)S(1)} %get-tuple-element.36), channel_id=1, source_target_pairs={{48,0},{96,48},{144,96},{192,144},{240,192},{288,240},{336,288},{3... | collective-permute-start | bytes 3145736 | tf_op jit(solution)/shard_map/ppermute | solution.py:22
  4.4 2.4 %collective-permute-start.1 = (bf16[512,128]{1,0:T(8,128)(2,1)S(1)}, bf16[512,128]{1,0:T(8,128)(2,1)S(1)}, u32[]{:S(2)}, u32[]{:S(2)}) collective-permute-start(bf16[512,128]{1,0:T(8,128)(2,1)S(1)} %convert_bitcast_fusion.1), channel_id=1, source_target_pairs={{48,0},{96,48},{144,96},{192,144},{240,192},{288,240},{336,288},{3... | collective-permute-start | bytes 393224 | tf_op jit(solution)/shard_map/ppermute | solution.py:22
  6.7 0.6 multiply_reduce_fusion
  8.0 0.7 and_reduce_fusion
  8.7 0.7 fusion.62
  9.5 0.9 convert_reduce_fusion.3
  10.4 23.8 %collective-permute-done = bf16[512,1024]{1,0:T(8,128)(2,1)} collective-permute-done((bf16[512,1024]{1,0:T(8,128)(2,1)S(1)}, bf16[512,1024]{1,0:T(8,128)(2,1)}, u32[]{:S(2)}, u32[]{:S(2)}) %collective-permute-start) | collective-permute-done | bytes 1048608 | tf_op jit(solution)/shard_map/ppermute | solution.py:22
  34.2 2.1 %convert_reduce_fusion.1 = (f32[512]{0:T(512)S(1)}, f32[512]{0:T(512)S(1)}, bf16[512,512]{0,1:T(8,128)(2,1)S(1)}) fusion(bf16[512,1024]{1,0:T(8,128)(2,1)S(1)} %get-tuple-element.36, bf16[512,1024]{1,0:T(8,128)(2,1)} %collective-permute-done), kind=kOutput, calls=%fused_computation.15 | convolution fusion | flops 538442752 | bytes 2625536 | tf_op jit(solution)/shard_map/dot_general | solution.py:44
  36.3 0.3 fusion.70
  36.6 1.9 %collective-permute-start.2 = (f32[516,128]{1,0:T(8,128)S(1)}, f32[516,128]{1,0:T(8,128)S(1)}, u32[]{:S(2)}, u32[]{:S(2)}) collective-permute-start(f32[516,128]{1,0:T(8,128)S(1)} %pad_maximum_fusion), channel_id=1, source_target_pairs={{0,48},{48,96},{96,144},{144,192},{192,240},{240,288},{288,336},{3... | collective-permute-start | bytes 792584 | tf_op jit(solution)/shard_map/ppermute | solution.py:27
  38.6 0.1 reshape.168
  38.7 0.7 slice.71
  40.0 1.9 %fusion.68 = f32[1,1]{1,0:T(1,128)} fusion(pred[1,1]{1,0:T(4,128)(4,1)} %bitcast.9, f32[1,1]{1,0:T(1,128)S(6)} %convert_element_type.90, s32[]{:T(128)} %bitcast.10, f32[1,12]{1,0:T(1,128)S(1)} %reshape.168), kind=kLoop, calls=%fused_computation.113 | loop fusion | flops 1 | bytes 61 | tf_op jit(solution)/shard_map/select.3
  42.0 1.4 scatter.9
  43.3 0.3 fusion.69
  43.7 1.3 collective-permute-done.2
  45.0 0.4 bitcast_reduce_fusion.1
  45.3 1.8 %all-gather.4 = f32[2,41,128]{2,1,0:T(8,128)S(1)} all-gather(f32[1,41,128]{2,1,0:T(8,128)S(1)} %maximum_bitcast_fusion), channel_id=2, replica_groups=mesh['seq'=16,'grp_z'=12,'grp_y'=2,'grp_c'=2] {'grp_c'}, dimensions={0}, use_global_device_ids=true | all-gather | bytes 62976 | tf_op jit(solution)/shard_map/all_gather | solution.py:116
  47.2 35.6 %all-gather.1 = f32[24,41,128]{2,1,0:T(8,128)S(1)} all-gather(f32[2,41,128]{2,1,0:T(8,128)S(1)} %all-gather.4), channel_id=3, replica_groups=mesh['seq'=16,'grp_z'=12,'grp_y'=2,'grp_c'=2] {'grp_z'}, dimensions={0}, use_global_device_ids=true | all-gather | bytes 545792 | tf_op jit(solution)/shard_map/all_gather | solution.py:116
  82.8 0.3 copy.39
  83.0 21.9 %all-gather.2 = f32[24,2,41,128]{3,1,2,0:T(2,128)S(1)} all-gather(f32[12,2,41,128]{3,1,2,0:T(2,128)S(1)} %copy.39), channel_id=4, replica_groups=mesh['seq'=16,'grp_z'=12,'grp_y'=2,'grp_c'=2] {'grp_y'}, dimensions={0}, use_global_device_ids=true | all-gather | bytes 1511424 | tf_op jit(solution)/shard_map/all_gather | solution.py:116
  105.0 0.3 copy.40
  105.3 0.1 copy.44
  105.4 0.3 fusion.23
  105.8 0.1 convert_reduce_fusion.6
  105.9 0.5 fusion.35
  106.4 0.1 fusion.42
  106.5 0.3 fusion.71
  106.8 0.3 fusion.72
  107.1 5.6 %collective-permute-start.4 = (f32[512,128]{1,0:T(8,128)S(1)}, f32[512,128]{1,0:T(8,128)S(1)}, u32[]{:S(2)}, u32[]{:S(2)}) collective-permute-start(f32[512,128]{1,0:T(8,128)S(1)} %fusion.72), channel_id=1, source_target_pairs={{0,48},{48,96},{96,144},{144,192},{192,240},{240,288},{288,336},{3... | collective-permute-start | bytes 786440 | tf_op jit(solution)/shard_map/ppermute | solution.py:27
  112.7 1.9 %collective-permute-start.3 = (bf16[512,128]{1,0:T(8,128)(2,1)S(1)}, bf16[512,128]{1,0:T(8,128)(2,1)S(1)}, u32[]{:S(2)}, u32[]{:S(2)}) collective-permute-start(bf16[512,128]{1,0:T(8,128)(2,1)S(1)} %fusion.42), channel_id=1, source_target_pairs={{48,0},{96,48},{144,96},{192,144},{240,192},{288,240},{336,288},{3... | collective-permute-start | bytes 393224 | tf_op jit(solution)/shard_map/ppermute | solution.py:22
  114.6 0.1 convert_reduce_fusion.5
  114.7 0.5 fusion.29
  115.3 0.1 convert_reduce_fusion.4
  115.4 8.1 %collective-permute-done.3 = bf16[512,128]{1,0:T(8,128)(2,1)S(1)} collective-permute-done((bf16[512,128]{1,0:T(8,128)(2,1)S(1)}, bf16[512,128]{1,0:T(8,128)(2,1)S(1)}, u32[]{:S(2)}, u32[]{:S(2)}) %collective-permute-start.3) | collective-permute-done | bytes 131104 | tf_op jit(solution)/shard_map/ppermute | solution.py:22
  123.5 0.4 bitcast_reduce_fusion
  123.8 0.1 fusion.39
  123.9 0.3 fusion.74
  124.2 1.9 %collective-permute-start.5 = (bf16[512,128]{1,0:T(8,128)(2,1)S(1)}, bf16[512,128]{1,0:T(8,128)(2,1)S(1)}, u32[]{:S(2)}, u32[]{:S(2)}) collective-permute-start(bf16[512,128]{1,0:T(8,128)(2,1)S(1)} %fusion.39), channel_id=1, source_target_pairs={{48,0},{96,48},{144,96},{192,144},{240,192},{288,240},{336,288},{3... | collective-permute-start | bytes 393224 | tf_op jit(solution)/shard_map/ppermute | solution.py:22
  126.1 7.8 %collective-permute-start.6 = (f32[512,128]{1,0:T(8,128)S(1)}, f32[512,128]{1,0:T(8,128)S(1)}, u32[]{:S(2)}, u32[]{:S(2)}) collective-permute-start(f32[512,128]{1,0:T(8,128)S(1)} %fusion.74), channel_id=1, source_target_pairs={{0,48},{48,96},{96,144},{144,192},{192,240},{240,288},{288,336},{3... | collective-permute-start | bytes 786440 | tf_op jit(solution)/shard_map/ppermute | solution.py:27
  134.0 1.8 %all-gather.3 = f32[32,128]{1,0:T(8,128)S(1)} all-gather(f32[16,128]{1,0:T(8,128)S(1)} %broadcast_multiply_fusion), channel_id=5, replica_groups=mesh['seq'=16,'grp_z'=12,'grp_y'=2,'grp_c'=2] {'grp_c'}, dimensions={0}, use_global_device_ids=true | all-gather | bytes 24576 | tf_op jit(solution)/shard_map/all_gather | solution.py:32
  135.8 8.3 %all_gather.34 = f32[4,16,128]{2,1,0:T(8,128)S(1)} all-gather(f32[2,16,128]{2,1,0:T(8,128)S(1)} %bitcast.124), channel_id=1, replica_groups=mesh['seq'=16,'grp_z'=12,'grp_y'=2,'grp_c'=2] {'grp_y'}, dimensions={0}, use_global_device_ids=true | all-gather | bytes 49152 | tf_op jit(solution)/shard_map/all_gather | solution.py:32
  144.1 21.7 %all_gather.35 = f32[48,16,128]{2,1,0:T(8,128)S(1)} all-gather(f32[4,16,128]{2,1,0:T(8,128)S(1)} %all_gather.34), channel_id=1, replica_groups=mesh['seq'=16,'grp_z'=12,'grp_y'=2,'grp_c'=2] {'grp_z'}, dimensions={0}, use_global_device_ids=true | all-gather | bytes 425984 | tf_op jit(solution)/shard_map/all_gather | solution.py:32
  165.9 0.7 fusion.33
  166.5 0.3 fusion.73
  166.9 1.1 fusion.19
  (30 shorter events, 0.2 us)
Async XLA Ops:
  0.0 1.6 copy-start.1
  1.6 2.7 %copy-start = (f32[1,1,512,128]{3,2,1,0:T(8,128)S(1)}, f32[1,1,512,128]{3,2,1,0:T(8,128)}, u32[]{:S(2)}) copy-start(f32[1,1,512,128]{3,2,1,0:T(8,128)} %param.9) | copy-start | bytes 786436
  1.6 7.1 %copy-start.2 = (s32[1,1,3,4]{3,1,2,0:T(1,128)S(1)}, s32[1,1,3,4]{3,1,2,0:T(1,128)}, u32[]{:S(2)}) copy-start(s32[1,1,3,4]{3,1,2,0:T(1,128)} %param.10) | copy-start | bytes 148
  2.0 32.2 %collective-permute-start = (bf16[512,1024]{1,0:T(8,128)(2,1)S(1)}, bf16[512,1024]{1,0:T(8,128)(2,1)}, u32[]{:S(2)}, u32[]{:S(2)}) collective-permute-start(bf16[512,1024]{1,0:T(8,128)(2,1)S(1)} %get-tuple-element.36), channel_id=1, source_target_pairs={{48,0},{96,48},{144,96},{192,144},{240,192},{288,240},{336,288},{3... | collective-permute-start | bytes 3145736 | tf_op jit(solution)/shard_map/ppermute | solution.py:22
  4.4 40.6 %collective-permute-start.1 = (bf16[512,128]{1,0:T(8,128)(2,1)S(1)}, bf16[512,128]{1,0:T(8,128)(2,1)S(1)}, u32[]{:S(2)}, u32[]{:S(2)}) collective-permute-start(bf16[512,128]{1,0:T(8,128)(2,1)S(1)} %convert_bitcast_fusion.1), channel_id=1, source_target_pairs={{48,0},{96,48},{144,96},{192,144},{240,192},{288,240},{336,288},{3... | collective-permute-start | bytes 393224 | tf_op jit(solution)/shard_map/ppermute | solution.py:22
  36.6 8.3 %collective-permute-start.2 = (f32[516,128]{1,0:T(8,128)S(1)}, f32[516,128]{1,0:T(8,128)S(1)}, u32[]{:S(2)}, u32[]{:S(2)}) collective-permute-start(f32[516,128]{1,0:T(8,128)S(1)} %pad_maximum_fusion), channel_id=1, source_target_pairs={{0,48},{48,96},{96,144},{144,192},{192,240},{240,288},{288,336},{3... | collective-permute-start | bytes 792584 | tf_op jit(solution)/shard_map/ppermute | solution.py:27
  107.1 16.3 %collective-permute-start.4 = (f32[512,128]{1,0:T(8,128)S(1)}, f32[512,128]{1,0:T(8,128)S(1)}, u32[]{:S(2)}, u32[]{:S(2)}) collective-permute-start(f32[512,128]{1,0:T(8,128)S(1)} %fusion.72), channel_id=1, source_target_pairs={{0,48},{48,96},{96,144},{144,192},{192,240},{240,288},{288,336},{3... | collective-permute-start | bytes 786440 | tf_op jit(solution)/shard_map/ppermute | solution.py:27
  112.7 10.8 %collective-permute-start.3 = (bf16[512,128]{1,0:T(8,128)(2,1)S(1)}, bf16[512,128]{1,0:T(8,128)(2,1)S(1)}, u32[]{:S(2)}, u32[]{:S(2)}) collective-permute-start(bf16[512,128]{1,0:T(8,128)(2,1)S(1)} %fusion.42), channel_id=1, source_target_pairs={{48,0},{96,48},{144,96},{192,144},{240,192},{288,240},{336,288},{3... | collective-permute-start | bytes 393224 | tf_op jit(solution)/shard_map/ppermute | solution.py:22
  124.2 42.7 %collective-permute-start.5 = (bf16[512,128]{1,0:T(8,128)(2,1)S(1)}, bf16[512,128]{1,0:T(8,128)(2,1)S(1)}, u32[]{:S(2)}, u32[]{:S(2)}) collective-permute-start(bf16[512,128]{1,0:T(8,128)(2,1)S(1)} %fusion.39), channel_id=1, source_target_pairs={{48,0},{96,48},{144,96},{192,144},{240,192},{288,240},{336,288},{3... | collective-permute-start | bytes 393224 | tf_op jit(solution)/shard_map/ppermute | solution.py:22
  126.1 40.8 %collective-permute-start.6 = (f32[512,128]{1,0:T(8,128)S(1)}, f32[512,128]{1,0:T(8,128)S(1)}, u32[]{:S(2)}, u32[]{:S(2)}) collective-permute-start(f32[512,128]{1,0:T(8,128)S(1)} %fusion.74), channel_id=1, source_target_pairs={{0,48},{48,96},{96,144},{144,192},{192,240},{240,288},{288,336},{3... | collective-permute-start | bytes 786440 | tf_op jit(solution)/shard_map/ppermute | solution.py:27
